TPU v7x, 128 devices: a whole 4x4x4 slice. The times are simulated.
128 devices in a mesh: req: 16 (over x, y), kv: 8 (over z, core).
Axes of the slice: x: 4, y: 4, z: 4, core: 2. Of those that a mesh axis runs over, the one named last changes fastest.
Arguments:
- hidden: bfloat16 [1024, 2048], P('req', 'kv'), may hold values from -6 to 6
- attn_gain: float32 [2048], replicated, may hold values from 0.25 to 1.75
- q_gain: float32 [128], replicated, may hold values from 0.25 to 1.75
- k_gain: float32 [128], replicated, may hold values from 0.25 to 1.75
- w_q: bfloat16 [2048, 2048], P(None, 'kv'), may hold values from -0.125 to 0.125
- w_gate_attn: bfloat16 [2048, 2048], P(None, 'kv'), may hold values from -0.125 to 0.125
- w_k: bfloat16 [2048, 1024], P(None, 'kv'), may hold values from -0.125 to 0.125
- w_v: bfloat16 [2048, 1024], P(None, 'kv'), may hold values from -0.125 to 0.125
- w_o: bfloat16 [2048, 2048], P('kv'), may hold values from -0.125 to 0.125
- k_pool: bfloat16 [2784, 128, 1024], P('req', None, 'kv'), may hold values from -245 to 245
- v_pool: bfloat16 [2784, 128, 1024], P('req', None, 'kv'), may hold values from -6 to 6
- lengths: int32 [1024], P('req'), may hold values from 1 to 4095, as said below
- page_table: int32 [1024, 32], P('req'), may hold values from 0 to 173, as said below
- mig_request: int32 [16, 16], P('req'), may hold values from 0 to 63, as said below
- mig_dest: int32 [16, 16], P('req'), may hold values from 0 to 15, as said below
- mlp_gain: float32 [2048], replicated, may hold values from 0.25 to 1.75
- w_gate: bfloat16 [2048, 6144], P(None, ('req', 'kv')), may hold values from -0.125 to 0.125
- w_up: bfloat16 [2048, 6144], P(None, ('req', 'kv')), may hold values from -0.125 to 0.125
- w_down: bfloat16 [2048, 6144], P(None, ('req', 'kv')), may hold values from -0.078125 to 0.078125
Outputs:
- out_hidden: bfloat16 [1024, 2048], P('req', 'kv')
- mig_keys: bfloat16 [256, 512, 1024], P('req', None, 'kv')
- mig_values: bfloat16 [256, 512, 1024], P('req', None, 'kv')
Inputs may be any that keep to these rules, and one draw needn't show every extreme that they name: lengths[r] tokens of request r are cached and its new token takes position lengths[r]; some request holds 4095 cached tokens. `page_table`: entries refer to the pool of the request's own device. The first lengths[r] // 128 + 1 entries of row r are the request's pages, distinct and never shared with another request of that device; later entries are valid pages that are not read. `mig_request`: row s names 16 different requests of device s; each has at most 511 cached tokens, and in every row one has exactly that many. `mig_dest`: each row is a permutation.
All inputs are finite; a program needn't handle non-finite values.
Results may differ from a plain program's by a relative error of at most 0.0093.
Values may be sent and summed in bfloat16 or wider, within the bound.
No kernel may reach another device: no remote copies, remote signals or barrier semaphores. Data moves between devices by JAX's collectives and lax.ppermute only.
A program may use at most 128 MiB of HBM per device.

v0:
```python
import jax
import jax.numpy as jnp
from jax import lax
from jax.sharding import PartitionSpec as P

MIGP = 4


EPSILON = 1e-06
ROPE_BASE = 1000000.0
SLOT_BLOCK = 4


def rms_norm(values, scale_row):
    values = values.astype(jnp.float32)
    return (
        values * lax.rsqrt(jnp.mean(values * values, axis=-1, keepdims=True) + EPSILON) * scale_row
    )


def rotate(values, position):
    half_dim = values.shape[-1] // 2
    frequency = ROPE_BASE ** (-jnp.arange(half_dim, dtype=jnp.float32) * 2.0 / values.shape[-1])
    angles = position.astype(jnp.float32)[:, None, None] * frequency
    cosine = jnp.cos(angles)
    sine_part = jnp.sin(angles)
    first_half = values[..., :half_dim]
    second = values[..., half_dim:]
    return jnp.concatenate(
        [first_half * cosine - second * sine_part, second * cosine + first_half * sine_part],
        axis=-1,
    )


def attend_slots(queries, new_keys, new_values, k_pool, v_pool, lengths, page_table):
    req_count, kv_local, group_size, head_dim = queries.shape
    page_size = k_pool.shape[1]
    slot_span = page_table.shape[1] * page_size
    score_scale = head_dim ** (-0.5)
    used_pages = jnp.max(lengths) // page_size + 1
    turn_count = (used_pages + SLOT_BLOCK - 1) // SLOT_BLOCK
    block_width = SLOT_BLOCK * page_size

    def score_block(turn_index, buffer):
        page_ids = lax.dynamic_slice_in_dim(page_table, turn_index * SLOT_BLOCK, SLOT_BLOCK, 1)
        key_block = k_pool[page_ids].reshape(req_count, block_width, kv_local, head_dim)
        scores = (
            jnp.einsum("rkgd,rtkd->rkgt", queries, key_block, preferred_element_type=jnp.float32)
            * score_scale
        )
        return lax.dynamic_update_slice_in_dim(buffer, scores, turn_index * block_width, 3)

    start_buffer = jnp.full((req_count, kv_local, group_size, slot_span), -jnp.inf, jnp.float32)
    scores = lax.fori_loop(0, turn_count, score_block, start_buffer)
    position = jnp.arange(slot_span, dtype=jnp.int32)
    scores = jnp.where(
        position[None, None, None, :] < lengths[:, None, None, None], scores, -jnp.inf
    )
    own_score = (
        jnp.einsum("rkgd,rkd->rkg", queries, new_keys, preferred_element_type=jnp.float32)
        * score_scale
    )
    row_top = jnp.maximum(jnp.max(scores, axis=-1), own_score)
    exps_all = jnp.exp(scores - row_top[..., None])
    own_exp = jnp.exp(own_score - row_top)
    denom_sum = jnp.sum(exps_all, axis=-1) + own_exp
    weights = (exps_all / denom_sum[..., None]).astype(jnp.bfloat16)
    own_weight = (own_exp / denom_sum).astype(jnp.bfloat16)

    def value_block(turn_index, context_sum):
        page_ids = lax.dynamic_slice_in_dim(page_table, turn_index * SLOT_BLOCK, SLOT_BLOCK, 1)
        val_block = v_pool[page_ids].reshape(req_count, block_width, kv_local, head_dim)
        weight_block = lax.dynamic_slice_in_dim(weights, turn_index * block_width, block_width, 3)
        return context_sum + jnp.einsum(
            "rkgt,rtkd->rkgd", weight_block, val_block, preferred_element_type=jnp.float32
        )

    start_sum = jnp.einsum(
        "rkg,rkd->rkgd", own_weight, new_values, preferred_element_type=jnp.float32
    )
    return lax.fori_loop(0, turn_count, value_block, start_sum)


def hidden_full_add(whole_rows, attn_sum):
    return whole_rows.astype(jnp.float32) + attn_sum


def per_device(
    hidden,
    attn_gain,
    q_gain,
    k_gain,
    w_q,
    w_gate_attn,
    w_k,
    w_v,
    w_o,
    k_pool,
    v_pool,
    lengths,
    page_table,
    mig_request,
    mig_dest,
    mlp_gain,
    w_gate,
    w_up,
    w_down,
):
    head_dim = q_gain.shape[0]
    req_count = hidden.shape[0]
    kv_local = w_k.shape[1] // head_dim
    q_local = w_q.shape[1] // head_dim
    group_size = q_local // kv_local
    page_size = k_pool.shape[1]
    channels = kv_local * head_dim
    model_width = mlp_gain.shape[0]
    whole_rows = lax.all_gather(hidden, "kv", axis=1, tiled=True)
    normed = rms_norm(whole_rows, attn_gain).astype(jnp.bfloat16)
    query_raw = jnp.dot(normed, w_q, preferred_element_type=jnp.float32).reshape(
        req_count, q_local, head_dim
    )
    gate_raw = jnp.dot(normed, w_gate_attn, preferred_element_type=jnp.float32)
    key_raw = jnp.dot(normed, w_k, preferred_element_type=jnp.float32).reshape(
        req_count, kv_local, head_dim
    )
    value_raw = jnp.dot(normed, w_v, preferred_element_type=jnp.float32).reshape(
        req_count, kv_local, head_dim
    )
    queries = rotate(rms_norm(query_raw, q_gain), lengths).astype(jnp.bfloat16)
    queries = queries.reshape(req_count, kv_local, group_size, head_dim)
    new_keys = rotate(rms_norm(key_raw, k_gain), lengths).astype(jnp.bfloat16)
    new_values = value_raw.astype(jnp.bfloat16)
    mig_rows = mig_request[0]
    dest_row = mig_dest[0]
    mig_count = mig_rows.shape[0]
    slot_count = MIGP * page_size
    moved_pages = page_table[mig_rows, :MIGP]
    slot_pos = jnp.arange(slot_count, dtype=jnp.int32)[None, :, None]
    moved_len = lengths[mig_rows][:, None, None]
    zero_value = jnp.zeros((), jnp.bfloat16)
    inverse = jnp.zeros_like(dest_row).at[dest_row].set(jnp.arange(mig_count, dtype=jnp.int32))

    def place_cache(pool, fresh_rows):
        cached = pool[moved_pages].reshape(mig_count, slot_count, channels)
        fresh_row = fresh_rows.reshape(req_count, channels)[mig_rows][:, None, :]
        filled = jnp.where(
            slot_pos < moved_len, cached, jnp.where(slot_pos == moved_len, fresh_row, zero_value)
        )
        return filled[inverse]

    mig_keys, mig_values = (
        lax.all_to_all(
            place_cache(k_pool, new_keys), "req", split_axis=0, concat_axis=0, tiled=True
        ),
        lax.all_to_all(
            place_cache(v_pool, new_values), "req", split_axis=0, concat_axis=0, tiled=True
        ),
    )
    context = attend_slots(queries, new_keys, new_values, k_pool, v_pool, lengths, page_table)
    gated = (jax.nn.sigmoid(gate_raw) * context.reshape(req_count, q_local * head_dim)).astype(
        jnp.bfloat16
    )
    head_terms = jnp.dot(gated, w_o, preferred_element_type=jnp.float32)
    attn_sum = lax.psum(head_terms, "kv")
    mid_stream = hidden_full_add(whole_rows, attn_sum).astype(jnp.bfloat16)
    normed_mlp = rms_norm(mid_stream, mlp_gain).astype(jnp.bfloat16)
    kv_count = lax.axis_size("kv")
    slice_width = model_width // kv_count
    slice_start = lax.axis_index("kv") * slice_width
    mid_slice = lax.dynamic_slice_in_dim(mid_stream, slice_start, slice_width, 1)
    row_piece = lax.all_gather(normed_mlp, "req", axis=0, tiled=True)
    gate_part = jnp.dot(row_piece, w_gate, preferred_element_type=jnp.float32)
    up_part = jnp.dot(row_piece, w_up, preferred_element_type=jnp.float32)
    activation = (jax.nn.silu(gate_part) * up_part).astype(jnp.bfloat16)
    req_groups = lax.axis_size("req")
    unit_count = activation.shape[1]
    grouped_act = activation.reshape(req_groups, req_count, unit_count)
    grouped_down = w_down.reshape(kv_count, slice_width, unit_count)
    term = jnp.einsum(
        "gru,hcu->ghrc", grouped_act, grouped_down, preferred_element_type=jnp.float32
    )
    term = term.reshape(req_groups * kv_count, req_count, slice_width)
    mlp_part = lax.psum_scatter(term, ("req", "kv"), scatter_dimension=0, tiled=True)[0]
    out_hidden = (mid_slice.astype(jnp.float32) + mlp_part).astype(jnp.bfloat16)
    return (out_hidden, mig_keys, mig_values)


def solution(mesh):
    return jax.shard_map(
        per_device,
        mesh=mesh,
        in_specs=(
            P("req", "kv"),
            P(),
            P(),
            P(),
            P(None, "kv"),
            P(None, "kv"),
            P(None, "kv"),
            P(None, "kv"),
            P("kv", None),
            P("req", None, "kv"),
            P("req", None, "kv"),
            P("req"),
            P("req", None),
            P("req", None),
            P("req", None),
            P(),
            P(None, ("req", "kv")),
            P(None, ("req", "kv")),
            P(None, ("req", "kv")),
        ),
        out_specs=(P("req", "kv"), P("req", None, "kv"), P("req", None, "kv")),
        check_vma=False,
    )
```

profile of v0, /device:TPU:1, one launch (start us, length us, event | category | flops | bytes accessed | tf_op | source)
XLA Modules:
  0.0 1110.7 jit_solution(7748420116868320905)
XLA Ops:
  7.2 1.4 fusion.58
  11.3 1.6 iota_compare_fusion
  12.8 15.6 %all_gather.6 = bf16[64,2048]{1,0:T(8,128)(2,1)S(1)} all-gather(bf16[64,256]{1,0:T(8,128)(2,1)} %param.23), channel_id=1, replica_groups=mesh['req'=16,'kv'=8] {'kv'}, dimensions={1}, use_global_device_ids=true | all-gather | bytes 294912 | tf_op jit(solution)/shard_map/all_gather | solution.py:117
  28.4 0.2 fusion.18
  28.6 1.6 fusion.53
  30.2 0.1 multiply_reduce_fusion
  30.5 0.1 multiply_multiply_fusion
  30.6 0.2 multiply_cosine_fusion.1
  30.8 0.2 subtract_convert_fusion
  31.0 0.6 copy-done.12
  31.6 0.1 pad_maximum_fusion.1
  31.7 1.0 broadcast_in_dim.61
  32.7 17.2 %while.20 = (s32[]{:T(128)}, f32[64,1,2,4096]{3,2,0,1:T(2,128)S(1)}, s32[]{:T(128)}, s32[64,32]{1,0:T(8,128)S(1)}, bf16[174,128,128]{2,1,0:T(8,128)(2,1)}, /*ind...) while((s32[]{:T(128)}, ...), condition=%wide.region_5.6_spmd, body=%wide.region_4.5_spmd.sunk | while | flops 16844552 | bytes 25471192 | solution.py:54
  32.8 0.1 reshape.565
  33.0 11.3 %gather_fusion = bf16[256,128,128]{2,1,0:T(8,128)(2,1)} fusion(bf16[174,128,128]{2,1,0:T(8,128)(2,1)} %get-tuple-element.265, s32[1024]{0:T(1024)S(1)} %pad_clamp_fusion.7), kind=kCustom, calls=%fused_computation.clone.1 | custom fusion | bytes 16778240 | tf_op jit(solution)/shard_map/while/body/gather | solution.py:46
  44.2 5.7 fusion.81
  50.0 1.5 multiply_reduce_fusion.1
  51.6 0.2 fusion.42
  51.8 0.1 fusion.72
  51.9 1.0 fusion.38
  52.9 2.6 fusion.7
  55.5 2.6 fusion.22
  58.1 3.4 divide_convert_fusion
  61.5 0.3 fusion.59
  61.8 0.1 multiply_bitcast_fusion
  61.9 16.4 %while.21 = (s32[]{:T(128)}, f32[64,1,2,128]{3,2,0,1:T(2,128)S(1)}, s32[]{:T(128)}, bf16[64,1,2,4096]{3,2,0,1:T(2,128)(2,1)}, s32[64,32]{1,0:T(8,128)S(1)}, /*in...) while((s32[]{:T(128)}, f32[64,1,2,128]{3,2,0,1:T(2,128)S(1)}, ...), condition=%wide.region_9.10_spmd, body=%wide.region_8.9_spmd.sunk | while | flops 16795400 | bytes 25438424 | solution.py:81
  62.2 0.1 reshape.568
  62.3 11.3 %gather_fusion.1 = bf16[256,128,128]{2,1,0:T(8,128)(2,1)} fusion(bf16[174,128,128]{2,1,0:T(8,128)(2,1)} %get-tuple-element.302, s32[1024]{0:T(1024)S(1)} %pad_clamp_fusion.8), kind=kCustom, calls=%fused_computation.1.clone.1 | custom fusion | bytes 16778240 | tf_op jit(solution)/shard_map/while/body/gather | solution.py:72
  73.6 4.7 fusion.84
  78.4 1.7 fusion.14
  80.1 292.3 %all-reduce.3.cloned.1.call-done = f32[64,2048]{1,0:T(8,128)} async-done(((f32[64,2048]{1,0:T(8,128)}), f32[64,2048]{1,0:T(8,128)}) %all-reduce.3.cloned.1.call-update) | async-done | bytes 524304 | tf_op jit(solution)/shard_map/psum | solution.py:164
  372.4 1.2 fusion.15
  373.7 0.8 fusion.17
  374.6 52.8 %all-gather.2.cloned.1.call-done = bf16[1024,2048]{1,0:T(8,128)(2,1)} async-done(((bf16[64,2048]{1,0:T(8,128)(2,1)}), bf16[1024,2048]{1,0:T(8,128)(2,1)}) %all-gather.2.cloned.1.call-update) | async-done | bytes 4194320 | tf_op jit(solution)/shard_map/all_gather | solution.py:171
  427.4 3.7 fusion.60
  431.2 1.4 fusion.8
  432.6 0.2 reshape.426
  432.7 4.5 fusion.23
  437.3 0.6 copy-done.19
  438.0 0.7 gather_fusion.11
  438.7 0.7 gather_fusion.12
  439.4 0.7 gather_fusion.9
  440.1 0.7 gather_fusion.10
  440.7 0.1 copy.42
  440.8 0.1 reshape.457
  440.9 3.6 gather_fusion.6
  444.5 4.8 gather_fusion.3
  449.4 0.7 gather_fusion.2
  450.0 0.1 pad_maximum_fusion.3
  450.1 0.6 gather_fusion.4
  450.7 0.6 gather_fusion.7
  451.3 0.6 scatter_custom_fusion
  451.9 0.1 iota_compare_fusion.2
  452.0 7.2 bitcast_select_fusion
  459.2 3.7 gather_fusion.5
  463.0 5.1 all-to-all-start
  468.1 2.1 gather_fusion.8
  470.2 24.9 %all-to-all-done = bf16[16,512,128]{2,1,0:T(8,128)(2,1)} async-done(((bf16[16,512,128]{2,1,0:T(8,128)(2,1)}), bf16[16,512,128]{2,1,0:T(8,128)(2,1)}, u32[]{:S(2)}, u32[]{:S(2)}) %all-to-all-start) | async-done | bytes 2097184 | tf_op jit(solution)/shard_map/all_to_all | solution.py:152
  495.2 5.1 all-to-all-start.1
  500.3 25.0 %all-to-all-done.1 = bf16[16,512,128]{2,1,0:T(8,128)(2,1)S(1)} async-done(((bf16[16,512,128]{2,1,0:T(8,128)(2,1)}), bf16[16,512,128]{2,1,0:T(8,128)(2,1)S(1)}, u32[]{:S(2)}, u32[]{:S(2)}) %all-to-all-start.1) | async-done | bytes 2097184 | tf_op jit(solution)/shard_map/all_to_all | solution.py:155
  525.3 573.0 %reduce-scatter.2.cloned.1.call-done = f32[1,64,256]{2,1,0:T(8,128)} async-done(((f32[128,64,256]{2,1,0:T(8,128)}), f32[1,64,256]{2,1,0:T(8,128)}) %reduce-scatter.2.cloned.1.call-update) | async-done | bytes 65552 | tf_op jit(solution)/shard_map/reduce_scatter | solution.py:183
  1098.3 1.5 fusion.28
  1099.7 3.1 copy.79
  1102.8 1.3 copy.80
  (72 shorter events, 0.9 us)
Async XLA Ops:
  7.2 71.2 %copy-start = (bf16[256,2048]{1,0:T(8,128)(2,1)S(1)}, bf16[256,2048]{1,0:T(8,128)(2,1)}, u32[]{:S(2)}) copy-start(bf16[256,2048]{1,0:T(8,128)(2,1)} %param.31) | copy-start | bytes 3145732
  7.2 23.2 %copy-start.2 = (s32[64,32]{0,1:T(8,128)S(1)}, s32[64,32]{0,1:T(8,128)}, u32[]{:S(2)}) copy-start(s32[64,32]{0,1:T(8,128)} %param.35) | copy-start | bytes 24580
  7.2 23.3 %copy-start.15 = (f32[128]{0:T(128)S(1)}, f32[128]{0:T(128)}, u32[]{:S(2)}) copy-start(f32[128]{0:T(128)} %param.25) | copy-start | bytes 1540
  7.2 365.2 %all-reduce.3.cloned.1.call-start = ((), (), s32[]{:S(2)}) async-start(), calls=%async_computation.3 | async-start | bytes 1048576 | tf_op jit(solution)/shard_map/psum | solution.py:164
  31.0 0.6 copy-start.12
  31.0 1.8 copy-start.11
  32.7 17.3 %copy-start.13 = (f32[2048]{0:T(1024)S(1)}, f32[2048]{0:T(1024)}, u32[]{:S(2)}) copy-start(f32[2048]{0:T(1024)} %param.24) | copy-start | bytes 24580
  32.7 18.8 %copy-start.16 = (f32[128]{0:T(128)S(1)}, f32[128]{0:T(128)}, u32[]{:S(2)}) copy-start(f32[128]{0:T(128)} %param.26) | copy-start | bytes 1540
  50.0 5.5 copy-start.5
  58.0 3.5 copy-start.8
  61.9 16.5 %copy-start.7 = (bf16[2048,256]{1,0:T(8,128)(2,1)S(1)}, bf16[2048,256]{1,0:T(8,128)(2,1)}, u32[]{:S(2)}) copy-start(bf16[2048,256]{1,0:T(8,128)(2,1)} %param.28) | copy-start | bytes 3145732
  78.4 295.3 %copy-start.14 = (f32[2048]{0:T(1024)S(1)}, f32[2048]{0:T(1024)}, u32[]{:S(2)}) copy-start(f32[2048]{0:T(1024)} %param.38) | copy-start | bytes 24580
  78.4 349.0 %copy-start.9 = (bf16[2048,48]{0,1:T(8,128)(2,1)S(1)}, bf16[2048,48]{0,1:T(8,128)(2,1)}, u32[]{:S(2)}) copy-start(bf16[2048,48]{0,1:T(8,128)(2,1)} %param.39) | copy-start | bytes 589828
  80.1 347.3 %all-gather.2.cloned.1.call-start = ((), (), s32[]{:S(2)}) async-start(), calls=%async_computation.4 | async-start | bytes 4456448 | tf_op jit(solution)/shard_map/all_gather | solution.py:171
  373.7 57.5 %copy-start.6 = (bf16[64,2048]{1,0:T(8,128)(2,1)}, bf16[64,2048]{1,0:T(8,128)(2,1)S(1)}, u32[]{:S(2)}) copy-start(bf16[64,2048]{1,0:T(8,128)(2,1)S(1)} %get-tuple-element.134) | copy-start | bytes 786436
  374.5 56.6 %copy-start.18 = (bf16[2048,48]{0,1:T(8,128)(2,1)S(1)}, bf16[2048,48]{0,1:T(8,128)(2,1)}, u32[]{:S(2)}) copy-start(bf16[2048,48]{0,1:T(8,128)(2,1)} %param.40) | copy-start | bytes 589828
  374.6 723.7 %reduce-scatter.2.cloned.1.call-start = ((), (), s32[]{:S(2)}) async-start(), calls=%async_computation.5 | async-start | bytes 8454144 | tf_op jit(solution)/shard_map/reduce_scatter | solution.py:183
  427.4 3.7 copy-start.4
  431.2 1.6 copy-start.10
  437.3 0.7 copy-start.19
  437.3 0.7 copy-start.17
  444.5 4.8 copy-start.1
  444.5 6.7 copy-start.20
  463.0 5.1 copy-start.3
  463.0 32.2 %all-to-all-start = ((bf16[16,512,128]{2,1,0:T(8,128)(2,1)}), bf16[16,512,128]{2,1,0:T(8,128)(2,1)}, u32[]{:S(2)}, u32[]{:S(2)}) async-start(bf16[16,512,128]{2,1,0:T(8,128)(2,1)} %gather_fusion.5), calls=%async_computation.1 | async-start | bytes 4194304 | tf_op jit(solution)/shard_map/all_to_all | solution.py:152
  495.2 30.1 %all-to-all-start.1 = ((bf16[16,512,128]{2,1,0:T(8,128)(2,1)}), bf16[16,512,128]{2,1,0:T(8,128)(2,1)S(1)}, u32[]{:S(2)}, u32[]{:S(2)}) async-start(bf16[16,512,128]{2,1,0:T(8,128)(2,1)} %gather_fusion.8), calls=%async_computation.2 | async-start | bytes 4194304 | tf_op jit(solution)/shard_map/all_to_all | solution.py:155
Sparse Core Ops, SparseCore 0:
  80.2 292.1 all-reduce.2
  375.1 52.2 all-gather.1
  437.4 660.7 reduce-scatter.1
where the time goes:
time: 1120 us; the launch traced here: 1110 us
  waiting for transfers between devices  968 us (86%)
  local copies, waits for them, and re-layouts  49.3 us (4%)
  matrix products  26.1 us (2%)
  other arithmetic  24.2 us (2%)
  between operations  16.8 us (2%)
  blocking collectives  15.6 us (1%)
    reduce_scatter x1, waiting for transfers between devices, per_device(): lax.psum_scatter(term, ('req', 'kv'), scatter_dimension=0, tiled=True)[0]  573 us
    psum x1, waiting for transfers between devices, per_device(): attn_sum = lax.psum(head_terms, 'kv')  292 us
    all_gather x1, waiting for transfers between devices, per_device(): row_piece = lax.all_gather(normed_mlp, 'req', axis=0, tiled=True)  52.8 us
    all_to_all x1, waiting for transfers between devices, per_device(): lax.all_to_all(place_cache(v_pool, new_values), 'req', split_axis=0, conc...  25 us
    all_to_all x1, waiting for transfers between devices, per_device(): lax.all_to_all(place_cache(k_pool, new_keys), 'req', split_axis=0, concat...  24.9 us
  transfers between devices with their start and end apart: 5, of which 5 were waited for; matrix products, arithmetic and copies ran while one was open for 2% of the time, Pallas kernels for 0%

commit v1 on v0

--- a/solution.py
+++ b/solution.py
@@ -81,8 +81,11 @@
     return lax.fori_loop(0, turn_count, value_block, start_sum)
 
 
-def hidden_full_add(whole_rows, attn_sum):
-    return whole_rows.astype(jnp.float32) + attn_sum
+def reduce_to_slice(partial, kv_count, slice_width):
+    rows = partial.shape[0]
+    pieces = partial.reshape(rows, kv_count, slice_width).transpose(1, 0, 2)
+    arrived = lax.all_to_all(pieces, "kv", 0, 0, tiled=True)
+    return jnp.sum(arrived, axis=0)
 
 
 def per_device(
@@ -114,6 +117,9 @@
     page_size = k_pool.shape[1]
     channels = kv_local * head_dim
     model_width = mlp_gain.shape[0]
+    gate_w = lax.all_gather(w_gate, "req", axis=1, tiled=True)
+    up_w = lax.all_gather(w_up, "req", axis=1, tiled=True)
+    down_w = lax.all_gather(w_down, "req", axis=1, tiled=True)
     whole_rows = lax.all_gather(hidden, "kv", axis=1, tiled=True)
     normed = rms_norm(whole_rows, attn_gain).astype(jnp.bfloat16)
     query_raw = jnp.dot(normed, w_q, preferred_element_type=jnp.float32).reshape(
@@ -161,26 +167,20 @@
         jnp.bfloat16
     )
     head_terms = jnp.dot(gated, w_o, preferred_element_type=jnp.float32)
-    attn_sum = lax.psum(head_terms, "kv")
-    mid_stream = hidden_full_add(whole_rows, attn_sum).astype(jnp.bfloat16)
-    normed_mlp = rms_norm(mid_stream, mlp_gain).astype(jnp.bfloat16)
     kv_count = lax.axis_size("kv")
     slice_width = model_width // kv_count
-    slice_start = lax.axis_index("kv") * slice_width
-    mid_slice = lax.dynamic_slice_in_dim(mid_stream, slice_start, slice_width, 1)
-    row_piece = lax.all_gather(normed_mlp, "req", axis=0, tiled=True)
-    gate_part = jnp.dot(row_piece, w_gate, preferred_element_type=jnp.float32)
-    up_part = jnp.dot(row_piece, w_up, preferred_element_type=jnp.float32)
+    mid_slice = (
+        hidden.astype(jnp.float32) + reduce_to_slice(head_terms, kv_count, slice_width)
+    ).astype(jnp.bfloat16)
+    mid_stream = lax.all_gather(mid_slice, "kv", axis=1, tiled=True)
+    normed_mlp = rms_norm(mid_stream, mlp_gain).astype(jnp.bfloat16)
+    gate_part = jnp.dot(normed_mlp, gate_w, preferred_element_type=jnp.float32)
+    up_part = jnp.dot(normed_mlp, up_w, preferred_element_type=jnp.float32)
     activation = (jax.nn.silu(gate_part) * up_part).astype(jnp.bfloat16)
-    req_groups = lax.axis_size("req")
-    unit_count = activation.shape[1]
-    grouped_act = activation.reshape(req_groups, req_count, unit_count)
-    grouped_down = w_down.reshape(kv_count, slice_width, unit_count)
-    term = jnp.einsum(
-        "gru,hcu->ghrc", grouped_act, grouped_down, preferred_element_type=jnp.float32
-    )
-    term = term.reshape(req_groups * kv_count, req_count, slice_width)
-    mlp_part = lax.psum_scatter(term, ("req", "kv"), scatter_dimension=0, tiled=True)[0]
+    down_part = jnp.einsum(
+        "ru,cu->rc", activation, down_w, preferred_element_type=jnp.float32
+    )
+    mlp_part = reduce_to_slice(down_part, kv_count, slice_width)
     out_hidden = (mid_slice.astype(jnp.float32) + mlp_part).astype(jnp.bfloat16)
     return (out_hidden, mig_keys, mig_values)
 

time: 1120 us -> 458 us (0.41)
  waiting for transfers between devices: 968 us -> 36.3 us
  starting transfers between devices: 10.3 us -> 254 us
  blocking collectives: 15.6 us -> 47 us
    reduce_scatter x1 -> x0, waiting for transfers between devices: 573 us -> none  [per_device(): lax.psum_scatter(term, ('req', 'kv'), scatter_dimension=0, tiled=True)[0]]
    psum x1 -> x0, waiting for transfers between devices: 292 us -> none  [per_device(): attn_sum = lax.psum(head_terms, 'kv')]
    all_to_all x1, starting transfers between devices: 5.11 us -> 242 us  [per_device(): lax.all_to_all(place_cache(k_pool, new_keys), 'req', split_axis=0, concat...]
    all_gather x1 -> x3, waiting for transfers between devices: 52.8 us -> 0.02 us  [the longest x1 0.02 us: per_device(): gate_w = lax.all_gather(w_gate, 'req', axis=1, tiled=True)]
    all_to_all x1, waiting for transfers between devices: 25 us -> 0.01 us  [per_device(): lax.all_to_all(place_cache(v_pool, new_values), 'req', split_axis=0, conc...]
    all_to_all x0 -> x1, blocking collectives: none -> 16.4 us  [reduce_to_slice(): arrived = lax.all_to_all(pieces, 'kv', 0, 0, tiled=True)]
    all_gather x0 -> x1, blocking collectives: none -> 14.9 us  [per_device(): mid_stream = lax.all_gather(mid_slice, 'kv', axis=1, tiled=True)]
  transfers between devices with their start and end apart: 5 -> 6, of which waited for: 5 -> 1; matrix products, arithmetic and copies ran while one was open for 2% -> 21% of each run, Pallas kernels for 0% -> 0%
where the time goes in v1:
time: 458 us; the launch traced here: 456 us
  starting transfers between devices  254 us (55%)
  local copies, waits for them, and re-layouts  52.4 us (11%)
  blocking collectives  47 us (10%)
  waiting for transfers between devices  36.3 us (8%)
  other arithmetic  25.1 us (5%)
  matrix products  25.1 us (5%)
  between operations  16.9 us (4%)
    all_to_all x1, starting transfers between devices, per_device(): lax.all_to_all(place_cache(k_pool, new_keys), 'req', split_axis=0, concat...  242 us
    all_to_all x1, waiting for transfers between devices, per_device(): lax.all_to_all(place_cache(k_pool, new_keys), 'req', split_axis=0, concat...  34.2 us
    all_to_all x1, blocking collectives, reduce_to_slice(): arrived = lax.all_to_all(pieces, 'kv', 0, 0, tiled=True)  16.4 us
    all_gather x1, blocking collectives, per_device(): whole_rows = lax.all_gather(hidden, 'kv', axis=1, tiled=True)  15.6 us
    all_gather x1, blocking collectives, per_device(): mid_stream = lax.all_gather(mid_slice, 'kv', axis=1, tiled=True)  14.9 us
    gather x1, local copies, waits for them, and re-layouts, value_block(): v_pool[page_ids].reshape(req_count, block_width, kv_local, head_dim)  11.4 us
    gather x1, local copies, waits for them, and re-layouts, score_block(): k_pool[page_ids].reshape(req_count, block_width, kv_local, head_dim)  11.3 us
  transfers between devices with their start and end apart: 6, of which 1 were waited for; matrix products, arithmetic and copies ran while one was open for 21% of the time, Pallas kernels for 0%

profile of v1, /device:TPU:1, one launch (start us, length us, event | category | flops | bytes accessed | tf_op | source)
XLA Modules:
  0.0 456.5 jit_solution(5833401506610360509)
XLA Ops:
  7.2 0.7 all-gather.4.cloned.1.call-update
  8.0 0.7 all-gather.6.cloned.1.call-update
  8.7 1.4 fusion.64
  12.7 1.6 iota_compare_fusion
  14.3 15.6 %all_gather.15 = bf16[64,2048]{1,0:T(8,128)(2,1)S(1)} all-gather(bf16[64,256]{1,0:T(8,128)(2,1)} %param.23), channel_id=1, replica_groups=mesh['req'=16,'kv'=8] {'kv'}, dimensions={1}, use_global_device_ids=true | all-gather | bytes 294912 | tf_op jit(solution)/shard_map/all_gather | solution.py:123
  29.8 0.2 fusion.16
  30.0 1.6 fusion.60
  31.6 0.1 multiply_reduce_fusion
  31.9 0.1 multiply_multiply_fusion
  32.0 0.2 multiply_cosine_fusion.1
  32.2 0.2 subtract_convert_fusion
  32.4 0.6 copy-done.11
  33.0 0.1 pad_maximum_fusion.1
  33.2 1.0 broadcast_in_dim.61
  34.2 17.5 %while.20 = (s32[]{:T(128)}, f32[64,1,2,4096]{3,2,0,1:T(2,128)S(1)}, s32[]{:T(128)}, s32[64,32]{1,0:T(8,128)S(1)}, bf16[174,128,128]{2,1,0:T(8,128)(2,1)}, /*ind...) while((s32[]{:T(128)}, ...), condition=%wide.region_5.6_spmd, body=%wide.region_4.5_spmd.sunk | while | flops 16844552 | bytes 25471192 | solution.py:54
  34.3 0.1 reshape.559
  34.4 11.3 %gather_fusion = bf16[256,128,128]{2,1,0:T(8,128)(2,1)} fusion(bf16[174,128,128]{2,1,0:T(8,128)(2,1)} %get-tuple-element.275, s32[1024]{0:T(1024)S(1)} %pad_clamp_fusion.7), kind=kCustom, calls=%fused_computation.clone.1 | custom fusion | bytes 16778240 | tf_op jit(solution)/shard_map/while/body/gather | solution.py:46
  45.8 5.7 %fusion.85 = f32[64,1,2,4096]{3,2,0,1:T(2,128)S(1)} fusion(f32[64,1,2,4096]{3,2,0,1:T(2,128)S(1)} %get-tuple-element.260, s32[]{:T(128)S(6)} %select_n.123, bf16[64,512,128]{2,1,0:T(8,128)(2,1)} %bitcast.114, bf16[64,1,2,128]{3,2,0,1:T(2,128)(2,1)S(1)} %get-tuple-element.276), kind=kOutput, calls=%fused_computation.16.clone.1 | convolution fusion | flops 16842752 | bytes 8683524 | tf_op jit(solution)/shard_map/while/body/rkgd,rtkd->rkgt/dot_general | solution.py:48
  51.7 1.4 multiply_reduce_fusion.1
  53.3 0.8 fusion.48
  54.1 2.5 fusion.7
  56.7 0.3 fusion.44
  57.1 0.6 copy-done.8
  57.6 3.4 fusion.22
  61.1 0.9 fusion.65
  62.0 0.1 multiply_bitcast_fusion
  62.2 3.4 divide_convert_fusion
  65.6 16.4 %while.21 = (s32[]{:T(128)}, f32[64,1,2,128]{3,2,0,1:T(2,128)S(1)}, s32[]{:T(128)}, bf16[64,1,2,4096]{3,2,0,1:T(2,128)(2,1)}, s32[64,32]{1,0:T(8,128)S(1)}, /*in...) while((s32[]{:T(128)}, f32[64,1,2,128]{3,2,0,1:T(2,128)S(1)}, ...), condition=%wide.region_9.10_spmd, body=%wide.region_8.9_spmd.sunk | while | flops 16795400 | bytes 25438424 | solution.py:81
  65.7 0.1 reshape.562
  65.8 11.4 %gather_fusion.1 = bf16[256,128,128]{2,1,0:T(8,128)(2,1)} fusion(bf16[174,128,128]{2,1,0:T(8,128)(2,1)} %get-tuple-element.312, s32[1024]{0:T(1024)S(1)} %pad_clamp_fusion.8), kind=kCustom, calls=%fused_computation.1.clone.1 | custom fusion | bytes 16778240 | tf_op jit(solution)/shard_map/while/body/gather | solution.py:72
  77.3 4.8 %fusion.88 = f32[64,1,2,128]{3,2,0,1:T(2,128)S(1)} fusion(f32[64,1,2,128]{3,2,0,1:T(2,128)S(1)} %get-tuple-element.296, bf16[64,512,128]{2,1,0:T(8,128)(2,1)} %bitcast.113, bf16[64,1,2,4096]{3,2,0,1:T(2,128)(2,1)} %get-tuple-element.310, s32[]{:T(128)S(6)} %select_n.127), kind=kOutput, calls=%fused_computation.21.clone.1 | convolution fusion | flops 16793600 | bytes 8650756 | tf_op jit(solution)/shard_map/while/body/rkgt,rtkd->rkgd/dot_general | solution.py:74
  82.1 0.8 fusion.15
  83.0 0.9 copy.59
  83.9 4.3 all-to-all-start
  88.2 0.7 all-gather.8.cloned.1.call-update
  89.0 0.7 gather_fusion.11
  89.7 0.7 gather_fusion.12
  90.4 0.7 gather_fusion.9
  91.1 0.7 gather_fusion.10
  91.8 0.1 reshape.453
  91.9 3.8 gather_fusion.3
  95.8 4.8 %gather_fusion.6 = bf16[64,128,128]{2,1,0:T(8,128)(2,1)} fusion(bf16[174,128,128]{2,1,0:T(8,128)(2,1)} %get-tuple-element.329, s32[1024]{0:T(1024)S(1)} %pad_clamp_fusion.3), kind=kCustom, calls=%fused_computation.6 | custom fusion | bytes 4194560 | tf_op jit(solution)/shard_map/gather | solution.py:150
  100.6 0.7 gather_fusion.2
  101.3 0.1 pad_maximum_fusion.3
  101.4 0.6 gather_fusion.4
  101.9 0.6 gather_fusion.7
  102.5 0.6 scatter_custom_fusion
  103.3 7.2 %bitcast_select_fusion = (bf16[16,512,128]{2,1,0:T(8,128)(2,1)}, bf16[16,512,128]{2,1,0:T(8,128)(2,1)}) fusion(pred[16,512]{1,0:T(8,128)(4,1)S(1)} %get-tuple-element.158, pred[16,512]{1,0:T(8,128)(4,1)S(1)} %get-tuple-element.157, bf16[16,128]{1,0:T(8,128)(2,1)S(1)} %gather_fusion.7, bf16[16,128]{1,0:T(8,128)(2,1)S(1)} %gather_fusion.4, ...), kind=kLoop, calls=%fused_computation.27 | loop fusion | flops 4194304 | bytes 8413184 | tf_op jit(solution)/shard_map/jit(_where)/select_n | solution.py:152
  110.5 3.7 gather_fusion.5
  114.2 241.7 %all-to-all-start.2 = ((bf16[16,512,128]{2,1,0:T(8,128)(2,1)}), bf16[16,512,128]{2,1,0:T(8,128)(2,1)}, u32[]{:S(2)}, u32[]{:S(2)}) async-start(bf16[16,512,128]{2,1,0:T(8,128)(2,1)} %gather_fusion.5), calls=%async_computation.2 | async-start | bytes 4194304 | tf_op jit(solution)/shard_map/all_to_all | solution.py:158
  355.9 2.1 gather_fusion.8
  358.0 34.2 %all-to-all-done.2 = bf16[16,512,128]{2,1,0:T(8,128)(2,1)} async-done(((bf16[16,512,128]{2,1,0:T(8,128)(2,1)}), bf16[16,512,128]{2,1,0:T(8,128)(2,1)}, u32[]{:S(2)}, u32[]{:S(2)}) %all-to-all-start.2) | async-done | bytes 2097184 | tf_op jit(solution)/shard_map/all_to_all | solution.py:158
  392.2 7.4 %all-to-all-start.3 = ((bf16[16,512,128]{2,1,0:T(8,128)(2,1)}), bf16[16,512,128]{2,1,0:T(8,128)(2,1)S(1)}, u32[]{:S(2)}, u32[]{:S(2)}) async-start(bf16[16,512,128]{2,1,0:T(8,128)(2,1)} %gather_fusion.8), calls=%async_computation.3 | async-start | bytes 4194304 | tf_op jit(solution)/shard_map/all_to_all | solution.py:161
  399.7 1.1 reduce_sum.67
  400.8 14.9 %all_gather.16 = bf16[64,2048]{1,0:T(8,128)(2,1)S(1)} all-gather(bf16[64,256]{1,0:T(8,128)(2,1)S(1)} %add_convert_fusion.1), channel_id=1, replica_groups=mesh['req'=16,'kv'=8] {'kv'}, dimensions={1}, use_global_device_ids=true | all-gather | bytes 294912 | tf_op jit(solution)/shard_map/all_gather | solution.py:175
  415.7 0.2 fusion.19
  415.9 3.7 fusion.31
  419.6 5.9 %fusion.9 = f32[64,2048]{1,0:T(8,128)} fusion(bf16[2048,768]{0,1:T(8,128)(2,1)} %all-gather.8.cloned.1.call-done, bf16[2048,768]{0,1:T(8,128)(2,1)} %all-gather.6.cloned.1.call-done, f32[64,768]{1,0:T(8,128)} %fusion.31, bf16[64,2048]{1,0:T(8,128)(2,1)S(1)} %all_gather.16, f32[2048]{0:T(1024)S(1)} %copy-done.18, f32[64]{0:T(128)S(1)} %add_rsqrt_fusion.1), kind=kOutput, calls=%fused_computation.35 | convolution fusion | flops 403472384 | bytes 7282944 | tf_op jit(solution)/shard_map/ru,cu->rc/dot_general | solution.py:180
  425.5 1.9 copy.58
  427.4 16.4 %all_to_all.20 = f32[8,64,256]{2,1,0:T(8,128)} all-to-all(f32[8,64,256]{2,1,0:T(8,128)} %bitcast.120), channel_id=1, replica_groups=mesh['req'=16,'kv'=8] {'kv'}, dimensions={0} | all-to-all | bytes 1048576 | tf_op jit(solution)/shard_map/all_to_all | solution.py:87
  443.8 1.1 reduce_sum.69
  444.9 0.6 add_convert_fusion
  445.5 3.1 copy.75
  448.6 1.3 copy.76
  (94 shorter events, 1.1 us)
Async XLA Ops:
  7.2 74.9 %copy-start = (bf16[256,2048]{1,0:T(8,128)(2,1)S(1)}, bf16[256,2048]{1,0:T(8,128)(2,1)}, u32[]{:S(2)}) copy-start(bf16[256,2048]{1,0:T(8,128)(2,1)} %param.31) | copy-start | bytes 3145732
  7.2 24.6 %copy-start.2 = (s32[64,32]{0,1:T(8,128)S(1)}, s32[64,32]{0,1:T(8,128)}, u32[]{:S(2)}) copy-start(s32[64,32]{0,1:T(8,128)} %param.35) | copy-start | bytes 24580
  7.2 24.7 %copy-start.24 = (f32[128]{0:T(128)S(1)}, f32[128]{0:T(128)}, u32[]{:S(2)}) copy-start(f32[128]{0:T(128)} %param.25) | copy-start | bytes 1540
  7.2 408.7 %all-gather.4.cloned.1.call-start = ((), (), s32[]{:S(2)}) async-start(), calls=%async_computation.4 | async-start | bytes 3342336 | tf_op jit(solution)/shard_map/all_gather | solution.py:120
  7.9 411.7 %all-gather.6.cloned.1.call-start = ((), (), s32[]{:S(2)}) async-start(), calls=%async_computation.5 | async-start | bytes 3342336 | tf_op jit(solution)/shard_map/all_gather | solution.py:121
  10.1 24.1 %copy-start.22 = (f32[64]{0:T(128)}, f32[64]{0:T(128)S(1)}, u32[]{:S(2)}) copy-start(f32[64]{0:T(128)S(1)} %get-tuple-element.162) | copy-start | bytes 772
  12.7 21.5 %copy-start.23 = (f32[64]{0:T(128)}, f32[64]{0:T(128)S(1)}, u32[]{:S(2)}) copy-start(f32[64]{0:T(128)S(1)} %multiply_power_fusion) | copy-start | bytes 772
  30.0 21.7 %copy-start.19 = (f32[64]{0:T(128)}, f32[64]{0:T(128)S(1)}, u32[]{:S(2)}) copy-start(f32[64]{0:T(128)S(1)} %add_rsqrt_fusion.3) | copy-start | bytes 772
  32.4 0.6 copy-start.11
  32.4 0.6 copy-start.13
  34.2 17.5 %copy-start.15 = (f32[2048]{0:T(1024)S(1)}, f32[2048]{0:T(1024)}, u32[]{:S(2)}) copy-start(f32[2048]{0:T(1024)} %param.24) | copy-start | bytes 24580
  34.2 19.0 %copy-start.25 = (f32[128]{0:T(128)S(1)}, f32[128]{0:T(128)}, u32[]{:S(2)}) copy-start(f32[128]{0:T(128)} %param.26) | copy-start | bytes 1540
  51.7 5.0 %copy-start.12 = (bf16[64,2,64]{2,1,0:T(2,128)(2,1)S(1)}, bf16[64,2,64]{2,1,0:T(2,128)(2,1)}, u32[]{:S(2)}) copy-start(bf16[64,2,64]{2,1,0:T(2,128)(2,1)} %copy-done.11) | copy-start | bytes 49156
  51.7 5.0 %copy-start.14 = (bf16[64,2,64]{2,1,0:T(2,128)(2,1)S(1)}, bf16[64,2,64]{2,1,0:T(2,128)(2,1)}, u32[]{:S(2)}) copy-start(bf16[64,2,64]{2,1,0:T(2,128)(2,1)} %copy-done.13) | copy-start | bytes 49156
  57.0 0.6 copy-start.8
  57.0 4.1 copy-start.6
  57.0 4.1 copy-start.16
  57.0 4.1 copy-start.20
  57.0 5.1 %copy-start.4 = (pred[64,4096]{1,0:T(8,128)(4,1)S(1)}, pred[64,4096]{1,0:T(8,128)(4,1)}, u32[]{:S(2)}) copy-start(pred[64,4096]{1,0:T(8,128)(4,1)} %iota_compare_fusion) | copy-start | bytes 786436
  57.6 3.5 copy-start.9
  65.6 16.4 %copy-start.5 = (bf16[2048,256]{1,0:T(8,128)(2,1)S(1)}, bf16[2048,256]{1,0:T(8,128)(2,1)}, u32[]{:S(2)}) copy-start(bf16[2048,256]{1,0:T(8,128)(2,1)} %param.28) | copy-start | bytes 3145732
  65.6 16.4 %copy-start.17 = (f32[2048]{0:T(1024)S(1)}, f32[2048]{0:T(1024)}, u32[]{:S(2)}) copy-start(f32[2048]{0:T(1024)} %param.24) | copy-start | bytes 24580
  65.6 16.4 %copy-start.21 = (f32[64]{0:T(128)S(1)}, f32[64]{0:T(128)}, u32[]{:S(2)}) copy-start(f32[64]{0:T(128)} %copy-done.19) | copy-start | bytes 772
  82.1 6.8 %copy-start.27 = (s32[1,16]{1,0:T(1,128)S(1)}, s32[1,16]{1,0:T(1,128)}, u32[]{:S(2)}) copy-start(s32[1,16]{1,0:T(1,128)} %param.36) | copy-start | bytes 196
  82.1 6.9 %copy-start.26 = (s32[2]{0:T(128)S(1)}, s32[2]{0:T(128)}, u32[]{:S(2)}) copy-start(s32[2]{0:T(128)} %constant.118) | copy-start | bytes 28
  83.9 30.4 %all-to-all-start = ((f32[8,64,256]{2,1,0:T(8,128)}), f32[8,64,256]{2,1,0:T(8,128)}, u32[]{:S(2)}, u32[]{:S(2)}) async-start(f32[8,64,256]{2,1,0:T(8,128)} %bitcast.95), calls=%async_computation | async-start | bytes 1048576 | tf_op jit(solution)/shard_map/all_to_all | solution.py:87
  88.2 331.4 %all-gather.8.cloned.1.call-start = ((), (), s32[]{:S(2)}) async-start(), calls=%async_computation.6 | async-start | bytes 3342336 | tf_op jit(solution)/shard_map/all_gather | solution.py:122
  95.7 4.9 %copy-start.1 = (s32[64]{0:T(128)S(1)}, s32[64]{0:T(128)}, u32[]{:S(2)}) copy-start(s32[64]{0:T(128)} %param.34) | copy-start | bytes 772
  95.7 6.2 %copy-start.7 = (bf16[64,128]{1,0:T(8,128)(2,1)S(1)}, bf16[64,128]{1,0:T(8,128)(2,1)}, u32[]{:S(2)}) copy-start(bf16[64,128]{1,0:T(8,128)(2,1)} %get-tuple-element.164) | copy-start | bytes 49156
  95.8 6.8 %copy-start.28 = (s32[1,16]{1,0:T(1,128)S(1)}, s32[1,16]{1,0:T(1,128)}, u32[]{:S(2)}) copy-start(s32[1,16]{1,0:T(1,128)} %param.37) | copy-start | bytes 196
  114.2 241.7 %copy-start.3 = (bf16[16,512,128]{2,1,0:T(8,128)(2,1)S(1)}, bf16[16,512,128]{2,1,0:T(8,128)(2,1)}, u32[]{:S(2)}) copy-start(bf16[16,512,128]{2,1,0:T(8,128)(2,1)} %get-tuple-element.151) | copy-start | bytes 6291460
  114.2 278.0 %all-to-all-start.2 = ((bf16[16,512,128]{2,1,0:T(8,128)(2,1)}), bf16[16,512,128]{2,1,0:T(8,128)(2,1)}, u32[]{:S(2)}, u32[]{:S(2)}) async-start(bf16[16,512,128]{2,1,0:T(8,128)(2,1)} %gather_fusion.5), calls=%async_computation.2 | async-start | bytes 4194304 | tf_op jit(solution)/shard_map/all_to_all | solution.py:158
  358.0 42.7 %copy-start.10 = (bf16[64,256]{1,0:T(8,128)(2,1)S(1)}, bf16[64,256]{1,0:T(8,128)(2,1)}, u32[]{:S(2)}) copy-start(bf16[64,256]{1,0:T(8,128)(2,1)} %param.23) | copy-start | bytes 98308
  358.0 57.9 %copy-start.18 = (f32[2048]{0:T(1024)S(1)}, f32[2048]{0:T(1024)}, u32[]{:S(2)}) copy-start(f32[2048]{0:T(1024)} %param.38) | copy-start | bytes 24580
  392.2 35.1 %all-to-all-start.3 = ((bf16[16,512,128]{2,1,0:T(8,128)(2,1)}), bf16[16,512,128]{2,1,0:T(8,128)(2,1)S(1)}, u32[]{:S(2)}, u32[]{:S(2)}) async-start(bf16[16,512,128]{2,1,0:T(8,128)(2,1)} %gather_fusion.8), calls=%async_computation.3 | async-start | bytes 4194304 | tf_op jit(solution)/shard_map/all_to_all | solution.py:161
Sparse Core Ops, SparseCore 0:
  10.2 50.3 all-gather.3
  62.8 46.3 all-gather.5
  111.3 286.2 all-gather.7

commit v2 on v1

--- a/solution.py
+++ b/solution.py
@@ -8,7 +8,6 @@
 
 EPSILON = 1e-06
 ROPE_BASE = 1000000.0
-SLOT_BLOCK = 4
 
 
 def rms_norm(values, scale_row):
@@ -32,30 +31,37 @@
     )
 
 
-def attend_slots(queries, new_keys, new_values, k_pool, v_pool, lengths, page_table):
+def attend_pool(queries, new_keys, new_values, k_pool, v_pool, lengths, page_table):
     req_count, kv_local, group_size, head_dim = queries.shape
-    page_size = k_pool.shape[1]
-    slot_span = page_table.shape[1] * page_size
+    pool_pages, page_size, _ = k_pool.shape
+    table_width = page_table.shape[1]
+    token_count = pool_pages * page_size
     score_scale = head_dim ** (-0.5)
-    used_pages = jnp.max(lengths) // page_size + 1
-    turn_count = (used_pages + SLOT_BLOCK - 1) // SLOT_BLOCK
-    block_width = SLOT_BLOCK * page_size
-
-    def score_block(turn_index, buffer):
-        page_ids = lax.dynamic_slice_in_dim(page_table, turn_index * SLOT_BLOCK, SLOT_BLOCK, 1)
-        key_block = k_pool[page_ids].reshape(req_count, block_width, kv_local, head_dim)
-        scores = (
-            jnp.einsum("rkgd,rtkd->rkgt", queries, key_block, preferred_element_type=jnp.float32)
-            * score_scale
-        )
-        return lax.dynamic_update_slice_in_dim(buffer, scores, turn_index * block_width, 3)
-
-    start_buffer = jnp.full((req_count, kv_local, group_size, slot_span), -jnp.inf, jnp.float32)
-    scores = lax.fori_loop(0, turn_count, score_block, start_buffer)
-    position = jnp.arange(slot_span, dtype=jnp.int32)
-    scores = jnp.where(
-        position[None, None, None, :] < lengths[:, None, None, None], scores, -jnp.inf
-    )
+    slot_ids = jnp.arange(table_width, dtype=jnp.int32)
+    in_use = slot_ids[None, :] < (lengths // page_size + 1)[:, None]
+    targets = jnp.where(in_use, page_table, pool_pages).reshape(-1)
+    owner = (
+        jnp.full((pool_pages,), -1, jnp.int32)
+        .at[targets]
+        .set(jnp.repeat(jnp.arange(req_count, dtype=jnp.int32), table_width), mode="drop")
+    )
+    first_pos = (
+        jnp.zeros((pool_pages,), jnp.int32)
+        .at[targets]
+        .set(jnp.tile(slot_ids * page_size, req_count), mode="drop")
+    )
+    token_owner = jnp.repeat(owner, page_size)
+    token_pos = (first_pos[:, None] + jnp.arange(page_size, dtype=jnp.int32)[None, :]).reshape(-1)
+    valid = (token_owner[None, :] == jnp.arange(req_count, dtype=jnp.int32)[:, None]) & (
+        token_pos[None, :] < lengths[:, None]
+    )
+    keys = k_pool.reshape(token_count, kv_local, head_dim)
+    values = v_pool.reshape(token_count, kv_local, head_dim)
+    scores = (
+        jnp.einsum("rkgd,tkd->rkgt", queries, keys, preferred_element_type=jnp.float32)
+        * score_scale
+    )
+    scores = jnp.where(valid[:, None, None, :], scores, -jnp.inf)
     own_score = (
         jnp.einsum("rkgd,rkd->rkg", queries, new_keys, preferred_element_type=jnp.float32)
         * score_scale
@@ -66,19 +72,12 @@
     denom_sum = jnp.sum(exps_all, axis=-1) + own_exp
     weights = (exps_all / denom_sum[..., None]).astype(jnp.bfloat16)
     own_weight = (own_exp / denom_sum).astype(jnp.bfloat16)
-
-    def value_block(turn_index, context_sum):
-        page_ids = lax.dynamic_slice_in_dim(page_table, turn_index * SLOT_BLOCK, SLOT_BLOCK, 1)
-        val_block = v_pool[page_ids].reshape(req_count, block_width, kv_local, head_dim)
-        weight_block = lax.dynamic_slice_in_dim(weights, turn_index * block_width, block_width, 3)
-        return context_sum + jnp.einsum(
-            "rkgt,rtkd->rkgd", weight_block, val_block, preferred_element_type=jnp.float32
-        )
-
     start_sum = jnp.einsum(
         "rkg,rkd->rkgd", own_weight, new_values, preferred_element_type=jnp.float32
     )
-    return lax.fori_loop(0, turn_count, value_block, start_sum)
+    return start_sum + jnp.einsum(
+        "rkgt,tkd->rkgd", weights, values, preferred_element_type=jnp.float32
+    )
 
 
 def reduce_to_slice(partial, kv_count, slice_width):
@@ -162,7 +161,7 @@
             place_cache(v_pool, new_values), "req", split_axis=0, concat_axis=0, tiled=True
         ),
     )
-    context = attend_slots(queries, new_keys, new_values, k_pool, v_pool, lengths, page_table)
+    context = attend_pool(queries, new_keys, new_values, k_pool, v_pool, lengths, page_table)
     gated = (jax.nn.sigmoid(gate_raw) * context.reshape(req_count, q_local * head_dim)).astype(
         jnp.bfloat16
     )

time: 458 us -> 234 us (0.51)
  starting transfers between devices: 254 us -> 19.2 us
  waiting for transfers between devices: 36.3 us -> 71.1 us
  other arithmetic: 25.1 us -> 16 us
  local copies, waits for them, and re-layouts: 52.4 us -> 43.6 us
    all_to_all x1, starting transfers between devices: 242 us -> 6.98 us  [per_device(): lax.all_to_all(place_cache(k_pool, new_keys), 'req', split_axis=0, concat...]
    all_gather x1, waiting for transfers between devices: 0.01 us -> 36.9 us  [per_device(): down_w = lax.all_gather(w_down, 'req', axis=1, tiled=True)]
    gather x2 -> x0, local copies, waits for them, and re-layouts: 22.8 us -> none  [the longest x1 11.4 us: value_block(): v_pool[page_ids].reshape(req_count, block_width, kv_local, head_dim)]
    scatter x0 -> x2, local copies, waits for them, and re-layouts: none -> 16.1 us  [the longest x1 8.04 us: attend_pool(): first_pos = jnp.zeros((pool_pages,), jnp.int32).at[targets].set(jnp.tile(...]
  transfers between devices with their start and end apart: 6 -> 6, of which waited for: 1 -> 2; matrix products, arithmetic and copies ran while one was open for 21% -> 33% of each run, Pallas kernels for 0% -> 0%
where the time goes in v2:
time: 234 us; the launch traced here: 233 us
  waiting for transfers between devices  71.1 us (30%)
  blocking collectives  44.7 us (19%)
  local copies, waits for them, and re-layouts  43.6 us (19%)
  matrix products  24.7 us (11%)
  starting transfers between devices  19.2 us (8%)
  other arithmetic  16 us (7%)
  between operations  14.2 us (6%)
    all_gather x1, waiting for transfers between devices, per_device(): down_w = lax.all_gather(w_down, 'req', axis=1, tiled=True)  36.9 us
    all_to_all x1, waiting for transfers between devices, per_device(): lax.all_to_all(place_cache(k_pool, new_keys), 'req', split_axis=0, concat...  32.1 us
    all_gather x1, blocking collectives, per_device(): whole_rows = lax.all_gather(hidden, 'kv', axis=1, tiled=True)  15.6 us
    all_to_all x1, blocking collectives, reduce_to_slice(): arrived = lax.all_to_all(pieces, 'kv', 0, 0, tiled=True)  15.1 us
    all_gather x1, blocking collectives, per_device(): mid_stream = lax.all_gather(mid_slice, 'kv', axis=1, tiled=True)  14 us
    gather x2, local copies, waits for them, and re-layouts, place_cache(): cached = pool[moved_pages].reshape(mig_count, slot_count, channels)  8.49 us
    scatter x1, local copies, waits for them, and re-layouts, attend_pool(): first_pos = jnp.zeros((pool_pages,), jnp.int32).at[targets].set(jnp.tile(...  8.04 us
    scatter x1, local copies, waits for them, and re-layouts, attend_pool(): owner = jnp.full((pool_pages,), -1, jnp.int32).at[targets].set(jnp.repeat...  8.04 us
  transfers between devices with their start and end apart: 6, of which 2 were waited for; matrix products, arithmetic and copies ran while one was open for 33% of the time, Pallas kernels for 0%

profile of v2, /device:TPU:1, one launch (start us, length us, event | category | flops | bytes accessed | tf_op | source)
XLA Modules:
  0.0 233.5 jit_solution(11153392332926695177)
XLA Ops:
  7.3 0.7 all-gather.4.cloned.1.call-update
  8.0 0.7 all-gather.6.cloned.1.call-update
  8.7 15.6 %all_gather.15 = bf16[64,2048]{1,0:T(8,128)(2,1)S(1)} all-gather(bf16[64,256]{1,0:T(8,128)(2,1)} %param.19), channel_id=1, replica_groups=mesh['req'=16,'kv'=8] {'kv'}, dimensions={1}, use_global_device_ids=true | all-gather | bytes 294912 | tf_op jit(solution)/shard_map/all_gather | solution.py:122
  24.3 0.2 fusion.20
  24.5 1.6 fusion.71
  26.1 0.1 multiply_reduce_fusion
  26.3 0.1 copy.35
  26.3 0.7 fusion.58
  27.1 1.4 multiply_reduce_fusion.1
  28.6 0.1 copy.37
  28.6 0.1 reshape.473
  28.9 8.0 %scatter_custom_fusion.1 = s32[174]{0:T(256)S(1)} fusion(s32[2048]{0:T(1024)S(1)} %bitcast.141, s32[2048]{0:T(1024)S(1)} %reshape.579, s32[]{:T(128)} %constant.29.clone.1), kind=kCustom, calls=%fused_computation.124 | custom fusion | bytes 700 | tf_op jit(solution)/shard_map/scatter | solution.py:51
  37.0 8.0 %scatter_custom_fusion = s32[174]{0:T(256)S(1)} fusion(s32[2048]{0:T(1024)S(1)} %bitcast.142, s32[2048]{0:T(1024)S(1)} %reshape.571, s32[]{:T(128)} %constant.27.clone.1), kind=kCustom, calls=%fused_computation.127 | custom fusion | bytes 700 | tf_op jit(solution)/shard_map/scatter | solution.py:46
  45.0 0.1 add_bitcast_fusion
  45.1 1.2 fusion.5
  46.3 0.1 multiply_bitcast_fusion
  46.4 0.2 fusion.52
  46.6 0.1 fusion.88
  46.7 0.2 multiply_cosine_fusion.1
  46.9 0.1 fusion.38
  47.0 0.1 subtract_convert_fusion
  47.1 0.1 pad_maximum_fusion
  47.2 0.2 fusion.48
  47.4 0.1 copy.44
  47.4 4.3 %fusion.75 = (f32[64,2]{0,1:T(2,128)S(1)}, f32[64,1,2,22272]{3,0,2,1:T(8,128)S(1)}) fusion(bf16[64,2,128]{2,0,1:T(8,128)(2,1)S(1)} %pad_maximum_fusion, bf16[22272,128,1]{1,0,2:T(8,128)(2,1)} %bitcast.133, pred[64,22272]{1,0:T(8,128)(4,1)S(1)} %fusion.5), kind=kOutput, calls=%fused_computation.141 | convolution fusion | flops 738361216 | bytes 18563584 | tf_op jit(solution)/shard_map/rkgd,tkd->rkgt/dot_general | solution.py:61
  51.8 2.3 fusion.2
  54.1 0.3 fusion.76
  54.4 5.4 %fusion.15 = f32[64,1,2,128]{3,0,2,1:T(8,128)S(1)} fusion(bf16[22272,128,1]{1,0,2:T(8,128)(2,1)} %bitcast.139, f32[64,2]{0,1:T(2,128)S(1)} %get-tuple-element.12, f32[64,1,2,22272]{3,0,2,1:T(8,128)S(1)} %get-tuple-element.26, f32[64,2]{0,1:T(2,128)S(1)} %fusion.54, f32[64,128]{1,0:T(8,128)S(1)} %get-tuple-element.27, f32[64,2]{0,1:T(2,128)S(1)} %get-tuple-element.11), kind=kOutput, calls=%fused_computation.35 | convolution fusion | flops 738394112 | bytes 17204736 | tf_op jit(solution)/shard_map/rkgt,tkd->rkgd/dot_general | solution.py:78
  59.8 2.1 fusion.19
  61.9 0.8 copy.61
  62.7 4.3 %all-to-all-start = ((f32[8,64,256]{2,1,0:T(8,128)}), f32[8,64,256]{2,1,0:T(8,128)}, u32[]{:S(2)}, u32[]{:S(2)}) async-start(f32[8,64,256]{2,1,0:T(8,128)} %bitcast.131), calls=%async_computation | async-start | bytes 1048576 | tf_op jit(solution)/shard_map/all_to_all | solution.py:86
  67.1 0.7 all-gather.8.cloned.1.call-update
  67.9 0.7 gather_fusion.9
  68.6 0.7 gather_fusion.10
  69.2 0.7 gather_fusion.7
  69.9 0.7 gather_fusion.8
  70.6 0.1 copy.41
  70.7 0.1 reshape.493
  70.8 3.7 %gather_fusion.4 = bf16[64,128,128]{2,1,0:T(8,128)(2,1)S(1)} fusion(bf16[174,128,128]{2,1,0:T(8,128)(2,1)} %param.29, s32[1024]{0:T(1024)S(1)} %pad_clamp_fusion.1), kind=kCustom, calls=%fused_computation.4 | custom fusion | bytes 4194560 | tf_op jit(solution)/shard_map/gather | solution.py:149
  74.5 4.8 %gather_fusion.1 = bf16[64,128,128]{2,1,0:T(8,128)(2,1)} fusion(bf16[174,128,128]{2,1,0:T(8,128)(2,1)} %param.28, s32[1024]{0:T(1024)S(1)} %pad_clamp_fusion.1), kind=kCustom, calls=%fused_computation.1 | custom fusion | bytes 4194560 | tf_op jit(solution)/shard_map/gather | solution.py:149
  79.3 0.7 gather_fusion
  80.0 0.1 pad_maximum_fusion.1
  80.0 0.6 gather_fusion.2
  80.6 0.6 gather_fusion.5
  81.2 0.6 scatter_custom_fusion.2
  81.9 0.1 iota_compare_fusion.2
  82.0 7.2 %bitcast_select_fusion = (bf16[16,512,128]{2,1,0:T(8,128)(2,1)}, bf16[16,512,128]{2,1,0:T(8,128)(2,1)}) fusion(pred[16,512]{1,0:T(8,128)(4,1)S(1)} %get-tuple-element.18, pred[16,512]{1,0:T(8,128)(4,1)S(1)} %get-tuple-element.17, bf16[16,128]{1,0:T(8,128)(2,1)S(1)} %gather_fusion.5, bf16[16,128]{1,0:T(8,128)(2,1)S(1)} %gather_fusion.2, ...), kind=kLoop, calls=%fused_computation.24 | loop fusion | flops 4194304 | bytes 8413184 | tf_op jit(solution)/shard_map/jit(_where)/select_n | solution.py:151
  89.2 3.9 %gather_fusion.3 = bf16[16,512,128]{2,1,0:T(8,128)(2,1)} fusion(bf16[16,512,128]{2,1,0:T(8,128)(2,1)} %get-tuple-element.10, s32[1024]{0:T(1024)S(1)} %pad_clamp_fusion), kind=kCustom, calls=%fused_computation.3 | custom fusion | bytes 4194368 | tf_op jit(solution)/shard_map/gather | solution.py:154
  93.0 7.0 %all-to-all-start.2 = ((bf16[16,512,128]{2,1,0:T(8,128)(2,1)}), bf16[16,512,128]{2,1,0:T(8,128)(2,1)}, u32[]{:S(2)}, u32[]{:S(2)}) async-start(bf16[16,512,128]{2,1,0:T(8,128)(2,1)} %gather_fusion.3), calls=%async_computation.2 | async-start | bytes 4194304 | tf_op jit(solution)/shard_map/all_to_all | solution.py:157
  100.0 2.1 gather_fusion.6
  102.2 32.1 %all-to-all-done.2 = bf16[16,512,128]{2,1,0:T(8,128)(2,1)} async-done(((bf16[16,512,128]{2,1,0:T(8,128)(2,1)}), bf16[16,512,128]{2,1,0:T(8,128)(2,1)}, u32[]{:S(2)}, u32[]{:S(2)}) %all-to-all-start.2) | async-done | bytes 2097184 | tf_op jit(solution)/shard_map/all_to_all | solution.py:157
  134.3 7.8 %all-to-all-start.3 = ((bf16[16,512,128]{2,1,0:T(8,128)(2,1)}), bf16[16,512,128]{2,1,0:T(8,128)(2,1)S(1)}, u32[]{:S(2)}, u32[]{:S(2)}) async-start(bf16[16,512,128]{2,1,0:T(8,128)(2,1)} %gather_fusion.6), calls=%async_computation.3 | async-start | bytes 4194304 | tf_op jit(solution)/shard_map/all_to_all | solution.py:160
  142.1 1.1 reduce_sum.67
  143.2 14.0 %all_gather.16 = bf16[64,2048]{1,0:T(8,128)(2,1)S(1)} all-gather(bf16[64,256]{1,0:T(8,128)(2,1)S(1)} %add_convert_fusion.1), channel_id=1, replica_groups=mesh['req'=16,'kv'=8] {'kv'}, dimensions={1}, use_global_device_ids=true | all-gather | bytes 294912 | tf_op jit(solution)/shard_map/all_gather | solution.py:174
  157.2 0.2 fusion.23
  157.4 3.7 %fusion.34 = f32[64,768]{1,0:T(8,128)} fusion(bf16[2048,768]{0,1:T(8,128)(2,1)} %all-gather.4.cloned.1.call-done, bf16[64,2048]{1,0:T(8,128)(2,1)S(1)} %all_gather.16, f32[2048]{0:T(1024)S(1)} %copy-done.7, f32[64]{0:T(128)S(1)} %add_rsqrt_fusion.1), kind=kOutput, calls=%fused_computation.58 | convolution fusion | flops 201850880 | bytes 3612928 | tf_op jit(solution)/shard_map/dot_general | solution.py:176
  161.0 36.9 %all-gather.8.cloned.1.call-done = bf16[2048,768]{0,1:T(8,128)(2,1)} async-done(((bf16[2048,48]{0,1:T(8,128)(2,1)}), bf16[2048,768]{0,1:T(8,128)(2,1)}) %all-gather.8.cloned.1.call-update) | async-done | bytes 3145744 | tf_op jit(solution)/shard_map/all_gather | solution.py:121
  197.9 5.9 %fusion.7 = f32[64,2048]{1,0:T(8,128)} fusion(bf16[2048,768]{0,1:T(8,128)(2,1)} %all-gather.8.cloned.1.call-done, bf16[2048,768]{0,1:T(8,128)(2,1)} %all-gather.6.cloned.1.call-done, f32[64,768]{1,0:T(8,128)} %fusion.34, bf16[64,2048]{1,0:T(8,128)(2,1)S(1)} %all_gather.16, f32[2048]{0:T(1024)S(1)} %copy-done.7, f32[64]{0:T(128)S(1)} %add_rsqrt_fusion.1), kind=kOutput, calls=%fused_computation.28 | convolution fusion | flops 403472384 | bytes 7282944 | tf_op jit(solution)/shard_map/ru,cu->rc/dot_general | solution.py:179
  203.8 1.9 copy.60
  205.7 15.1 %all_to_all.20 = f32[8,64,256]{2,1,0:T(8,128)} all-to-all(f32[8,64,256]{2,1,0:T(8,128)} %bitcast.138), channel_id=1, replica_groups=mesh['req'=16,'kv'=8] {'kv'}, dimensions={0} | all-to-all | bytes 1048576 | tf_op jit(solution)/shard_map/all_to_all | solution.py:86
  220.8 1.1 reduce_sum.69
  221.9 0.6 add_convert_fusion
  222.5 3.1 %copy.64 = bf16[16,512,128]{2,1,0:T(8,128)(2,1)} copy(bf16[16,512,128]{2,1,0:T(8,128)(2,1)} %all-to-all-done.2) | data formatting | bytes 4194304
  225.6 1.3 copy.65
  (62 shorter events, 0.7 us)
Async XLA Ops:
  7.2 52.6 %copy-start = (bf16[256,2048]{1,0:T(8,128)(2,1)S(1)}, bf16[256,2048]{1,0:T(8,128)(2,1)}, u32[]{:S(2)}) copy-start(bf16[256,2048]{1,0:T(8,128)(2,1)} %param.27) | copy-start | bytes 3145732
  7.2 37.9 %copy-start.1 = (s32[64]{0:T(128)S(1)}, s32[64]{0:T(128)}, u32[]{:S(2)}) copy-start(s32[64]{0:T(128)} %param.30) | copy-start | bytes 772
  7.2 21.4 %copy-start.2 = (s32[64,32]{0,1:T(8,128)S(1)}, s32[64,32]{0,1:T(8,128)}, u32[]{:S(2)}) copy-start(s32[64,32]{0,1:T(8,128)} %param.31) | copy-start | bytes 24580
  7.2 39.1 %copy-start.8 = (f32[128]{0:T(128)S(1)}, f32[128]{0:T(128)}, u32[]{:S(2)}) copy-start(f32[128]{0:T(128)} %param.22) | copy-start | bytes 1540
  7.2 39.7 %copy-start.9 = (f32[128]{0:T(128)S(1)}, f32[128]{0:T(128)}, u32[]{:S(2)}) copy-start(f32[128]{0:T(128)} %param.21) | copy-start | bytes 1540
  7.2 150.1 %all-gather.4.cloned.1.call-start = ((), (), s32[]{:S(2)}) async-start(), calls=%async_computation.4 | async-start | bytes 3342336 | tf_op jit(solution)/shard_map/all_gather | solution.py:119
  8.0 153.1 %all-gather.6.cloned.1.call-start = ((), (), s32[]{:S(2)}) async-start(), calls=%async_computation.5 | async-start | bytes 3342336 | tf_op jit(solution)/shard_map/all_gather | solution.py:120
  51.7 2.3 copy-start.4
  51.8 2.3 copy-start.6
  59.7 8.0 %copy-start.11 = (s32[1,16]{1,0:T(1,128)S(1)}, s32[1,16]{1,0:T(1,128)}, u32[]{:S(2)}) copy-start(s32[1,16]{1,0:T(1,128)} %param.32) | copy-start | bytes 196
  59.7 8.1 %copy-start.10 = (s32[2]{0:T(128)S(1)}, s32[2]{0:T(128)}, u32[]{:S(2)}) copy-start(s32[2]{0:T(128)} %constant.75) | copy-start | bytes 28
  62.7 30.3 %all-to-all-start = ((f32[8,64,256]{2,1,0:T(8,128)}), f32[8,64,256]{2,1,0:T(8,128)}, u32[]{:S(2)}, u32[]{:S(2)}) async-start(f32[8,64,256]{2,1,0:T(8,128)} %bitcast.131), calls=%async_computation | async-start | bytes 1048576 | tf_op jit(solution)/shard_map/all_to_all | solution.py:86
  67.0 130.9 %all-gather.8.cloned.1.call-start = ((), (), s32[]{:S(2)}) async-start(), calls=%async_computation.6 | async-start | bytes 3342336 | tf_op jit(solution)/shard_map/all_gather | solution.py:121
  74.5 6.7 %copy-start.12 = (s32[1,16]{1,0:T(1,128)S(1)}, s32[1,16]{1,0:T(1,128)}, u32[]{:S(2)}) copy-start(s32[1,16]{1,0:T(1,128)} %param.33) | copy-start | bytes 196
  93.0 7.0 %copy-start.3 = (bf16[16,512,128]{2,1,0:T(8,128)(2,1)S(1)}, bf16[16,512,128]{2,1,0:T(8,128)(2,1)}, u32[]{:S(2)}) copy-start(bf16[16,512,128]{2,1,0:T(8,128)(2,1)} %get-tuple-element.9) | copy-start | bytes 6291460
  93.0 41.3 %all-to-all-start.2 = ((bf16[16,512,128]{2,1,0:T(8,128)(2,1)}), bf16[16,512,128]{2,1,0:T(8,128)(2,1)}, u32[]{:S(2)}, u32[]{:S(2)}) async-start(bf16[16,512,128]{2,1,0:T(8,128)(2,1)} %gather_fusion.3), calls=%async_computation.2 | async-start | bytes 4194304 | tf_op jit(solution)/shard_map/all_to_all | solution.py:157
  102.2 41.0 %copy-start.5 = (bf16[64,256]{1,0:T(8,128)(2,1)S(1)}, bf16[64,256]{1,0:T(8,128)(2,1)}, u32[]{:S(2)}) copy-start(bf16[64,256]{1,0:T(8,128)(2,1)} %param.19) | copy-start | bytes 98308
  102.2 55.2 %copy-start.7 = (f32[2048]{0:T(1024)S(1)}, f32[2048]{0:T(1024)}, u32[]{:S(2)}) copy-start(f32[2048]{0:T(1024)} %param.34) | copy-start | bytes 24580
  134.3 71.4 %all-to-all-start.3 = ((bf16[16,512,128]{2,1,0:T(8,128)(2,1)}), bf16[16,512,128]{2,1,0:T(8,128)(2,1)S(1)}, u32[]{:S(2)}, u32[]{:S(2)}) async-start(bf16[16,512,128]{2,1,0:T(8,128)(2,1)} %gather_fusion.6), calls=%async_computation.3 | async-start | bytes 4194304 | tf_op jit(solution)/shard_map/all_to_all | solution.py:160
Sparse Core Ops, SparseCore 0:
  10.2 50.2 all-gather.3
  62.7 59.2 all-gather.5
  124.2 73.6 all-gather.7

commit v3 on v2

--- a/solution.py
+++ b/solution.py
@@ -32,28 +32,21 @@
 
 
 def attend_pool(queries, new_keys, new_values, k_pool, v_pool, lengths, page_table):
-    req_count, kv_local, group_size, head_dim = queries.shape
+    req_count, kv_local, _, head_dim = queries.shape
     pool_pages, page_size, _ = k_pool.shape
     table_width = page_table.shape[1]
     token_count = pool_pages * page_size
     score_scale = head_dim ** (-0.5)
     slot_ids = jnp.arange(table_width, dtype=jnp.int32)
     in_use = slot_ids[None, :] < (lengths // page_size + 1)[:, None]
-    targets = jnp.where(in_use, page_table, pool_pages).reshape(-1)
-    owner = (
-        jnp.full((pool_pages,), -1, jnp.int32)
-        .at[targets]
-        .set(jnp.repeat(jnp.arange(req_count, dtype=jnp.int32), table_width), mode="drop")
-    )
-    first_pos = (
-        jnp.zeros((pool_pages,), jnp.int32)
-        .at[targets]
-        .set(jnp.tile(slot_ids * page_size, req_count), mode="drop")
-    )
-    token_owner = jnp.repeat(owner, page_size)
-    token_pos = (first_pos[:, None] + jnp.arange(page_size, dtype=jnp.int32)[None, :]).reshape(-1)
-    valid = (token_owner[None, :] == jnp.arange(req_count, dtype=jnp.int32)[:, None]) & (
-        token_pos[None, :] < lengths[:, None]
+    match = (
+        page_table[:, :, None] == jnp.arange(pool_pages, dtype=jnp.int32)[None, None, :]
+    ) & in_use[:, :, None]
+    page_mine = jnp.any(match, axis=1)
+    page_start = jnp.sum(jnp.where(match, slot_ids[None, :, None] * page_size, 0), axis=1)
+    token_pos = page_start[:, :, None] + jnp.arange(page_size, dtype=jnp.int32)[None, None, :]
+    valid = (page_mine[:, :, None] & (token_pos < lengths[:, None, None])).reshape(
+        req_count, token_count
     )
     keys = k_pool.reshape(token_count, kv_local, head_dim)
     values = v_pool.reshape(token_count, kv_local, head_dim)
@@ -87,7 +80,7 @@
     return jnp.sum(arrived, axis=0)
 
 
-def per_device(
+def layer_body(
     hidden,
     attn_gain,
     q_gain,
@@ -116,9 +109,13 @@
     page_size = k_pool.shape[1]
     channels = kv_local * head_dim
     model_width = mlp_gain.shape[0]
-    gate_w = lax.all_gather(w_gate, "req", axis=1, tiled=True)
-    up_w = lax.all_gather(w_up, "req", axis=1, tiled=True)
-    down_w = lax.all_gather(w_down, "req", axis=1, tiled=True)
+    unit_count = w_gate.shape[1]
+    stacked = lax.all_gather(
+        jnp.concatenate([w_gate, w_up, w_down], axis=1), "req", axis=0, tiled=False
+    )
+    gate_w = stacked[:, :, :unit_count]
+    up_w = stacked[:, :, unit_count : 2 * unit_count]
+    down_w = stacked[:, :, 2 * unit_count :]
     whole_rows = lax.all_gather(hidden, "kv", axis=1, tiled=True)
     normed = rms_norm(whole_rows, attn_gain).astype(jnp.bfloat16)
     query_raw = jnp.dot(normed, w_q, preferred_element_type=jnp.float32).reshape(
@@ -173,11 +170,11 @@
     ).astype(jnp.bfloat16)
     mid_stream = lax.all_gather(mid_slice, "kv", axis=1, tiled=True)
     normed_mlp = rms_norm(mid_stream, mlp_gain).astype(jnp.bfloat16)
-    gate_part = jnp.dot(normed_mlp, gate_w, preferred_element_type=jnp.float32)
-    up_part = jnp.dot(normed_mlp, up_w, preferred_element_type=jnp.float32)
+    gate_part = jnp.einsum("rd,sdu->rsu", normed_mlp, gate_w, preferred_element_type=jnp.float32)
+    up_part = jnp.einsum("rd,sdu->rsu", normed_mlp, up_w, preferred_element_type=jnp.float32)
     activation = (jax.nn.silu(gate_part) * up_part).astype(jnp.bfloat16)
     down_part = jnp.einsum(
-        "ru,cu->rc", activation, down_w, preferred_element_type=jnp.float32
+        "rsu,scu->rc", activation, down_w, preferred_element_type=jnp.float32
     )
     mlp_part = reduce_to_slice(down_part, kv_count, slice_width)
     out_hidden = (mid_slice.astype(jnp.float32) + mlp_part).astype(jnp.bfloat16)
@@ -186,7 +183,7 @@
 
 def solution(mesh):
     return jax.shard_map(
-        per_device,
+        layer_body,
         mesh=mesh,
         in_specs=(
             P("req", "kv"),

time: 234 us -> 178 us (0.76)
  waiting for transfers between devices: 71.1 us -> 13 us
  local copies, waits for them, and re-layouts: 43.6 us -> 51.9 us
  matrix products: 24.7 us -> 17.3 us
  other arithmetic: 16 us -> 19.7 us
  starting transfers between devices: 19.2 us -> 16.1 us
    all_gather x3 -> x1, waiting for transfers between devices: 36.9 us -> 0.02 us  [layer_body(): lax.all_gather(jnp.concatenate([w_gate, w_up, w_down], axis=1), 'req', ax...]
    all_to_all x2, waiting for transfers between devices: 32.1 us -> 13 us  [the longest x1 13 us: layer_body(): lax.all_to_all(place_cache(k_pool, new_keys), 'req', split_axis=0, concat...]
    unnamed x28 -> x38, local copies, waits for them, and re-layouts: 4.5 us -> 22.8 us
    scatter x3 -> x1, local copies, waits for them, and re-layouts: 16.7 us -> 0.62 us  [layer_body(): jnp.zeros_like(dest_row).at[dest_row]]
    dot_general x6 -> x5, matrix products: 14.9 us -> 5.43 us  [the longest x1 2.32 us: layer_body(): jnp.einsum('rsu,scu->rc', activation, down_w, preferred_element_type=jnp....]
    slice x0 -> x1, local copies, waits for them, and re-layouts: none -> 4.55 us  [layer_body(): gate_w = stacked[:, :, :unit_count]]
    all_to_all x2, starting transfers between devices: 14.8 us -> 11.7 us  [the longest x1 6.62 us: layer_body(): lax.all_to_all(place_cache(k_pool, new_keys), 'req', split_axis=0, concat...]
    and x1, other arithmetic: 1.17 us -> 3.88 us  [attend_pool(): page_mine[:, :, None] & (token_pos < lengths[:, None, None])]
  transfers between devices with their start and end apart: 6 -> 4, of which waited for: 2 -> 1; matrix products, arithmetic and copies ran while one was open for 33% -> 46% of each run, Pallas kernels for 0% -> 0%
where the time goes in v3:
time: 178 us; the launch traced here: 177 us
  local copies, waits for them, and re-layouts  51.9 us (29%)
  blocking collectives  44.9 us (25%)
  other arithmetic  19.7 us (11%)
  matrix products  17.3 us (10%)
  starting transfers between devices  16.1 us (9%)
  between operations  14.6 us (8%)
  waiting for transfers between devices  13 us (7%)
    unnamed x38, local copies, waits for them, and re-layouts  22.8 us
    all_gather x1, blocking collectives, layer_body(): whole_rows = lax.all_gather(hidden, 'kv', axis=1, tiled=True)  15.6 us
    all_to_all x1, blocking collectives, reduce_to_slice(): arrived = lax.all_to_all(pieces, 'kv', 0, 0, tiled=True)  15.4 us
    all_gather x1, blocking collectives, layer_body(): mid_stream = lax.all_gather(mid_slice, 'kv', axis=1, tiled=True)  13.9 us
    all_to_all x1, waiting for transfers between devices, layer_body(): lax.all_to_all(place_cache(k_pool, new_keys), 'req', split_axis=0, concat...  13 us
    gather x2, local copies, waits for them, and re-layouts, place_cache(): cached = pool[moved_pages].reshape(mig_count, slot_count, channels)  8.67 us
    select_n x1, other arithmetic, place_cache(): jnp.where(slot_pos < moved_len, cached, jnp.where(slot_pos == moved_len,...  7.25 us
    all_to_all x1, starting transfers between devices, layer_body(): lax.all_to_all(place_cache(k_pool, new_keys), 'req', split_axis=0, concat...  6.62 us
  transfers between devices with their start and end apart: 4, of which 1 were waited for; matrix products, arithmetic and copies ran while one was open for 46% of the time, Pallas kernels for 0%

profile of v3, /device:TPU:1, one launch (start us, length us, event | category | flops | bytes accessed | tf_op | source)
XLA Modules:
  0.0 177.5 jit_solution(1352648915899886418)
XLA Ops:
  7.3 2.1 %pad_maximum_fusion = bf16[2048,144]{0,1:T(8,128)(2,1)} fusion(bf16[2048,48]{0,1:T(8,128)(2,1)} %param.37, bf16[2048,48]{0,1:T(8,128)(2,1)} %param.36, bf16[2048,48]{0,1:T(8,128)(2,1)} %param.35), kind=kLoop, calls=%fused_computation.45 | loop fusion | flops 1769472 | bytes 1179648 | tf_op jit(solution)/shard_map/concatenate | solution.py:114
  9.4 15.6 %all_gather.12 = bf16[64,2048]{1,0:T(8,128)(2,1)S(1)} all-gather(bf16[64,256]{1,0:T(8,128)(2,1)} %param.19), channel_id=1, replica_groups=mesh['req'=16,'kv'=8] {'kv'}, dimensions={1}, use_global_device_ids=true | all-gather | bytes 294912 | tf_op jit(solution)/shard_map/all_gather | solution.py:119
  25.0 0.2 fusion.23
  25.2 1.6 fusion.64
  26.8 0.1 multiply_reduce_fusion
  26.9 0.1 copy.51
  27.0 0.4 multiply_reduce_fusion.1
  27.5 0.1 multiply_bitcast_fusion
  27.5 0.2 fusion.50
  27.7 0.1 fusion.81
  27.8 0.2 multiply_cosine_fusion.1
  28.0 0.1 fusion.36
  28.1 0.1 subtract_convert_fusion
  28.2 0.1 pad_maximum_fusion.1
  28.3 0.2 fusion.46
  28.5 0.1 copy.63
  28.6 0.1 copy.53
  28.7 0.1 iota_compare_fusion.3
  28.8 0.7 fusion.10
  29.5 1.0 select_reduce_fusion
  30.6 1.6 add.138
  32.2 2.1 %and.30 = pred[64,174,128]{2,1,0:T(8,128)(4,1)S(1)} broadcast(pred[64,174]{1,0:T(8,128)(4,1)S(1)} %fusion.10), dimensions={0,1} | broadcast | bytes 1436544 | tf_op jit(solution)/shard_map/and | solution.py:48
  34.3 3.9 %fusion.6 = pred[64,22272]{1,0:T(8,128)(4,1)S(1)} fusion(s32[8,8,174,128]{3,2,1,0:T(8,128)S(1)} %bitcast.153, pred[8,8,174,128]{3,2,1,0:T(8,128)(4,1)S(1)} %bitcast.160, s32[64]{0:T(128)S(1)} %copy-done.2, s32[22272]{0:T(1024)S(1)} %iota_bitcast_fusion), kind=kLoop, calls=%fused_computation.22 | loop fusion | flops 4276224 | bytes 8641792 | tf_op jit(solution)/shard_map/and | solution.py:48
  38.2 4.2 %fusion.69 = (f32[64,2]{0,1:T(2,128)S(1)}, f32[64,1,2,22272]{3,0,2,1:T(8,128)S(1)}) fusion(bf16[64,2,128]{2,0,1:T(8,128)(2,1)S(1)} %pad_maximum_fusion.1, bf16[22272,128,1]{1,0,2:T(8,128)(2,1)} %bitcast.156, pred[64,22272]{1,0:T(8,128)(4,1)S(1)} %fusion.6), kind=kOutput, calls=%fused_computation.135 | convolution fusion | flops 738361216 | bytes 18563584 | tf_op jit(solution)/shard_map/rkgd,tkd->rkgt/dot_general | solution.py:54
  42.5 2.3 %fusion.2 = f32[64,2]{0,1:T(2,128)S(1)} fusion(f32[64,1,2,22272]{3,0,2,1:T(8,128)S(1)} %get-tuple-element.29, f32[64,2]{0,1:T(2,128)S(1)} %fusion.51), kind=kLoop, calls=%fused_computation.17 | loop fusion | flops 5701504 | bytes 11404288 | tf_op jit(solution)/shard_map/reduce_sum | solution.py:65
  44.8 0.3 fusion.70
  45.1 5.3 %fusion.18 = f32[64,1,2,128]{3,0,2,1:T(8,128)S(1)} fusion(bf16[22272,128,1]{1,0,2:T(8,128)(2,1)} %bitcast.163, f32[64,2]{0,1:T(2,128)S(1)} %get-tuple-element.15, f32[64,1,2,22272]{3,0,2,1:T(8,128)S(1)} %get-tuple-element.29, f32[64,2]{0,1:T(2,128)S(1)} %fusion.51, f32[64,128]{1,0:T(8,128)S(1)} %get-tuple-element.30, f32[64,2]{0,1:T(2,128)S(1)} %get-tuple-element.14), kind=kOutput, calls=%fused_computation.37 | convolution fusion | flops 738394112 | bytes 17204736 | tf_op jit(solution)/shard_map/rkgt,tkd->rkgd/dot_general | solution.py:71
  50.5 0.9 fusion.22
  51.4 0.8 copy.92
  52.2 4.3 %all-to-all-start = ((f32[8,64,256]{2,1,0:T(8,128)}), f32[8,64,256]{2,1,0:T(8,128)S(1)}, u32[]{:S(2)}, u32[]{:S(2)}) async-start(f32[8,64,256]{2,1,0:T(8,128)} %bitcast.150), calls=%async_computation | async-start | bytes 1048576 | tf_op jit(solution)/shard_map/all_to_all | solution.py:79
  56.6 0.1 iota_add_fusion.2
  56.7 0.7 gather_fusion.9
  57.3 0.7 gather_fusion.10
  58.0 0.7 gather_fusion.7
  58.7 0.7 gather_fusion.8
  59.4 0.1 copy.60
  59.5 0.1 reshape.450
  59.6 3.7 %gather_fusion.4 = bf16[64,128,128]{2,1,0:T(8,128)(2,1)S(1)} fusion(bf16[174,128,128]{2,1,0:T(8,128)(2,1)} %param.29, s32[1024]{0:T(1024)S(1)} %pad_clamp_fusion.1), kind=kCustom, calls=%fused_computation.4 | custom fusion | bytes 4194560 | tf_op jit(solution)/shard_map/gather | solution.py:146
  63.3 5.0 %gather_fusion.1 = bf16[64,128,128]{2,1,0:T(8,128)(2,1)} fusion(bf16[174,128,128]{2,1,0:T(8,128)(2,1)} %param.28, s32[1024]{0:T(1024)S(1)} %pad_clamp_fusion.1), kind=kCustom, calls=%fused_computation.1 | custom fusion | bytes 4194560 | tf_op jit(solution)/shard_map/gather | solution.py:146
  68.3 0.7 gather_fusion
  68.9 0.1 pad_maximum_fusion.2
  69.0 0.6 gather_fusion.2
  69.6 0.6 gather_fusion.5
  70.2 0.6 scatter_custom_fusion
  70.8 0.1 iota_compare_fusion.2
  70.9 7.3 %bitcast_select_fusion = (bf16[16,512,128]{2,1,0:T(8,128)(2,1)}, bf16[16,512,128]{2,1,0:T(8,128)(2,1)}) fusion(pred[16,512]{1,0:T(8,128)(4,1)S(1)} %get-tuple-element.21, pred[16,512]{1,0:T(8,128)(4,1)S(1)} %get-tuple-element.20, bf16[16,128]{1,0:T(8,128)(2,1)S(1)} %gather_fusion.5, bf16[16,128]{1,0:T(8,128)(2,1)S(1)} %gather_fusion.2, ...), kind=kLoop, calls=%fused_computation.25 | loop fusion | flops 4194304 | bytes 8413184 | tf_op jit(solution)/shard_map/jit(_where)/select_n | solution.py:148
  78.2 3.7 %gather_fusion.3 = bf16[16,512,128]{2,1,0:T(8,128)(2,1)} fusion(bf16[16,512,128]{2,1,0:T(8,128)(2,1)} %get-tuple-element.13, s32[1024]{0:T(1024)S(1)} %pad_clamp_fusion), kind=kCustom, calls=%fused_computation.3 | custom fusion | bytes 4194368 | tf_op jit(solution)/shard_map/gather | solution.py:151
  81.9 6.6 %all-to-all-start.2 = ((bf16[16,512,128]{2,1,0:T(8,128)(2,1)}), bf16[16,512,128]{2,1,0:T(8,128)(2,1)}, u32[]{:S(2)}, u32[]{:S(2)}) async-start(bf16[16,512,128]{2,1,0:T(8,128)(2,1)} %gather_fusion.3), calls=%async_computation.2 | async-start | bytes 4194304 | tf_op jit(solution)/shard_map/all_to_all | solution.py:154
  88.5 2.1 %gather_fusion.6 = bf16[16,512,128]{2,1,0:T(8,128)(2,1)} fusion(bf16[16,512,128]{2,1,0:T(8,128)(2,1)S(1)} %copy-done.4, s32[1024]{0:T(1024)S(1)} %pad_clamp_fusion), kind=kCustom, calls=%fused_computation.6 | custom fusion | bytes 4194368 | tf_op jit(solution)/shard_map/gather | solution.py:151
  90.7 13.9 %all_gather.13 = bf16[64,2048]{1,0:T(8,128)(2,1)S(1)} all-gather(bf16[64,256]{1,0:T(8,128)(2,1)S(1)} %add_convert_fusion.1), channel_id=1, replica_groups=mesh['req'=16,'kv'=8] {'kv'}, dimensions={1}, use_global_device_ids=true | all-gather | bytes 294912 | tf_op jit(solution)/shard_map/all_gather | solution.py:171
  104.7 0.2 fusion.26
  104.8 13.0 %all-to-all-done.2 = bf16[16,512,128]{2,1,0:T(8,128)(2,1)} async-done(((bf16[16,512,128]{2,1,0:T(8,128)(2,1)}), bf16[16,512,128]{2,1,0:T(8,128)(2,1)}, u32[]{:S(2)}, u32[]{:S(2)}) %all-to-all-start.2) | async-done | bytes 2097184 | tf_op jit(solution)/shard_map/all_to_all | solution.py:154
  117.8 5.1 %all-to-all-start.3 = ((bf16[16,512,128]{2,1,0:T(8,128)(2,1)}), bf16[16,512,128]{2,1,0:T(8,128)(2,1)S(1)}, u32[]{:S(2)}, u32[]{:S(2)}) async-start(bf16[16,512,128]{2,1,0:T(8,128)(2,1)} %gather_fusion.6), calls=%async_computation.3 | async-start | bytes 4194304 | tf_op jit(solution)/shard_map/all_to_all | solution.py:157
  122.9 14.6 %copy.73 = bf16[18,8,16,2048]{3,2,1,0:T(8,128)(2,1)} copy(bf16[18,8,16,2048]{3,1,2,0:T(8,128)(2,1)} %bitcast.157) | data formatting | bytes 18874368
  137.6 4.5 %fusion.68 = (bf16[16,2048,48]{1,0,2:T(8,128)(2,1)S(1)}, bf16[16,2048,48]{1,0,2:T(8,128)(2,1)S(1)}, bf16[16,2048,48]{1,0,2:T(8,128)(2,1)S(1)}) fusion(bf16[16,2048,144]{1,0,2:T(8,128)(2,1)} %bitcast.152), kind=kLoop, calls=%fused_computation.134 | loop fusion | bytes 18874368 | tf_op jit(solution)/shard_map/slice | solution.py:116
  142.1 1.7 copy.64
  143.9 1.7 copy.65
  145.6 1.0 fusion.32
  146.6 1.0 fusion.30
  147.7 2.3 %fusion.7 = f32[64,2048,1]{1,0,2:T(8,128)S(1)} fusion(bf16[16,2048,48]{1,0,2:T(8,128)(2,1)S(1)} %get-tuple-element.7, f32[64,16,48]{0,2,1:T(8,128)S(1)} %bitcast.166, f32[64,16,48]{0,2,1:T(8,128)S(1)} %bitcast.165), kind=kOutput, calls=%fused_computation.23 | convolution fusion | flops 201621504 | bytes 4063232 | tf_op jit(solution)/shard_map/rsu,scu->rc/dot_general | solution.py:176
  150.1 15.4 %all_to_all.20 = f32[8,64,256]{2,1,0:T(8,128)S(1)} all-to-all(f32[8,64,256]{2,1,0:T(8,128)S(1)} %bitcast.162), channel_id=1, replica_groups=mesh['req'=16,'kv'=8] {'kv'}, dimensions={0} | all-to-all | bytes 1048576 | tf_op jit(solution)/shard_map/all_to_all | solution.py:79
  165.5 0.6 add_convert_fusion
  166.1 3.2 %copy.95 = bf16[16,512,128]{2,1,0:T(8,128)(2,1)} copy(bf16[16,512,128]{2,1,0:T(8,128)(2,1)} %all-to-all-done.2) | data formatting | bytes 4194304
  169.3 1.3 copy.96
  (64 shorter events, 0.5 us)
Async XLA Ops:
  7.2 43.3 %copy-start = (bf16[256,2048]{1,0:T(8,128)(2,1)S(1)}, bf16[256,2048]{1,0:T(8,128)(2,1)}, u32[]{:S(2)}) copy-start(bf16[256,2048]{1,0:T(8,128)(2,1)} %param.27) | copy-start | bytes 3145732
  7.2 19.8 %copy-start.8 = (f32[2048]{0:T(1024)S(1)}, f32[2048]{0:T(1024)}, u32[]{:S(2)}) copy-start(f32[2048]{0:T(1024)} %param.20) | copy-start | bytes 24580
  7.2 19.8 %copy-start.13 = (bf16[2048,128]{1,0:T(8,128)(2,1)S(1)}, bf16[2048,128]{1,0:T(8,128)(2,1)}, u32[]{:S(2)}) copy-start(bf16[2048,128]{1,0:T(8,128)(2,1)} %param.25) | copy-start | bytes 1572868
  7.2 20.2 %copy-start.2 = (s32[64]{0:T(128)S(1)}, s32[64]{0:T(128)}, u32[]{:S(2)}) copy-start(s32[64]{0:T(128)} %param.30) | copy-start | bytes 772
  7.2 20.2 %copy-start.10 = (f32[128]{0:T(128)S(1)}, f32[128]{0:T(128)}, u32[]{:S(2)}) copy-start(f32[128]{0:T(128)} %param.22) | copy-start | bytes 1540
  7.2 20.8 %copy-start.11 = (f32[128]{0:T(128)S(1)}, f32[128]{0:T(128)}, u32[]{:S(2)}) copy-start(f32[128]{0:T(128)} %param.21) | copy-start | bytes 1540
  7.2 21.4 %copy-start.3 = (s32[64,32]{0,1:T(8,128)S(1)}, s32[64,32]{0,1:T(8,128)}, u32[]{:S(2)}) copy-start(s32[64,32]{0,1:T(8,128)} %param.31) | copy-start | bytes 24580
  7.2 115.7 %all-gather.3.cloned.1.call-start = ((), (), s32[]{:S(2)}) async-start(), calls=%async_computation.4 | async-start | bytes 10027008 | tf_op jit(solution)/shard_map/all_gather | solution.py:113
  42.5 2.3 %copy-start.6 = (bf16[2048,128]{1,0:T(8,128)(2,1)S(1)}, bf16[2048,128]{1,0:T(8,128)(2,1)}, u32[]{:S(2)}) copy-start(bf16[2048,128]{1,0:T(8,128)(2,1)} %param.26) | copy-start | bytes 1572868
  45.1 5.4 %copy-start.5 = (bf16[2048,256]{1,0:T(8,128)(2,1)S(1)}, bf16[2048,256]{1,0:T(8,128)(2,1)}, u32[]{:S(2)}) copy-start(bf16[2048,256]{1,0:T(8,128)(2,1)} %param.24) | copy-start | bytes 3145732
  50.4 6.1 %copy-start.14 = (s32[1,16]{1,0:T(1,128)S(1)}, s32[1,16]{1,0:T(1,128)}, u32[]{:S(2)}) copy-start(s32[1,16]{1,0:T(1,128)} %param.32) | copy-start | bytes 196
  50.4 6.1 %copy-start.12 = (s32[2]{0:T(128)S(1)}, s32[2]{0:T(128)}, u32[]{:S(2)}) copy-start(s32[2]{0:T(128)} %constant.73) | copy-start | bytes 28
  52.2 29.7 %all-to-all-start = ((f32[8,64,256]{2,1,0:T(8,128)}), f32[8,64,256]{2,1,0:T(8,128)S(1)}, u32[]{:S(2)}, u32[]{:S(2)}) async-start(f32[8,64,256]{2,1,0:T(8,128)} %bitcast.150), calls=%async_computation | async-start | bytes 1048576 | tf_op jit(solution)/shard_map/all_to_all | solution.py:79
  63.3 6.9 %copy-start.15 = (s32[1,16]{1,0:T(1,128)S(1)}, s32[1,16]{1,0:T(1,128)}, u32[]{:S(2)}) copy-start(s32[1,16]{1,0:T(1,128)} %param.33) | copy-start | bytes 196
  81.9 6.6 %copy-start.4 = (bf16[16,512,128]{2,1,0:T(8,128)(2,1)S(1)}, bf16[16,512,128]{2,1,0:T(8,128)(2,1)}, u32[]{:S(2)}) copy-start(bf16[16,512,128]{2,1,0:T(8,128)(2,1)} %get-tuple-element.12) | copy-start | bytes 6291460
  81.9 35.9 %all-to-all-start.2 = ((bf16[16,512,128]{2,1,0:T(8,128)(2,1)}), bf16[16,512,128]{2,1,0:T(8,128)(2,1)}, u32[]{:S(2)}, u32[]{:S(2)}) async-start(bf16[16,512,128]{2,1,0:T(8,128)(2,1)} %gather_fusion.3), calls=%async_computation.2 | async-start | bytes 4194304 | tf_op jit(solution)/shard_map/all_to_all | solution.py:154
  88.5 2.2 %copy-start.7 = (bf16[64,256]{1,0:T(8,128)(2,1)S(1)}, bf16[64,256]{1,0:T(8,128)(2,1)}, u32[]{:S(2)}) copy-start(bf16[64,256]{1,0:T(8,128)(2,1)} %param.19) | copy-start | bytes 98308
  117.8 32.3 %all-to-all-start.3 = ((bf16[16,512,128]{2,1,0:T(8,128)(2,1)}), bf16[16,512,128]{2,1,0:T(8,128)(2,1)S(1)}, u32[]{:S(2)}, u32[]{:S(2)}) async-start(bf16[16,512,128]{2,1,0:T(8,128)(2,1)} %gather_fusion.6), calls=%async_computation.3 | async-start | bytes 4194304 | tf_op jit(solution)/shard_map/all_to_all | solution.py:157
  143.8 1.7 copy-start.9
  166.1 4.5 %copy-start.1 = (bf16[256,2048]{1,0:T(8,128)(2,1)S(1)}, bf16[256,2048]{1,0:T(8,128)(2,1)}, u32[]{:S(2)}) copy-start(bf16[256,2048]{1,0:T(8,128)(2,1)} %param.27) | copy-start | bytes 3145732
Sparse Core Ops, SparseCore 0:
  10.3 78.4 all-gather.2

commit v4 on v3

--- a/solution.py
+++ b/solution.py
@@ -111,11 +111,11 @@
     model_width = mlp_gain.shape[0]
     unit_count = w_gate.shape[1]
     stacked = lax.all_gather(
-        jnp.concatenate([w_gate, w_up, w_down], axis=1), "req", axis=0, tiled=False
-    )
-    gate_w = stacked[:, :, :unit_count]
-    up_w = stacked[:, :, unit_count : 2 * unit_count]
-    down_w = stacked[:, :, 2 * unit_count :]
+        jnp.concatenate([w_gate.T, w_up.T, w_down.T], axis=0), "req", axis=0, tiled=False
+    )
+    gate_w = stacked[:, :unit_count, :]
+    up_w = stacked[:, unit_count : 2 * unit_count, :]
+    down_w = stacked[:, 2 * unit_count :, :]
     whole_rows = lax.all_gather(hidden, "kv", axis=1, tiled=True)
     normed = rms_norm(whole_rows, attn_gain).astype(jnp.bfloat16)
     query_raw = jnp.dot(normed, w_q, preferred_element_type=jnp.float32).reshape(
@@ -136,28 +136,29 @@
     dest_row = mig_dest[0]
     mig_count = mig_rows.shape[0]
     slot_count = MIGP * page_size
-    moved_pages = page_table[mig_rows, :MIGP]
+    inverse = jnp.zeros_like(dest_row).at[dest_row].set(jnp.arange(mig_count, dtype=jnp.int32))
+    sent_rows = mig_rows[inverse]
+    moved_pages = page_table[sent_rows, :MIGP]
     slot_pos = jnp.arange(slot_count, dtype=jnp.int32)[None, :, None]
-    moved_len = lengths[mig_rows][:, None, None]
+    moved_len = lengths[sent_rows][:, None, None]
     zero_value = jnp.zeros((), jnp.bfloat16)
-    inverse = jnp.zeros_like(dest_row).at[dest_row].set(jnp.arange(mig_count, dtype=jnp.int32))
 
     def place_cache(pool, fresh_rows):
         cached = pool[moved_pages].reshape(mig_count, slot_count, channels)
-        fresh_row = fresh_rows.reshape(req_count, channels)[mig_rows][:, None, :]
-        filled = jnp.where(
+        fresh_row = fresh_rows.reshape(req_count, channels)[sent_rows][:, None, :]
+        return jnp.where(
             slot_pos < moved_len, cached, jnp.where(slot_pos == moved_len, fresh_row, zero_value)
         )
-        return filled[inverse]
-
-    mig_keys, mig_values = (
-        lax.all_to_all(
-            place_cache(k_pool, new_keys), "req", split_axis=0, concat_axis=0, tiled=True
-        ),
-        lax.all_to_all(
-            place_cache(v_pool, new_values), "req", split_axis=0, concat_axis=0, tiled=True
-        ),
-    )
+
+    moving = lax.all_to_all(
+        jnp.stack([place_cache(k_pool, new_keys), place_cache(v_pool, new_values)], axis=1),
+        "req",
+        0,
+        0,
+        tiled=True,
+    )
+    mig_keys = moving[:, 0]
+    mig_values = moving[:, 1]
     context = attend_pool(queries, new_keys, new_values, k_pool, v_pool, lengths, page_table)
     gated = (jax.nn.sigmoid(gate_raw) * context.reshape(req_count, q_local * head_dim)).astype(
         jnp.bfloat16
@@ -170,11 +171,11 @@
     ).astype(jnp.bfloat16)
     mid_stream = lax.all_gather(mid_slice, "kv", axis=1, tiled=True)
     normed_mlp = rms_norm(mid_stream, mlp_gain).astype(jnp.bfloat16)
-    gate_part = jnp.einsum("rd,sdu->rsu", normed_mlp, gate_w, preferred_element_type=jnp.float32)
-    up_part = jnp.einsum("rd,sdu->rsu", normed_mlp, up_w, preferred_element_type=jnp.float32)
+    gate_part = jnp.einsum("rd,sud->rsu", normed_mlp, gate_w, preferred_element_type=jnp.float32)
+    up_part = jnp.einsum("rd,sud->rsu", normed_mlp, up_w, preferred_element_type=jnp.float32)
     activation = (jax.nn.silu(gate_part) * up_part).astype(jnp.bfloat16)
     down_part = jnp.einsum(
-        "rsu,scu->rc", activation, down_w, preferred_element_type=jnp.float32
+        "rsu,suc->rc", activation, down_w, preferred_element_type=jnp.float32
     )
     mlp_part = reduce_to_slice(down_part, kv_count, slice_width)
     out_hidden = (mid_slice.astype(jnp.float32) + mlp_part).astype(jnp.bfloat16)

time: 178 us -> 177 us (level); the launches traced: 177 us -> 174 us
  local copies, waits for them, and re-layouts: 51.9 us -> 25 us
  waiting for transfers between devices: 13 us -> 35.9 us
  blocking collectives: 44.9 us -> 29.5 us
  starting transfers between devices: 16.1 us -> 28.4 us
  other arithmetic: 19.7 us -> 21.7 us
    unnamed x38 -> x33, local copies, waits for them, and re-layouts: 22.8 us -> 0.17 us
    all_to_all x2 -> x1, waiting for transfers between devices: 13 us -> 31.3 us  [layer_body(): lax.all_to_all(jnp.stack([place_cache(k_pool, new_keys), place_cache(v_po...]
    all_to_all x1 -> x2, starting transfers between devices: 4.34 us -> 21.2 us  [reduce_to_slice(): arrived = lax.all_to_all(pieces, 'kv', 0, 0, tiled=True)]
    all_to_all x1 -> x0, blocking collectives: 15.4 us -> none  [reduce_to_slice(): arrived = lax.all_to_all(pieces, 'kv', 0, 0, tiled=True)]
    dot_general x1 -> x2, matrix products: 2.32 us -> 8.12 us  [the longest x1 5.18 us: layer_body(): jnp.einsum('rsu,suc->rc', activation, down_w, preferred_element_type=jnp....]
    gather x9 -> x8, local copies, waits for them, and re-layouts: 10.3 us -> 5.12 us  [the longest x4 2.66 us: layer_body(): moved_pages = page_table[sent_rows, :MIGP]]
    squeeze x0 -> x1, local copies, waits for them, and re-layouts: none -> 4.69 us  [layer_body(): mig_values = moving[:, 1]]
    all_to_all x1 -> x2, waiting for transfers between devices: 0.01 us -> 4.66 us  [reduce_to_slice(): arrived = lax.all_to_all(pieces, 'kv', 0, 0, tiled=True)]
  transfers between devices with their start and end apart: 4 -> 4, of which waited for: 1 -> 2; matrix products, arithmetic and copies ran while one was open for 46% -> 36% of each run, Pallas kernels for 0% -> 0%
where the time goes in v4:
time: 177 us; the launch traced here: 174 us
  waiting for transfers between devices  35.9 us (20%)
  blocking collectives  29.5 us (17%)
  starting transfers between devices  28.4 us (16%)
  local copies, waits for them, and re-layouts  25 us (14%)
  other arithmetic  21.7 us (12%)
  matrix products  18.9 us (11%)
  between operations  14.6 us (8%)
    all_to_all x1, waiting for transfers between devices, layer_body(): lax.all_to_all(jnp.stack([place_cache(k_pool, new_keys), place_cache(v_po...  31.3 us
    all_to_all x2, starting transfers between devices, reduce_to_slice(): arrived = lax.all_to_all(pieces, 'kv', 0, 0, tiled=True)  21.2 us
    all_gather x1, blocking collectives, layer_body(): whole_rows = lax.all_gather(hidden, 'kv', axis=1, tiled=True)  15.6 us
    all_gather x1, blocking collectives, layer_body(): mid_stream = lax.all_gather(mid_slice, 'kv', axis=1, tiled=True)  13.9 us
    gather x2, local copies, waits for them, and re-layouts, place_cache(): cached = pool[moved_pages].reshape(mig_count, slot_count, channels)  8.4 us
    all_to_all x1, starting transfers between devices, layer_body(): lax.all_to_all(jnp.stack([place_cache(k_pool, new_keys), place_cache(v_po...  7.19 us
    select_n x1, other arithmetic, place_cache(): jnp.where(slot_pos < moved_len, cached, jnp.where(slot_pos == moved_len,...  5.69 us
    dot_general x1, matrix products, attend_pool(): jnp.einsum('rkgt,tkd->rkgd', weights, values, preferred_element_type=jnp....  5.31 us
  transfers between devices with their start and end apart: 4, of which 2 were waited for; matrix products, arithmetic and copies ran while one was open for 36% of the time, Pallas kernels for 0%

profile of v4, /device:TPU:1, one launch (start us, length us, event | category | flops | bytes accessed | tf_op | source)
XLA Modules:
  0.0 174.1 jit_solution(5157770401696378622)
XLA Ops:
  7.2 0.0 all-gather.3.cloned.1.call-start
  7.3 2.1 %pad_maximum_fusion.1 = bf16[144,2048]{1,0:T(8,128)(2,1)} fusion(bf16[48,2048]{1,0:T(8,128)(2,1)} %bitcast.161, bf16[48,2048]{1,0:T(8,128)(2,1)} %bitcast.162, bf16[48,2048]{1,0:T(8,128)(2,1)} %bitcast.163), kind=kLoop, calls=%fused_computation.53 | loop fusion | flops 1769472 | bytes 1179648 | tf_op jit(solution)/shard_map/concatenate | solution.py:114
  9.4 0.0 all-gather.3.cloned.1.call-update
  9.4 15.6 %all_gather.12 = bf16[64,2048]{1,0:T(8,128)(2,1)S(1)} all-gather(bf16[64,256]{1,0:T(8,128)(2,1)} %param.19), channel_id=1, replica_groups=mesh['req'=16,'kv'=8] {'kv'}, dimensions={1}, use_global_device_ids=true | all-gather | bytes 294912 | tf_op jit(solution)/shard_map/all_gather | solution.py:119
  25.0 0.2 fusion.35
  25.2 1.5 multiply_reduce_fusion.1
  26.8 0.3 fusion.81
  27.2 0.1 multiply_reduce_fusion
  27.3 0.1 multiply_bitcast_fusion
  27.4 0.2 fusion.67
  27.6 0.1 fusion.95
  27.7 0.1 copy.43
  27.8 0.2 multiply_cosine_fusion.1
  28.0 0.1 fusion.53
  28.1 0.1 subtract_convert_fusion
  28.2 0.1 pad_maximum_fusion.2
  28.2 0.2 fusion.63
  28.5 0.1 copy.52
  28.5 0.1 copy.45
  28.6 0.1 iota_compare_fusion.3
  28.7 0.7 fusion.14
  29.5 1.0 select_reduce_fusion
  30.5 1.6 add.137
  32.2 2.1 %and.30 = pred[64,174,128]{2,1,0:T(8,128)(4,1)S(1)} broadcast(pred[64,174]{1,0:T(8,128)(4,1)S(1)} %fusion.14), dimensions={0,1} | broadcast | bytes 1436544 | tf_op jit(solution)/shard_map/and | solution.py:48
  34.3 3.9 %fusion.6 = pred[64,22272]{1,0:T(8,128)(4,1)S(1)} fusion(s32[8,8,174,128]{3,2,1,0:T(8,128)S(1)} %bitcast.150, pred[8,8,174,128]{3,2,1,0:T(8,128)(4,1)S(1)} %bitcast.156, s32[64]{0:T(128)S(1)} %copy-done.1, s32[22272]{0:T(1024)S(1)} %iota_bitcast_fusion), kind=kLoop, calls=%fused_computation.21 | loop fusion | flops 4276224 | bytes 8641792 | tf_op jit(solution)/shard_map/and | solution.py:48
  38.2 2.3 %fusion.85 = (f32[64,2]{0,1:T(2,128)S(1)}, f32[64,1,2,22272]{3,0,2,1:T(8,128)S(1)}) fusion(bf16[64,2,128]{2,0,1:T(8,128)(2,1)S(1)} %pad_maximum_fusion.2, bf16[22272,128,1]{1,0,2:T(8,128)(2,1)S(1)} %bitcast.153, pred[64,22272]{1,0:T(8,128)(4,1)S(1)} %fusion.6), kind=kOutput, calls=%fused_computation.145 | convolution fusion | flops 738361216 | bytes 18563584 | tf_op jit(solution)/shard_map/rkgd,tkd->rkgt/dot_general | solution.py:54
  40.5 2.3 %fusion.2 = f32[64,2]{0,1:T(2,128)S(1)} fusion(f32[64,1,2,22272]{3,0,2,1:T(8,128)S(1)} %get-tuple-element.28, f32[64,2]{0,1:T(2,128)S(1)} %fusion.68), kind=kLoop, calls=%fused_computation.16 | loop fusion | flops 5701504 | bytes 11404288 | tf_op jit(solution)/shard_map/reduce_sum | solution.py:65
  42.9 0.3 fusion.86
  43.2 5.3 %fusion.30 = f32[64,1,2,128]{3,0,2,1:T(8,128)S(1)} fusion(bf16[22272,128,1]{1,0,2:T(8,128)(2,1)} %bitcast.158, f32[64,2]{0,1:T(2,128)S(1)} %get-tuple-element.14, f32[64,1,2,22272]{3,0,2,1:T(8,128)S(1)} %get-tuple-element.28, f32[64,2]{0,1:T(2,128)S(1)} %fusion.68, f32[64,128]{1,0:T(8,128)S(1)} %get-tuple-element.29, f32[64,2]{0,1:T(2,128)S(1)} %get-tuple-element.13), kind=kOutput, calls=%fused_computation.45 | convolution fusion | flops 738394112 | bytes 17204736 | tf_op jit(solution)/shard_map/rkgt,tkd->rkgd/dot_general | solution.py:71
  48.5 0.1 copy.46
  48.6 0.9 fusion.34
  49.4 0.9 copy.75
  50.3 4.2 %all-to-all-start = ((f32[8,64,256]{2,1,0:T(8,128)}), f32[8,64,256]{2,1,0:T(8,128)}, u32[]{:S(2)}, u32[]{:S(2)}) async-start(f32[8,64,256]{2,1,0:T(8,128)} %bitcast.148), calls=%async_computation | async-start | bytes 1048576 | tf_op jit(solution)/shard_map/all_to_all | solution.py:79
  54.5 0.8 scatter_custom_fusion
  55.4 0.7 gather_fusion
  56.1 0.1 iota_add_fusion.2
  56.2 0.7 gather_fusion.8
  56.8 0.7 gather_fusion.9
  57.5 0.7 gather_fusion.6
  58.2 0.7 gather_fusion.7
  58.9 0.1 copy.49
  58.9 0.1 reshape.469
  59.0 3.6 %gather_fusion.2 = bf16[64,128,128]{2,1,0:T(8,128)(2,1)S(1)} fusion(bf16[174,128,128]{2,1,0:T(8,128)(2,1)} %param.28, s32[1024]{0:T(1024)S(1)} %pad_clamp_fusion), kind=kCustom, calls=%fused_computation.2 | custom fusion | bytes 4194560 | tf_op jit(solution)/shard_map/gather | solution.py:147
  62.6 4.8 %gather_fusion.4 = bf16[64,128,128]{2,1,0:T(8,128)(2,1)} fusion(bf16[174,128,128]{2,1,0:T(8,128)(2,1)} %param.29, s32[1024]{0:T(1024)S(1)} %pad_clamp_fusion), kind=kCustom, calls=%fused_computation.4 | custom fusion | bytes 4194560 | tf_op jit(solution)/shard_map/gather | solution.py:147
  67.5 0.7 gather_fusion.1
  68.1 0.1 pad_maximum_fusion.3
  68.2 0.6 gather_fusion.3
  68.8 0.6 gather_fusion.5
  69.4 0.1 iota_compare_fusion.2
  69.4 5.7 %select_select_fusion.1 = (bf16[16,1,512,128]{3,2,1,0:T(8,128)(2,1)S(1)}, bf16[16,1,512,128]{3,2,1,0:T(8,128)(2,1)S(1)}) fusion(bf16[16,1,512,128]{3,2,1,0:T(8,128)(2,1)S(1)} %bitcast.154, pred[16,512]{1,0:T(8,128)(4,1)S(1)} %get-tuple-element.20, pred[16,512]{1,0:T(8,128)(4,1)S(1)} %get-tuple-element.19, bf16[16,128]{1,0:T(8,128)(2,1)S(1)} %gather_fusion.3, ...), kind=kLoop, calls=%fused_computation.32 | loop fusion | flops 4194304 | bytes 8413184 | tf_op jit(solution)/shard_map/jit(_where)/select_n | solution.py:149
  75.1 2.5 %pad_maximum_fusion = bf16[16,2,512,128]{3,2,1,0:T(8,128)(2,1)} fusion(bf16[16,1,512,128]{3,2,1,0:T(8,128)(2,1)S(1)} %get-tuple-element.12, bf16[16,1,512,128]{3,2,1,0:T(8,128)(2,1)S(1)} %get-tuple-element.11), kind=kLoop, calls=%fused_computation.22 | loop fusion | flops 2097152 | bytes 8388608 | tf_op jit(solution)/shard_map/stack | solution.py:154
  77.6 7.2 %all-to-all-start.2 = ((bf16[16,2,512,128]{3,2,1,0:T(8,128)(2,1)}), bf16[16,2,512,128]{3,2,1,0:T(8,128)(2,1)}, u32[]{:S(2)}, u32[]{:S(2)}) async-start(bf16[16,2,512,128]{3,2,1,0:T(8,128)(2,1)} %pad_maximum_fusion), calls=%async_computation.2 | async-start | bytes 8388608 | tf_op jit(solution)/shard_map/all_to_all | solution.py:153
  84.8 1.1 reduce_sum.77
  85.9 13.9 %all_gather.13 = bf16[64,2048]{1,0:T(8,128)(2,1)S(1)} all-gather(bf16[64,256]{1,0:T(8,128)(2,1)S(1)} %add_convert_fusion.1), channel_id=1, replica_groups=mesh['req'=16,'kv'=8] {'kv'}, dimensions={1}, use_global_device_ids=true | all-gather | bytes 294912 | tf_op jit(solution)/shard_map/all_gather | solution.py:172
  99.8 0.2 fusion.38
  100.0 0.0 all-gather.3.cloned.1.call-done
  100.0 2.9 %fusion.11 = f32[64,16,48]{0,2,1:T(8,128)S(1)} fusion(bf16[16,144,2048]{2,1,0:T(8,128)(2,1)} %bitcast.168, bf16[64,2048]{1,0:T(8,128)(2,1)S(1)} %all_gather.13, f32[2048]{0:T(1024)S(1)} %copy-done.12, f32[64]{0:T(128)S(1)} %add_rsqrt_fusion.1), kind=kOutput, calls=%fused_computation.27 | convolution fusion | flops 201850880 | bytes 3612928 | tf_op jit(solution)/shard_map/rd,sud->rsu/dot_general | solution.py:174
  102.9 5.2 %fusion.7 = f32[64,2048,1]{1,0,2:T(8,128)S(1)} fusion(bf16[16,144,2048]{2,1,0:T(8,128)(2,1)} %bitcast.169, f32[64,16,48]{0,2,1:T(8,128)S(1)} %fusion.11, bf16[64,2048]{1,0:T(8,128)(2,1)S(1)} %all_gather.13, f32[2048]{0:T(1024)S(1)} %copy-done.12, f32[64]{0:T(128)S(1)} %add_rsqrt_fusion.1), kind=kOutput, calls=%fused_computation.23 | convolution fusion | flops 403472384 | bytes 7282944 | tf_op jit(solution)/shard_map/rsu,suc->rc/dot_general | solution.py:177
  108.1 0.8 copy.74
  109.0 31.3 %all-to-all-done.2 = bf16[16,2,512,128]{3,2,1,0:T(8,128)(2,1)} async-done(((bf16[16,2,512,128]{3,2,1,0:T(8,128)(2,1)}), bf16[16,2,512,128]{3,2,1,0:T(8,128)(2,1)}, u32[]{:S(2)}, u32[]{:S(2)}) %all-to-all-start.2) | async-done | bytes 4194336 | tf_op jit(solution)/shard_map/all_to_all | solution.py:153
  140.2 17.0 %all-to-all-start.1 = ((f32[8,64,256]{2,1,0:T(8,128)}), f32[8,64,256]{2,1,0:T(8,128)S(1)}, u32[]{:S(2)}, u32[]{:S(2)}) async-start(f32[8,64,256]{2,1,0:T(8,128)} %bitcast.146), calls=%async_computation.1 | async-start | bytes 1048576 | tf_op jit(solution)/shard_map/all_to_all | solution.py:79
  157.2 4.7 %slice_bitcast_fusion = (bf16[16,512,128]{2,1,0:T(8,128)(2,1)}, bf16[16,512,128]{2,1,0:T(8,128)(2,1)}) fusion(bf16[16,2,512,128]{3,2,1,0:T(8,128)(2,1)} %all-to-all-done.2), kind=kLoop, calls=%fused_computation.29 | loop fusion | bytes 8388608 | tf_op jit(solution)/shard_map/squeeze | solution.py:161
  161.9 4.7 %all-to-all-done.1 = f32[8,64,256]{2,1,0:T(8,128)S(1)} async-done(((f32[8,64,256]{2,1,0:T(8,128)}), f32[8,64,256]{2,1,0:T(8,128)S(1)}, u32[]{:S(2)}, u32[]{:S(2)}) %all-to-all-start.1) | async-done | bytes 524320 | tf_op jit(solution)/shard_map/all_to_all | solution.py:79
  166.6 0.6 add_convert_fusion
  (58 shorter events, 0.4 us)
Async XLA Ops:
  7.2 41.4 %copy-start = (bf16[256,2048]{1,0:T(8,128)(2,1)S(1)}, bf16[256,2048]{1,0:T(8,128)(2,1)}, u32[]{:S(2)}) copy-start(bf16[256,2048]{1,0:T(8,128)(2,1)} %param.27) | copy-start | bytes 3145732
  7.2 19.6 %copy-start.8 = (f32[2048]{0:T(1024)S(1)}, f32[2048]{0:T(1024)}, u32[]{:S(2)}) copy-start(f32[2048]{0:T(1024)} %param.20) | copy-start | bytes 24580
  7.2 19.5 %copy-start.1 = (s32[64]{0:T(128)S(1)}, s32[64]{0:T(128)}, u32[]{:S(2)}) copy-start(s32[64]{0:T(128)} %param.30) | copy-start | bytes 772
  7.2 19.5 %copy-start.5 = (bf16[2048,256]{1,0:T(8,128)(2,1)S(1)}, bf16[2048,256]{1,0:T(8,128)(2,1)}, u32[]{:S(2)}) copy-start(bf16[2048,256]{1,0:T(8,128)(2,1)} %param.23) | copy-start | bytes 3145732
  7.2 20.1 %copy-start.9 = (f32[128]{0:T(128)S(1)}, f32[128]{0:T(128)}, u32[]{:S(2)}) copy-start(f32[128]{0:T(128)} %param.22) | copy-start | bytes 1540
  7.2 20.7 %copy-start.10 = (f32[128]{0:T(128)S(1)}, f32[128]{0:T(128)}, u32[]{:S(2)}) copy-start(f32[128]{0:T(128)} %param.21) | copy-start | bytes 1540
  7.2 21.3 %copy-start.3 = (s32[64,32]{0,1:T(8,128)S(1)}, s32[64,32]{0,1:T(8,128)}, u32[]{:S(2)}) copy-start(s32[64,32]{0,1:T(8,128)} %param.31) | copy-start | bytes 24580
  7.2 92.7 %all-gather.3.cloned.1.call-start = ((), (), s32[]{:S(2)}) async-start(), calls=%async_computation.3 | async-start | bytes 10027008 | tf_op jit(solution)/shard_map/all_gather | solution.py:113
  30.5 7.6 %slice-start = ((s8[5701632]{0:T(1024)(128)(4,1)}), s8[4194304]{0:T(1024)(128)(4,1)S(1)}, s32[]{:S(2)}) async-start(s8[5701632]{0:T(1024)(128)(4,1)} %bitcast.151), calls=%async_computation.4 | async-start | bytes 8388608
  34.3 3.9 %slice-start.1 = ((s8[5701632]{0:T(1024)(128)(4,1)}), s8[1507328]{0:T(1024)(128)(4,1)S(1)}, s32[]{:S(2)}) async-start(s8[5701632]{0:T(1024)(128)(4,1)} %bitcast.151), calls=%async_computation.5 | async-start | bytes 3014656
  40.5 2.3 %copy-start.6 = (bf16[2048,128]{1,0:T(8,128)(2,1)S(1)}, bf16[2048,128]{1,0:T(8,128)(2,1)}, u32[]{:S(2)}) copy-start(bf16[2048,128]{1,0:T(8,128)(2,1)} %param.26) | copy-start | bytes 1572868
  43.1 5.4 %copy-start.4 = (bf16[2048,256]{1,0:T(8,128)(2,1)S(1)}, bf16[2048,256]{1,0:T(8,128)(2,1)}, u32[]{:S(2)}) copy-start(bf16[2048,256]{1,0:T(8,128)(2,1)} %param.24) | copy-start | bytes 3145732
  48.5 6.1 %copy-start.13 = (s32[1,16]{1,0:T(1,128)S(1)}, s32[1,16]{1,0:T(1,128)}, u32[]{:S(2)}) copy-start(s32[1,16]{1,0:T(1,128)} %param.33) | copy-start | bytes 196
  48.5 6.9 %copy-start.2 = (s32[1,16]{1,0:T(1,128)S(1)}, s32[1,16]{1,0:T(1,128)}, u32[]{:S(2)}) copy-start(s32[1,16]{1,0:T(1,128)} %param.32) | copy-start | bytes 196
  48.5 7.6 %copy-start.11 = (s32[2]{0:T(128)S(1)}, s32[2]{0:T(128)}, u32[]{:S(2)}) copy-start(s32[2]{0:T(128)} %constant.73) | copy-start | bytes 28
  50.3 27.3 %all-to-all-start = ((f32[8,64,256]{2,1,0:T(8,128)}), f32[8,64,256]{2,1,0:T(8,128)}, u32[]{:S(2)}, u32[]{:S(2)}) async-start(f32[8,64,256]{2,1,0:T(8,128)} %bitcast.148), calls=%async_computation | async-start | bytes 1048576 | tf_op jit(solution)/shard_map/all_to_all | solution.py:79
  77.6 8.3 %copy-start.7 = (bf16[64,256]{1,0:T(8,128)(2,1)S(1)}, bf16[64,256]{1,0:T(8,128)(2,1)}, u32[]{:S(2)}) copy-start(bf16[64,256]{1,0:T(8,128)(2,1)} %param.19) | copy-start | bytes 98308
  77.6 22.4 %copy-start.12 = (f32[2048]{0:T(1024)S(1)}, f32[2048]{0:T(1024)}, u32[]{:S(2)}) copy-start(f32[2048]{0:T(1024)} %param.34) | copy-start | bytes 24580
  77.6 62.6 %all-to-all-start.2 = ((bf16[16,2,512,128]{3,2,1,0:T(8,128)(2,1)}), bf16[16,2,512,128]{3,2,1,0:T(8,128)(2,1)}, u32[]{:S(2)}, u32[]{:S(2)}) async-start(bf16[16,2,512,128]{3,2,1,0:T(8,128)(2,1)} %pad_maximum_fusion), calls=%async_computation.2 | async-start | bytes 8388608 | tf_op jit(solution)/shard_map/all_to_all | solution.py:153
  140.2 26.4 %all-to-all-start.1 = ((f32[8,64,256]{2,1,0:T(8,128)}), f32[8,64,256]{2,1,0:T(8,128)S(1)}, u32[]{:S(2)}, u32[]{:S(2)}) async-start(f32[8,64,256]{2,1,0:T(8,128)} %bitcast.146), calls=%async_computation.1 | async-start | bytes 1048576 | tf_op jit(solution)/shard_map/all_to_all | solution.py:79
Sparse Core Ops, SparseCore 0:
  10.8 78.4 all-gather.2

commit v5 on v4

--- a/solution.py
+++ b/solution.py
@@ -150,13 +150,22 @@
             slot_pos < moved_len, cached, jnp.where(slot_pos == moved_len, fresh_row, zero_value)
         )
 
-    moving = lax.all_to_all(
-        jnp.stack([place_cache(k_pool, new_keys), place_cache(v_pool, new_values)], axis=1),
-        "req",
-        0,
-        0,
-        tiled=True,
-    )
+    payload = jnp.stack(
+        [place_cache(k_pool, new_keys), place_cache(v_pool, new_values)], axis=1
+    )
+    req_groups = lax.axis_size("req")
+    me = lax.axis_index("req")
+    arrived = [payload[me]]
+    for shift in range(1, req_groups):
+        arrived.append(
+            lax.ppermute(
+                payload[(me + shift) % req_groups],
+                "req",
+                [(s, (s + shift) % req_groups) for s in range(req_groups)],
+            )
+        )
+    by_shift = jnp.stack(arrived, axis=0)
+    moving = by_shift[(me - jnp.arange(req_groups, dtype=jnp.int32)) % req_groups]
     mig_keys = moving[:, 0]
     mig_values = moving[:, 1]
     context = attend_pool(queries, new_keys, new_values, k_pool, v_pool, lengths, page_table)

time: 177 us -> 222 us (1.25)
  the two profiles are of different devices: /device:TPU:1 before, /device:TPU:25 now
where the time goes in v5:
time: 222 us; the launch traced here: 221 us
  local copies, waits for them, and re-layouts  51.8 us (23%)
  waiting for transfers between devices  39.6 us (18%)
  other arithmetic  32.7 us (15%)
  blocking collectives  29.1 us (13%)
  starting transfers between devices  28.5 us (13%)
  matrix products  24.5 us (11%)
  between operations  14.7 us (7%)
    ppermute x15, waiting for transfers between devices, layer_body(): lax.ppermute(payload[(me + shift) % req_groups], 'req', [(s, (s + shift)...  39.5 us
    ppermute x15, starting transfers between devices, layer_body(): lax.ppermute(payload[(me + shift) % req_groups], 'req', [(s, (s + shift)...  19.3 us
    unnamed x51, local copies, waits for them, and re-layouts  16.4 us
    all_gather x1, blocking collectives, layer_body(): whole_rows = lax.all_gather(hidden, 'kv', axis=1, tiled=True)  14.8 us
    all_gather x1, blocking collectives, layer_body(): mid_stream = lax.all_gather(mid_slice, 'kv', axis=1, tiled=True)  14.3 us
    gather x2, local copies, waits for them, and re-layouts, place_cache(): cached = pool[moved_pages].reshape(mig_count, slot_count, channels)  9.56 us
    all_to_all x2, starting transfers between devices, reduce_to_slice(): arrived = lax.all_to_all(pieces, 'kv', 0, 0, tiled=True)  9.22 us
    select_n x1, other arithmetic, place_cache(): jnp.where(slot_pos < moved_len, cached, jnp.where(slot_pos == moved_len,...  6.15 us
  transfers between devices with their start and end apart: 18, of which 6 were waited for; matrix products, arithmetic and copies ran while one was open for 47% of the time, Pallas kernels for 0%

profile of v5, /device:TPU:25, one launch (start us, length us, event | category | flops | bytes accessed | tf_op | source)
XLA Modules:
  0.0 220.9 jit_solution(4136299773862454131)
XLA Ops:
  7.2 2.1 pad_maximum_fusion
  9.4 14.8 %all_gather.12 = bf16[64,2048]{1,0:T(8,128)(2,1)S(1)} all-gather(bf16[64,256]{1,0:T(8,128)(2,1)} %param.19), channel_id=1, replica_groups=mesh['req'=16,'kv'=8] {'kv'}, dimensions={1}, use_global_device_ids=true | all-gather | bytes 294912 | tf_op jit(solution)/shard_map/all_gather | solution.py:119
  24.3 1.4 multiply_reduce_fusion.1
  25.7 1.3 fusion.104
  28.4 1.3 gather_fusion
  29.7 0.7 iota_add_fusion.2
  30.5 0.7 multiply_bitcast_fusion
  35.8 4.8 %gather_fusion.2 = bf16[64,128,128]{2,1,0:T(8,128)(2,1)} fusion(bf16[174,128,128]{2,1,0:T(8,128)(2,1)} %param.28, s32[1024]{0:T(1024)S(1)} %pad_clamp_fusion.1), kind=kCustom, calls=%fused_computation.2 | custom fusion | bytes 4194560 | tf_op jit(solution)/shard_map/gather | solution.py:147
  40.6 4.7 %gather_fusion.4 = bf16[64,128,128]{2,1,0:T(8,128)(2,1)} fusion(bf16[174,128,128]{2,1,0:T(8,128)(2,1)} %param.29, s32[1024]{0:T(1024)S(1)} %pad_clamp_fusion.1), kind=kCustom, calls=%fused_computation.4 | custom fusion | bytes 4194560 | tf_op jit(solution)/shard_map/gather | solution.py:147
  45.4 0.9 fusion.120
  46.9 6.2 %select_select_fusion = (bf16[16,1,512,128]{3,2,1,0:T(8,128)(2,1)S(1)}, bf16[16,1,512,128]{3,2,1,0:T(8,128)(2,1)S(1)}) fusion(bf16[16,1,512,128]{3,2,1,0:T(8,128)(2,1)} %bitcast.215, pred[16,512]{1,0:T(8,128)(4,1)S(1)} %get-tuple-element.36, pred[16,512]{1,0:T(8,128)(4,1)S(1)} %get-tuple-element.35, bf16[16,128]{1,0:T(8,128)(2,1)S(1)} %gather_fusion.5, ...), kind=kLoop, calls=%fused_computation.63 | loop fusion | flops 4194304 | bytes 8413184 | tf_op jit(solution)/shard_map/jit(_where)/select_n | solution.py:149
  53.1 1.3 copy-done.3
  54.4 1.2 fusion.78
  55.6 0.9 collective-permute-start
  56.5 2.3 %collective-permute-start.1 = (bf16[2,512,128]{2,1,0:T(8,128)(2,1)}, bf16[2,512,128]{2,1,0:T(8,128)(2,1)}, u32[]{:S(2)}, u32[]{:S(2)}) collective-permute-start(bf16[2,512,128]{2,1,0:T(8,128)(2,1)} %get-tuple-element.10), channel_id=1, source_target_pairs={{0,16},{8,24},{16,32},{24,40},{32,48},{40,56},{48,64},{56,72},{64,... | collective-permute-start | bytes 786440 | tf_op jit(solution)/shard_map/ppermute | solution.py:161
  59.3 0.9 collective-permute-start.3
  60.2 2.4 %fusion.64 = (bf16[2,512,128]{2,1,0:T(8,128)(2,1)}, bf16[2,512,128]{2,1,0:T(8,128)(2,1)}, bf16[2,512,128]{2,1,0:T(8,128)(2,1)}, bf16[2,512,128]{2,1,0:T(8,128)(2...) fusion(s32[]{:T(128)S(6)} %select_n.265, bf16[16,1,512,128]{3,2,1,0:T(8,128)(2,1)S(1)} %get-tuple-element.27, ...), kind=kLoop, calls=%fused_computation.132 | loop fusion | flops 786432 | bytes 5767192 | tf_op jit(solution)/shard_map/squeeze | solution.py:162
  62.6 3.6 %collective-permute-start.4 = (bf16[2,512,128]{2,1,0:T(8,128)(2,1)}, bf16[2,512,128]{2,1,0:T(8,128)(2,1)}, u32[]{:S(2)}, u32[]{:S(2)}) collective-permute-start(bf16[2,512,128]{2,1,0:T(8,128)(2,1)} %get-tuple-element.14), channel_id=1, source_target_pairs={{0,40},{8,48},{16,56},{24,64},{32,72},{40,80},{48,88},{56,96},{64,... | collective-permute-start | bytes 786440 | tf_op jit(solution)/shard_map/ppermute | solution.py:161
  66.3 1.6 fusion.115
  68.5 1.6 multiply_reduce_fusion
  70.1 1.4 copy.43
  71.5 0.8 fusion.129
  73.0 0.9 multiply_cosine_fusion.1
  73.9 0.7 fusion.85
  75.1 0.8 iota_compare_fusion.3
  75.9 0.7 fusion.14
  76.6 1.0 select_reduce_fusion
  77.7 1.6 add.299
  79.4 2.1 and.110
  81.5 3.9 %fusion.6 = pred[64,22272]{1,0:T(8,128)(4,1)S(1)} fusion(s32[8,8,174,128]{3,2,1,0:T(8,128)S(1)} %bitcast.212, pred[8,8,174,128]{3,2,1,0:T(8,128)(4,1)S(1)} %bitcast.216, s32[64]{0:T(128)S(1)} %copy-done.1, s32[22272]{0:T(1024)S(1)} %iota_bitcast_fusion), kind=kLoop, calls=%fused_computation.54 | loop fusion | flops 4276224 | bytes 8641792 | tf_op jit(solution)/shard_map/and | solution.py:48
  85.4 4.2 %fusion.119 = (f32[64,2]{0,1:T(2,128)S(1)}, f32[64,1,2,22272]{3,0,2,1:T(8,128)S(1)}) fusion(bf16[64,2,128]{2,0,1:T(8,128)(2,1)S(1)} %copy-done.11, bf16[22272,128,1]{1,0,2:T(8,128)(2,1)} %bitcast.213, pred[64,22272]{1,0:T(8,128)(4,1)S(1)} %fusion.6), kind=kOutput, calls=%fused_computation.231 | convolution fusion | flops 738361216 | bytes 18563584 | tf_op jit(solution)/shard_map/rkgd,tkd->rkgt/dot_general | solution.py:54
  89.6 2.3 %fusion.2 = f32[64,2]{0,1:T(2,128)S(1)} fusion(f32[64,1,2,22272]{3,0,2,1:T(8,128)S(1)} %get-tuple-element.44, f32[64,2]{0,1:T(2,128)S(1)} %fusion.100), kind=kLoop, calls=%fused_computation.49 | loop fusion | flops 5701504 | bytes 11404288 | tf_op jit(solution)/shard_map/reduce_sum | solution.py:65
  91.9 5.2 %fusion.30 = f32[64,1,2,128]{3,0,2,1:T(8,128)S(1)} fusion(bf16[22272,128,1]{1,0,2:T(8,128)(2,1)} %bitcast.219, f32[64,2]{0,1:T(2,128)S(1)} %get-tuple-element.30, f32[64,1,2,22272]{3,0,2,1:T(8,128)S(1)} %get-tuple-element.44, f32[64,2]{0,1:T(2,128)S(1)} %fusion.100, f32[64,128]{1,0:T(8,128)S(1)} %copy-done.14, f32[64,2]{0,1:T(2,128)S(1)} %get-tuple-element.29), kind=kOutput, calls=%fused_computation.77 | convolution fusion | flops 738394112 | bytes 17204736 | tf_op jit(solution)/shard_map/rkgt,tkd->rkgd/dot_general | solution.py:71
  97.2 2.9 %fusion.34 = f32[64,2048]{1,0:T(8,128)} fusion(bf16[256,2048]{1,0:T(8,128)(2,1)S(1)} %copy-done, bf16[2048,256]{1,0:T(8,128)(2,1)} %param.24, f32[8,8,2,128]{3,2,1,0:T(2,128)S(1)} %bitcast.221, bf16[64,2048]{1,0:T(8,128)(2,1)S(1)} %all_gather.12, f32[2048]{0:T(1024)S(1)} %copy-done.13, f32[64]{0:T(128)S(1)} %add_rsqrt_fusion.3), kind=kOutput, calls=%fused_computation.79 | convolution fusion | flops 134823936 | bytes 2957568 | tf_op jit(solution)/shard_map/dot_general | solution.py:175
  100.1 1.9 copy.75
  102.0 5.7 %all-to-all-start = ((f32[8,64,256]{2,1,0:T(8,128)}), f32[8,64,256]{2,1,0:T(8,128)}, u32[]{:S(2)}, u32[]{:S(2)}) async-start(f32[8,64,256]{2,1,0:T(8,128)} %bitcast.218), calls=%async_computation | async-start | bytes 1048576 | tf_op jit(solution)/shard_map/all_to_all | solution.py:79
  107.8 1.3 fusion.65
  109.1 1.5 collective-permute-start.5
  110.6 1.7 bitcast_dynamic-update-slice_fusion.14
  112.3 1.4 collective-permute-start.6
  113.7 1.7 bitcast_dynamic-update-slice_fusion.13
  115.4 1.8 collective-permute-start.7
  117.1 1.7 bitcast_dynamic-update-slice_fusion.12
  118.8 1.7 collective-permute-start.8
  120.5 1.7 bitcast_dynamic-update-slice_fusion.11
  122.2 3.7 %collective-permute-start.9 = (bf16[2,512,128]{2,1,0:T(8,128)(2,1)S(1)}, bf16[2,512,128]{2,1,0:T(8,128)(2,1)S(1)}, u32[]{:S(2)}, u32[]{:S(2)}) collective-permute-start(bf16[2,512,128]{2,1,0:T(8,128)(2,1)S(1)} %get-tuple-element.20), channel_id=1, source_target_pairs={{0,80},{8,88},{16,96},{24,104},{32,112},{40,120},{48,0},{56,8},{64... | collective-permute-start | bytes 786440 | tf_op jit(solution)/shard_map/ppermute | solution.py:161
  125.9 1.7 bitcast_dynamic-update-slice_fusion.10
  129.2 4.6 %collective-permute-done.7 = bf16[2,512,128]{2,1,0:T(8,128)(2,1)S(1)} collective-permute-done((bf16[2,512,128]{2,1,0:T(8,128)(2,1)}, bf16[2,512,128]{2,1,0:T(8,128)(2,1)S(1)}, u32[]{:S(2)}, u32[]{:S(2)}) %collective-permute-start.7) | collective-permute-done | bytes 262176 | tf_op jit(solution)/shard_map/ppermute | solution.py:161
  133.9 0.8 collective-permute-start.12
  135.4 5.3 %collective-permute-done.8 = bf16[2,512,128]{2,1,0:T(8,128)(2,1)S(1)} collective-permute-done((bf16[2,512,128]{2,1,0:T(8,128)(2,1)}, bf16[2,512,128]{2,1,0:T(8,128)(2,1)S(1)}, u32[]{:S(2)}, u32[]{:S(2)}) %collective-permute-start.8) | collective-permute-done | bytes 262176 | tf_op jit(solution)/shard_map/ppermute | solution.py:161
  141.4 8.7 %collective-permute-done.9 = bf16[2,512,128]{2,1,0:T(8,128)(2,1)S(1)} collective-permute-done((bf16[2,512,128]{2,1,0:T(8,128)(2,1)S(1)}, bf16[2,512,128]{2,1,0:T(8,128)(2,1)S(1)}, u32[]{:S(2)}, u32[]{:S(2)}) %collective-permute-start.9) | collective-permute-done | bytes 262176 | tf_op jit(solution)/shard_map/ppermute | solution.py:161
  150.9 2.2 %collective-permute-done.10 = bf16[2,512,128]{2,1,0:T(8,128)(2,1)S(1)} collective-permute-done((bf16[2,512,128]{2,1,0:T(8,128)(2,1)S(1)}, bf16[2,512,128]{2,1,0:T(8,128)(2,1)S(1)}, u32[]{:S(2)}, u32[]{:S(2)}) %collective-permute-start.10) | collective-permute-done | bytes 262176 | tf_op jit(solution)/shard_map/ppermute | solution.py:161
  153.1 0.7 bitcast_dynamic-update-slice_fusion.4
  153.8 0.7 bitcast_dynamic-update-slice_fusion.3
  154.6 8.9 %collective-permute-done.12 = bf16[2,512,128]{2,1,0:T(8,128)(2,1)S(1)} collective-permute-done((bf16[2,512,128]{2,1,0:T(8,128)(2,1)S(1)}, bf16[2,512,128]{2,1,0:T(8,128)(2,1)S(1)}, u32[]{:S(2)}, u32[]{:S(2)}) %collective-permute-start.12) | collective-permute-done | bytes 262176 | tf_op jit(solution)/shard_map/ppermute | solution.py:161
  164.2 9.7 %collective-permute-done.13 = bf16[2,512,128]{2,1,0:T(8,128)(2,1)S(1)} collective-permute-done((bf16[2,512,128]{2,1,0:T(8,128)(2,1)S(1)}, bf16[2,512,128]{2,1,0:T(8,128)(2,1)S(1)}, u32[]{:S(2)}, u32[]{:S(2)}) %collective-permute-start.13) | collective-permute-done | bytes 262176 | tf_op jit(solution)/shard_map/ppermute | solution.py:161
  174.6 1.1 reduce_sum.77
  175.7 14.3 %all_gather.13 = bf16[64,2048]{1,0:T(8,128)(2,1)S(1)} all-gather(bf16[64,256]{1,0:T(8,128)(2,1)S(1)} %add_convert_fusion.1), channel_id=1, replica_groups=mesh['req'=16,'kv'=8] {'kv'}, dimensions={1}, use_global_device_ids=true | all-gather | bytes 294912 | tf_op jit(solution)/shard_map/all_gather | solution.py:181
  190.3 2.9 %fusion.11 = f32[64,16,48]{0,2,1:T(8,128)S(1)} fusion(bf16[16,144,2048]{2,1,0:T(8,128)(2,1)} %bitcast.229, bf16[64,2048]{1,0:T(8,128)(2,1)S(1)} %all_gather.13, f32[2048]{0:T(1024)S(1)} %copy-done.17, f32[64]{0:T(128)S(1)} %add_rsqrt_fusion.1), kind=kOutput, calls=%fused_computation.59 | convolution fusion | flops 201850880 | bytes 3612928 | tf_op jit(solution)/shard_map/rd,sud->rsu/dot_general | solution.py:183
  193.2 5.2 %fusion.7 = f32[64,2048,1]{1,0,2:T(8,128)S(1)} fusion(bf16[16,144,2048]{2,1,0:T(8,128)(2,1)} %bitcast.230, f32[64,16,48]{0,2,1:T(8,128)S(1)} %fusion.11, bf16[64,2048]{1,0:T(8,128)(2,1)S(1)} %all_gather.13, f32[2048]{0:T(1024)S(1)} %copy-done.17, f32[64]{0:T(128)S(1)} %add_rsqrt_fusion.1), kind=kOutput, calls=%fused_computation.55 | convolution fusion | flops 403472384 | bytes 7282944 | tf_op jit(solution)/shard_map/rsu,suc->rc/dot_general | solution.py:186
  198.4 0.9 copy.74
  199.2 3.6 %all-to-all-start.1 = ((f32[8,64,256]{2,1,0:T(8,128)}), f32[8,64,256]{2,1,0:T(8,128)S(1)}, u32[]{:S(2)}, u32[]{:S(2)}) async-start(f32[8,64,256]{2,1,0:T(8,128)} %bitcast.208), calls=%async_computation.1 | async-start | bytes 1048576 | tf_op jit(solution)/shard_map/all_to_all | solution.py:79
  203.5 5.2 %gather_fusion.6 = bf16[16,2,512,128]{3,2,1,0:T(8,128)(2,1)} fusion(bf16[16,2,512,128]{3,2,1,0:T(8,128)(2,1)} %bitcast_dynamic-update-slice_fusion, s32[1024]{0:T(1024)S(1)} %pad_clamp_fusion), kind=kCustom, calls=%fused_computation.6 | custom fusion | bytes 8388672 | tf_op jit(solution)/shard_map/gather | solution.py:168
  208.7 4.7 %slice_bitcast_fusion = (bf16[16,512,128]{2,1,0:T(8,128)(2,1)}, bf16[16,512,128]{2,1,0:T(8,128)(2,1)}) fusion(bf16[16,2,512,128]{3,2,1,0:T(8,128)(2,1)} %gather_fusion.6), kind=kLoop, calls=%fused_computation.61 | loop fusion | bytes 8388608 | tf_op jit(solution)/shard_map/squeeze | solution.py:170
  (109 shorter events, 16.0 us)
Async XLA Ops:
  7.2 90.1 %copy-start = (bf16[256,2048]{1,0:T(8,128)(2,1)S(1)}, bf16[256,2048]{1,0:T(8,128)(2,1)}, u32[]{:S(2)}) copy-start(bf16[256,2048]{1,0:T(8,128)(2,1)} %param.27) | copy-start | bytes 3145732
  7.2 24.5 %copy-start.1 = (s32[64]{0:T(128)S(1)}, s32[64]{0:T(128)}, u32[]{:S(2)}) copy-start(s32[64]{0:T(128)} %param.30) | copy-start | bytes 772
  7.2 25.7 %copy-start.2 = (s32[64,32]{0,1:T(8,128)S(1)}, s32[64,32]{0,1:T(8,128)}, u32[]{:S(2)}) copy-start(s32[64,32]{0,1:T(8,128)} %param.31) | copy-start | bytes 24580
  7.2 183.0 %all-gather.3.cloned.1.call-start = ((), (), s32[]{:S(2)}) async-start(), calls=%async_computation.2 | async-start | bytes 10027008 | tf_op jit(solution)/shard_map/all_gather | solution.py:113
  9.3 22.1 %copy-start.15 = (f32[64]{0:T(128)}, f32[64]{0:T(128)S(1)}, u32[]{:S(2)}) copy-start(f32[64]{0:T(128)S(1)} %multiply_power_fusion) | copy-start | bytes 772
  27.1 4.4 %copy-start.16 = (f32[64]{0:T(128)}, f32[64]{0:T(128)S(1)}, u32[]{:S(2)}) copy-start(f32[64]{0:T(128)S(1)} %get-tuple-element.40) | copy-start | bytes 772
  31.4 13.9 %copy-start.9 = (bf16[64,64]{1,0:T(8,128)(2,1)}, bf16[64,64]{1,0:T(8,128)(2,1)S(1)}, u32[]{:S(2)}) copy-start(bf16[64,64]{1,0:T(8,128)(2,1)S(1)} %get-tuple-element.26) | copy-start | bytes 24580
  35.8 9.6 %copy-start.4 = (bf16[2048,128]{1,0:T(8,128)(2,1)S(1)}, bf16[2048,128]{1,0:T(8,128)(2,1)}, u32[]{:S(2)}) copy-start(bf16[2048,128]{1,0:T(8,128)(2,1)} %param.26) | copy-start | bytes 1572868
  35.8 9.6 %copy-start.13 = (f32[2048]{0:T(1024)S(1)}, f32[2048]{0:T(1024)}, u32[]{:S(2)}) copy-start(f32[2048]{0:T(1024)} %param.20) | copy-start | bytes 24580
  53.1 1.3 copy-start.3
  55.6 53.5 %collective-permute-start = (bf16[2,512,128]{2,1,0:T(8,128)(2,1)}, bf16[2,512,128]{2,1,0:T(8,128)(2,1)}, u32[]{:S(2)}, u32[]{:S(2)}) collective-permute-start(bf16[2,512,128]{2,1,0:T(8,128)(2,1)} %get-tuple-element.9), channel_id=1, source_target_pairs={{0,8},{8,16},{16,24},{24,32},{32,40},{40,48},{48,56},{56,64},{64,7... | collective-permute-start | bytes 786440 | tf_op jit(solution)/shard_map/ppermute | solution.py:161
  56.5 55.9 %collective-permute-start.1 = (bf16[2,512,128]{2,1,0:T(8,128)(2,1)}, bf16[2,512,128]{2,1,0:T(8,128)(2,1)}, u32[]{:S(2)}, u32[]{:S(2)}) collective-permute-start(bf16[2,512,128]{2,1,0:T(8,128)(2,1)} %get-tuple-element.10), channel_id=1, source_target_pairs={{0,16},{8,24},{16,32},{24,40},{32,48},{40,56},{48,64},{56,72},{64,... | collective-permute-start | bytes 786440 | tf_op jit(solution)/shard_map/ppermute | solution.py:161
  58.8 56.6 %collective-permute-start.2 = (bf16[2,512,128]{2,1,0:T(8,128)(2,1)}, bf16[2,512,128]{2,1,0:T(8,128)(2,1)}, u32[]{:S(2)}, u32[]{:S(2)}) collective-permute-start(bf16[2,512,128]{2,1,0:T(8,128)(2,1)} %get-tuple-element.11), channel_id=1, source_target_pairs={{0,24},{8,32},{16,40},{24,48},{32,56},{40,64},{48,72},{56,80},{64,... | collective-permute-start | bytes 786440 | tf_op jit(solution)/shard_map/ppermute | solution.py:161
  59.3 59.5 %collective-permute-start.3 = (bf16[2,512,128]{2,1,0:T(8,128)(2,1)}, bf16[2,512,128]{2,1,0:T(8,128)(2,1)}, u32[]{:S(2)}, u32[]{:S(2)}) collective-permute-start(bf16[2,512,128]{2,1,0:T(8,128)(2,1)} %get-tuple-element.12), channel_id=1, source_target_pairs={{0,32},{8,40},{16,48},{24,56},{32,64},{40,72},{48,80},{56,88},{64,... | collective-permute-start | bytes 786440 | tf_op jit(solution)/shard_map/ppermute | solution.py:161
  62.6 59.5 %collective-permute-start.4 = (bf16[2,512,128]{2,1,0:T(8,128)(2,1)}, bf16[2,512,128]{2,1,0:T(8,128)(2,1)}, u32[]{:S(2)}, u32[]{:S(2)}) collective-permute-start(bf16[2,512,128]{2,1,0:T(8,128)(2,1)} %get-tuple-element.14), channel_id=1, source_target_pairs={{0,40},{8,48},{16,56},{24,64},{32,72},{40,80},{48,88},{56,96},{64,... | collective-permute-start | bytes 786440 | tf_op jit(solution)/shard_map/ppermute | solution.py:161
  74.8 1.1 copy-start.10
  81.5 3.9 %copy-start.11 = (bf16[64,2,128]{2,0,1:T(8,128)(2,1)S(1)}, bf16[64,2,128]{2,0,1:T(8,128)(2,1)}, u32[]{:S(2)}) copy-start(bf16[64,2,128]{2,0,1:T(8,128)(2,1)} %copy-done.10) | copy-start | bytes 98308
  89.6 2.3 %copy-start.14 = (f32[64,128]{1,0:T(8,128)S(1)}, f32[64,128]{1,0:T(8,128)}, u32[]{:S(2)}) copy-start(f32[64,128]{1,0:T(8,128)} %get-tuple-element.45) | copy-start | bytes 98308
  102.0 72.6 %all-to-all-start = ((f32[8,64,256]{2,1,0:T(8,128)}), f32[8,64,256]{2,1,0:T(8,128)}, u32[]{:S(2)}, u32[]{:S(2)}) async-start(f32[8,64,256]{2,1,0:T(8,128)} %bitcast.218), calls=%async_computation | async-start | bytes 1048576 | tf_op jit(solution)/shard_map/all_to_all | solution.py:79
  107.7 1.4 copy-start.8
  107.7 4.6 %copy-start.7 = (bf16[2,512,128]{2,1,0:T(8,128)(2,1)S(1)}, bf16[2,512,128]{2,1,0:T(8,128)(2,1)}, u32[]{:S(2)}) copy-start(bf16[2,512,128]{2,1,0:T(8,128)(2,1)} %get-tuple-element.16) | copy-start | bytes 786436
  107.8 33.0 %copy-start.6 = (bf16[2,512,128]{2,1,0:T(8,128)(2,1)S(1)}, bf16[2,512,128]{2,1,0:T(8,128)(2,1)}, u32[]{:S(2)}) copy-start(bf16[2,512,128]{2,1,0:T(8,128)(2,1)} %get-tuple-element.13) | copy-start | bytes 786436
  107.8 42.4 %copy-start.5 = (bf16[2,512,128]{2,1,0:T(8,128)(2,1)S(1)}, bf16[2,512,128]{2,1,0:T(8,128)(2,1)}, u32[]{:S(2)}) copy-start(bf16[2,512,128]{2,1,0:T(8,128)(2,1)} %get-tuple-element.7) | copy-start | bytes 786436
  109.1 66.6 %copy-start.12 = (bf16[64,256]{1,0:T(8,128)(2,1)S(1)}, bf16[64,256]{1,0:T(8,128)(2,1)}, u32[]{:S(2)}) copy-start(bf16[64,256]{1,0:T(8,128)(2,1)} %param.19) | copy-start | bytes 98308
  109.1 18.4 %collective-permute-start.5 = (bf16[2,512,128]{2,1,0:T(8,128)(2,1)S(1)}, bf16[2,512,128]{2,1,0:T(8,128)(2,1)S(1)}, u32[]{:S(2)}, u32[]{:S(2)}) collective-permute-start(bf16[2,512,128]{2,1,0:T(8,128)(2,1)S(1)} %copy-done.8), channel_id=1, source_target_pairs={{0,48},{8,56},{16,64},{24,72},{32,80},{40,88},{48,96},{56,104},{64... | collective-permute-start | bytes 786440 | tf_op jit(solution)/shard_map/ppermute | solution.py:161
  110.6 79.6 %copy-start.17 = (f32[2048]{0:T(1024)S(1)}, f32[2048]{0:T(1024)}, u32[]{:S(2)}) copy-start(f32[2048]{0:T(1024)} %param.34) | copy-start | bytes 24580
  112.3 15.9 %collective-permute-start.6 = (bf16[2,512,128]{2,1,0:T(8,128)(2,1)S(1)}, bf16[2,512,128]{2,1,0:T(8,128)(2,1)S(1)}, u32[]{:S(2)}, u32[]{:S(2)}) collective-permute-start(bf16[2,512,128]{2,1,0:T(8,128)(2,1)S(1)} %copy-done.7), channel_id=1, source_target_pairs={{0,56},{8,64},{16,72},{24,80},{32,88},{40,96},{48,104},{56,112},{6... | collective-permute-start | bytes 786440 | tf_op jit(solution)/shard_map/ppermute | solution.py:161
  115.4 18.5 %collective-permute-start.7 = (bf16[2,512,128]{2,1,0:T(8,128)(2,1)}, bf16[2,512,128]{2,1,0:T(8,128)(2,1)S(1)}, u32[]{:S(2)}, u32[]{:S(2)}) collective-permute-start(bf16[2,512,128]{2,1,0:T(8,128)(2,1)} %get-tuple-element.17), channel_id=1, source_target_pairs={{0,64},{8,72},{16,80},{24,88},{32,96},{40,104},{48,112},{56,120},{... | collective-permute-start | bytes 786440 | tf_op jit(solution)/shard_map/ppermute | solution.py:161
  118.8 21.9 %collective-permute-start.8 = (bf16[2,512,128]{2,1,0:T(8,128)(2,1)}, bf16[2,512,128]{2,1,0:T(8,128)(2,1)S(1)}, u32[]{:S(2)}, u32[]{:S(2)}) collective-permute-start(bf16[2,512,128]{2,1,0:T(8,128)(2,1)} %get-tuple-element.18), channel_id=1, source_target_pairs={{0,72},{8,80},{16,88},{24,96},{32,104},{40,112},{48,120},{56,0},{6... | collective-permute-start | bytes 786440 | tf_op jit(solution)/shard_map/ppermute | solution.py:161
  122.2 28.0 %collective-permute-start.9 = (bf16[2,512,128]{2,1,0:T(8,128)(2,1)S(1)}, bf16[2,512,128]{2,1,0:T(8,128)(2,1)S(1)}, u32[]{:S(2)}, u32[]{:S(2)}) collective-permute-start(bf16[2,512,128]{2,1,0:T(8,128)(2,1)S(1)} %get-tuple-element.20), channel_id=1, source_target_pairs={{0,80},{8,88},{16,96},{24,104},{32,112},{40,120},{48,0},{56,8},{64... | collective-permute-start | bytes 786440 | tf_op jit(solution)/shard_map/ppermute | solution.py:161
  127.5 25.6 %collective-permute-start.10 = (bf16[2,512,128]{2,1,0:T(8,128)(2,1)S(1)}, bf16[2,512,128]{2,1,0:T(8,128)(2,1)S(1)}, u32[]{:S(2)}, u32[]{:S(2)}) collective-permute-start(bf16[2,512,128]{2,1,0:T(8,128)(2,1)S(1)} %get-tuple-element.21), channel_id=1, source_target_pairs={{0,88},{8,96},{16,104},{24,112},{32,120},{40,0},{48,8},{56,16},{64... | collective-permute-start | bytes 786440 | tf_op jit(solution)/shard_map/ppermute | solution.py:161
  128.3 25.6 %collective-permute-start.11 = (bf16[2,512,128]{2,1,0:T(8,128)(2,1)S(1)}, bf16[2,512,128]{2,1,0:T(8,128)(2,1)S(1)}, u32[]{:S(2)}, u32[]{:S(2)}) collective-permute-start(bf16[2,512,128]{2,1,0:T(8,128)(2,1)S(1)} %get-tuple-element.22), channel_id=1, source_target_pairs={{0,96},{8,104},{16,112},{24,120},{32,0},{40,8},{48,16},{56,24},{64... | collective-permute-start | bytes 786440 | tf_op jit(solution)/shard_map/ppermute | solution.py:161
  133.9 29.6 %collective-permute-start.12 = (bf16[2,512,128]{2,1,0:T(8,128)(2,1)S(1)}, bf16[2,512,128]{2,1,0:T(8,128)(2,1)S(1)}, u32[]{:S(2)}, u32[]{:S(2)}) collective-permute-start(bf16[2,512,128]{2,1,0:T(8,128)(2,1)S(1)} %get-tuple-element.19), channel_id=1, source_target_pairs={{0,104},{8,112},{16,120},{24,0},{32,8},{40,16},{48,24},{56,32},{64... | collective-permute-start | bytes 786440 | tf_op jit(solution)/shard_map/ppermute | solution.py:161
  140.7 33.2 %collective-permute-start.13 = (bf16[2,512,128]{2,1,0:T(8,128)(2,1)S(1)}, bf16[2,512,128]{2,1,0:T(8,128)(2,1)S(1)}, u32[]{:S(2)}, u32[]{:S(2)}) collective-permute-start(bf16[2,512,128]{2,1,0:T(8,128)(2,1)S(1)} %copy-done.6), channel_id=1, source_target_pairs={{0,112},{8,120},{16,0},{24,8},{32,16},{40,24},{48,32},{56,40},{64,... | collective-permute-start | bytes 786440 | tf_op jit(solution)/shard_map/ppermute | solution.py:161
  150.1 52.6 %collective-permute-start.14 = (bf16[2,512,128]{2,1,0:T(8,128)(2,1)S(1)}, bf16[2,512,128]{2,1,0:T(8,128)(2,1)S(1)}, u32[]{:S(2)}, u32[]{:S(2)}) collective-permute-start(bf16[2,512,128]{2,1,0:T(8,128)(2,1)S(1)} %copy-done.5), channel_id=1, source_target_pairs={{0,120},{8,0},{16,8},{24,16},{32,24},{40,32},{48,40},{56,48},{64,5... | collective-permute-start | bytes 786440 | tf_op jit(solution)/shard_map/ppermute | solution.py:161
  199.2 14.2 %all-to-all-start.1 = ((f32[8,64,256]{2,1,0:T(8,128)}), f32[8,64,256]{2,1,0:T(8,128)S(1)}, u32[]{:S(2)}, u32[]{:S(2)}) async-start(f32[8,64,256]{2,1,0:T(8,128)} %bitcast.208), calls=%async_computation.1 | async-start | bytes 1048576 | tf_op jit(solution)/shard_map/all_to_all | solution.py:79
Sparse Core Ops, SparseCore 0:
  10.2 103.9 all-gather.2

commit v6 on v4

--- a/solution.py
+++ b/solution.py
@@ -116,7 +116,14 @@
     gate_w = stacked[:, :unit_count, :]
     up_w = stacked[:, unit_count : 2 * unit_count, :]
     down_w = stacked[:, 2 * unit_count :, :]
-    whole_rows = lax.all_gather(hidden, "kv", axis=1, tiled=True)
+    kv_count = lax.axis_size("kv")
+    whole_rows = (
+        lax.all_to_all(
+            jnp.broadcast_to(hidden[None], (kv_count,) + hidden.shape), "kv", 0, 0, tiled=True
+        )
+        .transpose(1, 0, 2)
+        .reshape(req_count, kv_count * hidden.shape[1])
+    )
     normed = rms_norm(whole_rows, attn_gain).astype(jnp.bfloat16)
     query_raw = jnp.dot(normed, w_q, preferred_element_type=jnp.float32).reshape(
         req_count, q_local, head_dim
@@ -143,15 +150,17 @@
     moved_len = lengths[sent_rows][:, None, None]
     zero_value = jnp.zeros((), jnp.bfloat16)
 
-    def place_cache(pool, fresh_rows):
-        cached = pool[moved_pages].reshape(mig_count, slot_count, channels)
+    cached_pages = lax.optimization_barrier((k_pool[moved_pages], v_pool[moved_pages]))
+
+    def place_cache(pool_pages, fresh_rows):
+        cached = pool_pages.reshape(mig_count, slot_count, channels)
         fresh_row = fresh_rows.reshape(req_count, channels)[sent_rows][:, None, :]
         return jnp.where(
             slot_pos < moved_len, cached, jnp.where(slot_pos == moved_len, fresh_row, zero_value)
         )
 
     moving = lax.all_to_all(
-        jnp.stack([place_cache(k_pool, new_keys), place_cache(v_pool, new_values)], axis=1),
+        jnp.stack([place_cache(cached_pages[0], new_keys), place_cache(cached_pages[1], new_values)], axis=1),
         "req",
         0,
         0,
@@ -164,7 +173,6 @@
         jnp.bfloat16
     )
     head_terms = jnp.dot(gated, w_o, preferred_element_type=jnp.float32)
-    kv_count = lax.axis_size("kv")
     slice_width = model_width // kv_count
     mid_slice = (
         hidden.astype(jnp.float32) + reduce_to_slice(head_terms, kv_count, slice_width)

time: 177 us -> 181 us (1.023)
  blocking collectives: 29.5 us -> 13.9 us
  matrix products: 18.9 us -> 26.1 us
  local copies, waits for them, and re-layouts: 25 us -> 31.8 us
  waiting for transfers between devices: 35.9 us -> 39.9 us
  starting transfers between devices: 28.4 us -> 31.1 us
    all_gather x1 -> x0, blocking collectives: 15.6 us -> none  [layer_body(): whole_rows = lax.all_gather(hidden, 'kv', axis=1, tiled=True)]
    all_to_all x1 -> x2, starting transfers between devices: 7.19 us -> 13.9 us  [the longest x1 7.11 us: layer_body(): lax.all_to_all(jnp.stack([place_cache(cached_pages[0], new_keys), place_c...]
    all_to_all x2, starting transfers between devices: 21.2 us -> 17.2 us  [reduce_to_slice(): arrived = lax.all_to_all(pieces, 'kv', 0, 0, tiled=True)]
    dot_general x1, matrix products: 2.31 us -> 5.17 us  [attend_pool(): jnp.einsum('rkgd,tkd->rkgt', queries, keys, preferred_element_type=jnp.fl...]
    all_to_all x1 -> x2, waiting for transfers between devices: 31.3 us -> 33.8 us  [the longest x1 33.8 us: layer_body(): lax.all_to_all(jnp.stack([place_cache(cached_pages[0], new_keys), place_c...]
    dot_general x0 -> x1, local copies, waits for them, and re-layouts: none -> 2.26 us  [layer_body(): jnp.dot(normed, w_q, preferred_element_type=jnp.float32)]
    dot_general x1, matrix products: 0.85 us -> 2.96 us  [layer_body(): head_terms = jnp.dot(gated, w_o, preferred_element_type=jnp.float32)]
  transfers between devices with their start and end apart: 4 -> 5, of which waited for: 2 -> 3; matrix products, arithmetic and copies ran while one was open for 36% -> 43% of each run, Pallas kernels for 0% -> 0%
where the time goes in v6:
time: 181 us; the launch traced here: 180 us
  waiting for transfers between devices  39.9 us (22%)
  local copies, waits for them, and re-layouts  31.8 us (18%)
  starting transfers between devices  31.1 us (17%)
  matrix products  26.1 us (14%)
  other arithmetic  22.3 us (12%)
  between operations  14.5 us (8%)
  blocking collectives  13.9 us (8%)
    all_to_all x1, waiting for transfers between devices, layer_body(): lax.all_to_all(jnp.stack([place_cache(cached_pages[0], new_keys), place_c...  33.8 us
    all_to_all x2, starting transfers between devices, reduce_to_slice(): arrived = lax.all_to_all(pieces, 'kv', 0, 0, tiled=True)  17.2 us
    all_gather x1, blocking collectives, layer_body(): mid_stream = lax.all_gather(mid_slice, 'kv', axis=1, tiled=True)  13.9 us
    all_to_all x1, starting transfers between devices, layer_body(): lax.all_to_all(jnp.stack([place_cache(cached_pages[0], new_keys), place_c...  7.11 us
    all_to_all x1, starting transfers between devices, layer_body(): lax.all_to_all(jnp.broadcast_to(hidden[None], (kv_count,) + hidden.shape)...  6.8 us
    all_to_all x2, waiting for transfers between devices, reduce_to_slice(): arrived = lax.all_to_all(pieces, 'kv', 0, 0, tiled=True)  6.05 us
    select_n x1, other arithmetic, place_cache(): jnp.where(slot_pos < moved_len, cached, jnp.where(slot_pos == moved_len,...  5.63 us
    dot_general x1, matrix products, attend_pool(): jnp.einsum('rkgt,tkd->rkgd', weights, values, preferred_element_type=jnp....  5.33 us
  transfers between devices with their start and end apart: 5, of which 3 were waited for; matrix products, arithmetic and copies ran while one was open for 43% of the time, Pallas kernels for 0%

profile of v6, /device:TPU:1, one launch (start us, length us, event | category | flops | bytes accessed | tf_op | source)
XLA Modules:
  0.0 179.6 jit_solution(17588488345183413323)
XLA Ops:
  7.2 1.6 broadcast_in_dim.64
  8.8 6.8 %all-to-all-start = ((bf16[8,64,256]{2,1,0:T(8,128)(2,1)}), bf16[8,64,256]{2,1,0:T(8,128)(2,1)S(1)}, u32[]{:S(2)}, u32[]{:S(2)}) async-start(bf16[8,64,256]{2,1,0:T(8,128)(2,1)} %broadcast_in_dim.64), calls=%async_computation | async-start | bytes 524288 | tf_op jit(solution)/shard_map/all_to_all | solution.py:121
  15.6 2.0 %pad_maximum_fusion.1 = bf16[144,2048]{1,0:T(8,128)(2,1)} fusion(bf16[48,2048]{1,0:T(8,128)(2,1)} %bitcast.173, bf16[48,2048]{1,0:T(8,128)(2,1)} %bitcast.174, bf16[48,2048]{1,0:T(8,128)(2,1)} %bitcast.175), kind=kLoop, calls=%fused_computation.54 | loop fusion | flops 1769472 | bytes 1179648 | tf_op jit(solution)/shard_map/concatenate | solution.py:114
  17.6 0.7 fusion.69
  18.3 0.6 scatter_custom_fusion
  18.9 1.3 gather_fusion
  20.4 0.1 copy.46
  20.5 0.7 gather_fusion.8
  21.1 0.7 gather_fusion.9
  21.8 0.7 gather_fusion.6
  22.5 0.7 gather_fusion.7
  23.2 0.1 copy.50
  23.2 0.1 reshape.482
  23.4 0.7 gather_fusion.1
  24.1 0.7 fusion.14
  24.9 1.0 select_reduce_fusion
  25.9 0.1 iota_compare_fusion.2
  26.0 1.6 add.137
  27.7 2.1 %and.30 = pred[64,174,128]{2,1,0:T(8,128)(4,1)S(1)} broadcast(pred[64,174]{1,0:T(8,128)(4,1)S(1)} %fusion.14), dimensions={0,1} | broadcast | bytes 1436544 | tf_op jit(solution)/shard_map/and | solution.py:48
  29.8 3.9 %fusion.6 = pred[64,22272]{1,0:T(8,128)(4,1)S(1)} fusion(s32[8,8,174,128]{3,2,1,0:T(8,128)S(1)} %bitcast.160, pred[8,8,174,128]{3,2,1,0:T(8,128)(4,1)S(1)} %bitcast.164, s32[64]{0:T(128)S(1)} %copy-done.1, s32[22272]{0:T(1024)S(1)} %iota_bitcast_fusion), kind=kLoop, calls=%fused_computation.21 | loop fusion | flops 4276224 | bytes 8641792 | tf_op jit(solution)/shard_map/and | solution.py:48
  33.7 4.8 %gather_fusion.2 = bf16[64,128,128]{2,1,0:T(8,128)(2,1)} fusion(bf16[174,128,128]{2,1,0:T(8,128)(2,1)} %param.28, s32[1024]{0:T(1024)S(1)} %pad_clamp_fusion), kind=kCustom, calls=%fused_computation.2 | custom fusion | bytes 4194560 | tf_op jit(solution)/shard_map/gather | solution.py:153
  38.5 4.8 %gather_fusion.3 = bf16[64,128,128]{2,1,0:T(8,128)(2,1)} fusion(bf16[174,128,128]{2,1,0:T(8,128)(2,1)} %param.29, s32[1024]{0:T(1024)S(1)} %pad_clamp_fusion), kind=kCustom, calls=%fused_computation.3 | custom fusion | bytes 4194560 | tf_op jit(solution)/shard_map/gather | solution.py:153
  43.3 2.3 %copy.54 = bf16[256,2048]{1,0:T(8,128)(2,1)} copy(bf16[256,2048]{0,1:T(8,128)(2,1)} %bitcast.169) | data formatting | bytes 2097152 | tf_op jit(solution)/shard_map/dot_general | solution.py:128
  45.6 0.2 multiply_cosine_fusion.1
  45.9 0.2 fusion.38
  46.1 0.1 multiply_convert_fusion
  46.2 1.4 multiply_reduce_fusion.1
  47.6 0.1 multiply_bitcast_fusion
  47.6 0.2 fusion.67
  47.9 0.1 pad_maximum_fusion.3
  47.9 0.6 gather_fusion.4
  48.5 1.3 fusion.79
  49.8 0.6 gather_fusion.5
  50.4 0.1 fusion.46
  50.5 0.2 copy.44
  50.6 0.1 reshape.552
  50.8 0.1 fusion.92
  50.9 1.8 multiply_reduce_fusion
  52.6 0.1 multiply_multiply_fusion
  52.7 0.1 subtract_convert_fusion
  52.8 0.1 pad_maximum_fusion.2
  52.9 0.2 fusion.63
  53.1 0.1 copy.53
  53.2 5.2 %fusion.78 = (f32[64,2]{0,1:T(2,128)S(1)}, f32[64,1,2,22272]{3,0,2,1:T(8,128)S(1)}) fusion(bf16[64,2,128]{2,0,1:T(8,128)(2,1)S(1)} %pad_maximum_fusion.2, bf16[22272,128,1]{1,0,2:T(8,128)(2,1)} %bitcast.161, pred[64,22272]{1,0:T(8,128)(4,1)S(1)} %fusion.6), kind=kOutput, calls=%fused_computation.145 | convolution fusion | flops 738361216 | bytes 18563584 | tf_op jit(solution)/shard_map/rkgd,tkd->rkgt/dot_general | solution.py:54
  58.4 2.3 %fusion.2 = f32[64,2]{0,1:T(2,128)S(1)} fusion(f32[64,1,2,22272]{3,0,2,1:T(8,128)S(1)} %get-tuple-element.34, f32[64,2]{0,1:T(2,128)S(1)} %fusion.68), kind=kLoop, calls=%fused_computation.16 | loop fusion | flops 5701504 | bytes 11404288 | tf_op jit(solution)/shard_map/reduce_sum | solution.py:65
  60.7 5.3 %fusion.30 = f32[64,1,2,128]{3,0,2,1:T(8,128)S(1)} fusion(bf16[22272,128,1]{1,0,2:T(8,128)(2,1)} %bitcast.170, f32[64,2]{0,1:T(2,128)S(1)} %get-tuple-element.18, f32[64,1,2,22272]{3,0,2,1:T(8,128)S(1)} %get-tuple-element.34, f32[64,2]{0,1:T(2,128)S(1)} %fusion.68, f32[64,128]{1,0:T(8,128)S(1)} %get-tuple-element.35, f32[64,2]{0,1:T(2,128)S(1)} %get-tuple-element.17), kind=kOutput, calls=%fused_computation.45 | convolution fusion | flops 738394112 | bytes 17204736 | tf_op jit(solution)/shard_map/rkgt,tkd->rkgd/dot_general | solution.py:71
  66.1 3.0 %fusion.34 = f32[64,2048]{1,0:T(8,128)} fusion(bf16[256,2048]{1,0:T(8,128)(2,1)S(1)} %copy-done, bf16[64,2048]{1,0:T(8,128)(2,1)S(1)} %multiply_convert_fusion, bf16[2048,256]{1,0:T(8,128)(2,1)} %param.24, f32[8,8,2,128]{3,2,1,0:T(2,128)S(1)} %bitcast.172), kind=kOutput, calls=%fused_computation.47 | convolution fusion | flops 134299648 | bytes 2949120 | tf_op jit(solution)/shard_map/dot_general | solution.py:175
  69.0 1.9 %copy.76 = f32[8,8,8,256]{3,2,0,1:T(8,128)} copy(f32[8,8,8,256]{3,2,1,0:T(8,128)} %bitcast.168) | data formatting | bytes 1048576 | tf_op jit(solution)/shard_map/reshape | solution.py:78
  70.9 4.5 %all-to-all-start.1 = ((f32[8,64,256]{2,1,0:T(8,128)}), f32[8,64,256]{2,1,0:T(8,128)}, u32[]{:S(2)}, u32[]{:S(2)}) async-start(f32[8,64,256]{2,1,0:T(8,128)} %bitcast.166), calls=%async_computation.1 | async-start | bytes 1048576 | tf_op jit(solution)/shard_map/all_to_all | solution.py:79
  75.4 5.6 %bitcast_select_fusion.1 = (bf16[16,1,512,128]{3,2,1,0:T(8,128)(2,1)S(1)}, bf16[16,1,512,128]{3,2,1,0:T(8,128)(2,1)S(1)}) fusion(pred[16,512]{1,0:T(8,128)(4,1)S(1)} %get-tuple-element.24, pred[16,512]{1,0:T(8,128)(4,1)S(1)} %get-tuple-element.23, bf16[16,128]{1,0:T(8,128)(2,1)S(1)} %gather_fusion.4, bf16[16,128]{1,0:T(8,128)(2,1)S(1)} %gather_fusion.5, ...), kind=kLoop, calls=%fused_computation.32 | loop fusion | flops 4194304 | bytes 8413184 | tf_op jit(solution)/shard_map/jit(_where)/select_n | solution.py:158
  81.1 2.4 %pad_maximum_fusion = bf16[16,2,512,128]{3,2,1,0:T(8,128)(2,1)} fusion(bf16[16,1,512,128]{3,2,1,0:T(8,128)(2,1)S(1)} %get-tuple-element.16, bf16[16,1,512,128]{3,2,1,0:T(8,128)(2,1)S(1)} %get-tuple-element.15), kind=kLoop, calls=%fused_computation.22 | loop fusion | flops 2097152 | bytes 8388608 | tf_op jit(solution)/shard_map/stack | solution.py:163
  83.5 1.4 all-to-all-done.1
  84.9 7.1 %all-to-all-start.3 = ((bf16[16,2,512,128]{3,2,1,0:T(8,128)(2,1)}), bf16[16,2,512,128]{3,2,1,0:T(8,128)(2,1)}, u32[]{:S(2)}, u32[]{:S(2)}) async-start(bf16[16,2,512,128]{3,2,1,0:T(8,128)(2,1)} %pad_maximum_fusion), calls=%async_computation.3 | async-start | bytes 8388608 | tf_op jit(solution)/shard_map/all_to_all | solution.py:162
  92.0 1.1 reduce_sum.77
  93.1 13.9 %all_gather.9 = bf16[64,2048]{1,0:T(8,128)(2,1)S(1)} all-gather(bf16[64,256]{1,0:T(8,128)(2,1)S(1)} %add_convert_fusion.1), channel_id=1, replica_groups=mesh['req'=16,'kv'=8] {'kv'}, dimensions={1}, use_global_device_ids=true | all-gather | bytes 294912 | tf_op jit(solution)/shard_map/all_gather | solution.py:180
  107.1 0.2 fusion.35
  107.2 2.9 %fusion.11 = f32[64,16,48]{0,2,1:T(8,128)S(1)} fusion(bf16[16,144,2048]{2,1,0:T(8,128)(2,1)} %bitcast.180, bf16[64,2048]{1,0:T(8,128)(2,1)S(1)} %all_gather.9, f32[2048]{0:T(1024)S(1)} %copy-done.9, f32[64]{0:T(128)S(1)} %add_rsqrt_fusion.1), kind=kOutput, calls=%fused_computation.27 | convolution fusion | flops 201850880 | bytes 3612928 | tf_op jit(solution)/shard_map/rd,sud->rsu/dot_general | solution.py:182
  110.2 5.2 %fusion.7 = f32[64,2048,1]{1,0,2:T(8,128)S(1)} fusion(bf16[16,144,2048]{2,1,0:T(8,128)(2,1)} %bitcast.181, f32[64,16,48]{0,2,1:T(8,128)S(1)} %fusion.11, bf16[64,2048]{1,0:T(8,128)(2,1)S(1)} %all_gather.9, f32[2048]{0:T(1024)S(1)} %copy-done.9, f32[64]{0:T(128)S(1)} %add_rsqrt_fusion.1), kind=kOutput, calls=%fused_computation.23 | convolution fusion | flops 403472384 | bytes 7282944 | tf_op jit(solution)/shard_map/rsu,suc->rc/dot_general | solution.py:185
  115.4 0.8 copy.75
  116.2 33.8 %all-to-all-done.3 = bf16[16,2,512,128]{3,2,1,0:T(8,128)(2,1)} async-done(((bf16[16,2,512,128]{3,2,1,0:T(8,128)(2,1)}), bf16[16,2,512,128]{3,2,1,0:T(8,128)(2,1)}, u32[]{:S(2)}, u32[]{:S(2)}) %all-to-all-start.3) | async-done | bytes 4194336 | tf_op jit(solution)/shard_map/all_to_all | solution.py:162
  150.0 12.7 %all-to-all-start.2 = ((f32[8,64,256]{2,1,0:T(8,128)}), f32[8,64,256]{2,1,0:T(8,128)S(1)}, u32[]{:S(2)}, u32[]{:S(2)}) async-start(f32[8,64,256]{2,1,0:T(8,128)} %bitcast.155), calls=%async_computation.2 | async-start | bytes 1048576 | tf_op jit(solution)/shard_map/all_to_all | solution.py:79
  162.7 4.7 %slice_bitcast_fusion = (bf16[16,512,128]{2,1,0:T(8,128)(2,1)}, bf16[16,512,128]{2,1,0:T(8,128)(2,1)}) fusion(bf16[16,2,512,128]{3,2,1,0:T(8,128)(2,1)} %all-to-all-done.3), kind=kLoop, calls=%fused_computation.29 | loop fusion | bytes 8388608 | tf_op jit(solution)/shard_map/squeeze | solution.py:170
  167.4 4.7 %all-to-all-done.2 = f32[8,64,256]{2,1,0:T(8,128)S(1)} async-done(((f32[8,64,256]{2,1,0:T(8,128)}), f32[8,64,256]{2,1,0:T(8,128)S(1)}, u32[]{:S(2)}, u32[]{:S(2)}) %all-to-all-start.2) | async-done | bytes 524320 | tf_op jit(solution)/shard_map/all_to_all | solution.py:79
  172.1 0.6 add_convert_fusion
  (52 shorter events, 0.6 us)
Async XLA Ops:
  7.2 58.9 %copy-start = (bf16[256,2048]{1,0:T(8,128)(2,1)S(1)}, bf16[256,2048]{1,0:T(8,128)(2,1)}, u32[]{:S(2)}) copy-start(bf16[256,2048]{1,0:T(8,128)(2,1)} %param.27) | copy-start | bytes 3145732
  7.2 13.1 %copy-start.8 = (s32[2]{0:T(128)S(1)}, s32[2]{0:T(128)}, u32[]{:S(2)}) copy-start(s32[2]{0:T(128)} %constant.73) | copy-start | bytes 28
  7.2 13.2 %copy-start.2 = (s32[64,32]{0,1:T(8,128)S(1)}, s32[64,32]{0,1:T(8,128)}, u32[]{:S(2)}) copy-start(s32[64,32]{0,1:T(8,128)} %param.31) | copy-start | bytes 24580
  7.2 16.2 %copy-start.1 = (s32[64]{0:T(128)S(1)}, s32[64]{0:T(128)}, u32[]{:S(2)}) copy-start(s32[64]{0:T(128)} %param.30) | copy-start | bytes 772
  8.8 37.0 %all-to-all-start = ((bf16[8,64,256]{2,1,0:T(8,128)(2,1)}), bf16[8,64,256]{2,1,0:T(8,128)(2,1)S(1)}, u32[]{:S(2)}, u32[]{:S(2)}) async-start(bf16[8,64,256]{2,1,0:T(8,128)(2,1)} %broadcast_in_dim.64), calls=%async_computation | async-start | bytes 524288 | tf_op jit(solution)/shard_map/all_to_all | solution.py:121
  15.6 91.7 %all-gather.3.cloned.1.call-start = ((), (), s32[]{:S(2)}) async-start(), calls=%async_computation.4 | async-start | bytes 10027008 | tf_op jit(solution)/shard_map/all_gather | solution.py:113
  38.5 4.8 %copy-start.5 = (f32[2048]{0:T(1024)S(1)}, f32[2048]{0:T(1024)}, u32[]{:S(2)}) copy-start(f32[2048]{0:T(1024)} %param.20) | copy-start | bytes 24580
  43.3 4.3 %copy-start.6 = (f32[128]{0:T(128)S(1)}, f32[128]{0:T(128)}, u32[]{:S(2)}) copy-start(f32[128]{0:T(128)} %param.22) | copy-start | bytes 1540
  45.9 6.7 %copy-start.7 = (f32[128]{0:T(128)S(1)}, f32[128]{0:T(128)}, u32[]{:S(2)}) copy-start(f32[128]{0:T(128)} %param.21) | copy-start | bytes 1540
  66.0 9.4 %copy-start.3 = (bf16[64,128,128]{2,1,0:T(8,128)(2,1)S(1)}, bf16[64,128,128]{2,1,0:T(8,128)(2,1)}, u32[]{:S(2)}) copy-start(bf16[64,128,128]{2,1,0:T(8,128)(2,1)} %gather_fusion.2) | copy-start | bytes 6291460
  70.9 14.0 %all-to-all-start.1 = ((f32[8,64,256]{2,1,0:T(8,128)}), f32[8,64,256]{2,1,0:T(8,128)}, u32[]{:S(2)}, u32[]{:S(2)}) async-start(f32[8,64,256]{2,1,0:T(8,128)} %bitcast.166), calls=%async_computation.1 | async-start | bytes 1048576 | tf_op jit(solution)/shard_map/all_to_all | solution.py:79
  83.5 9.6 %copy-start.4 = (bf16[64,256]{1,0:T(8,128)(2,1)S(1)}, bf16[64,256]{1,0:T(8,128)(2,1)}, u32[]{:S(2)}) copy-start(bf16[64,256]{1,0:T(8,128)(2,1)} %param.19) | copy-start | bytes 98308
  83.5 23.7 %copy-start.9 = (f32[2048]{0:T(1024)S(1)}, f32[2048]{0:T(1024)}, u32[]{:S(2)}) copy-start(f32[2048]{0:T(1024)} %param.34) | copy-start | bytes 24580
  84.9 65.1 %all-to-all-start.3 = ((bf16[16,2,512,128]{3,2,1,0:T(8,128)(2,1)}), bf16[16,2,512,128]{3,2,1,0:T(8,128)(2,1)}, u32[]{:S(2)}, u32[]{:S(2)}) async-start(bf16[16,2,512,128]{3,2,1,0:T(8,128)(2,1)} %pad_maximum_fusion), calls=%async_computation.3 | async-start | bytes 8388608 | tf_op jit(solution)/shard_map/all_to_all | solution.py:162
  150.0 22.1 %all-to-all-start.2 = ((f32[8,64,256]{2,1,0:T(8,128)}), f32[8,64,256]{2,1,0:T(8,128)S(1)}, u32[]{:S(2)}, u32[]{:S(2)}) async-start(f32[8,64,256]{2,1,0:T(8,128)} %bitcast.155), calls=%async_computation.2 | async-start | bytes 1048576 | tf_op jit(solution)/shard_map/all_to_all | solution.py:79
Sparse Core Ops, SparseCore 0:
  18.6 76.5 all-gather.2

commit v7 on v4

--- a/solution.py
+++ b/solution.py
@@ -78,6 +78,20 @@
     pieces = partial.reshape(rows, kv_count, slice_width).transpose(1, 0, 2)
     arrived = lax.all_to_all(pieces, "kv", 0, 0, tiled=True)
     return jnp.sum(arrived, axis=0)
+
+
+def reduce_by_permutes(partial, kv_count, slice_width):
+    rows = partial.shape[0]
+    pieces = partial.reshape(rows, kv_count, slice_width).transpose(1, 0, 2)
+    me = lax.axis_index("kv")
+    total = pieces[me]
+    for shift in range(1, kv_count):
+        total = total + lax.ppermute(
+            pieces[(me + shift) % kv_count],
+            "kv",
+            [(k, (k + shift) % kv_count) for k in range(kv_count)],
+        )
+    return total
 
 
 def layer_body(
@@ -177,7 +191,7 @@
     down_part = jnp.einsum(
         "rsu,suc->rc", activation, down_w, preferred_element_type=jnp.float32
     )
-    mlp_part = reduce_to_slice(down_part, kv_count, slice_width)
+    mlp_part = reduce_by_permutes(down_part, kv_count, slice_width)
     out_hidden = (mid_slice.astype(jnp.float32) + mlp_part).astype(jnp.bfloat16)
     return (out_hidden, mig_keys, mig_values)
 

time: 177 us -> 161 us (0.910)
  the two profiles are of different devices: /device:TPU:1 before, /device:TPU:52 now
where the time goes in v7:
time: 161 us
  waiting for transfers between devices  31.8 us (20%)
  blocking collectives  26.8 us (17%)
  local copies, waits for them, and re-layouts  24.8 us (15%)
  other arithmetic  21.6 us (13%)
  matrix products  21.1 us (13%)
  starting transfers between devices  20 us (12%)
  between operations  14.6 us (9%)
    all_to_all x1, waiting for transfers between devices, layer_body(): lax.all_to_all(jnp.stack([place_cache(k_pool, new_keys), place_cache(v_po...  31.8 us
    all_gather x1, blocking collectives, layer_body(): whole_rows = lax.all_gather(hidden, 'kv', axis=1, tiled=True)  14 us
    all_gather x1, blocking collectives, layer_body(): mid_stream = lax.all_gather(mid_slice, 'kv', axis=1, tiled=True)  12.8 us
    gather x2, local copies, waits for them, and re-layouts, place_cache(): cached = pool[moved_pages].reshape(mig_count, slot_count, channels)  8.44 us
    ppermute x7, starting transfers between devices, reduce_by_permutes(): lax.ppermute(pieces[(me + shift) % kv_count], 'kv', [(k, (k + shift) % kv...  8.1 us
    all_to_all x1, starting transfers between devices, layer_body(): lax.all_to_all(jnp.stack([place_cache(k_pool, new_keys), place_cache(v_po...  7.36 us
    select_n x1, other arithmetic, place_cache(): jnp.where(slot_pos < moved_len, cached, jnp.where(slot_pos == moved_len,...  5.63 us
    dot_general x1, matrix products, attend_pool(): jnp.einsum('rkgt,tkd->rkgd', weights, values, preferred_element_type=jnp....  5.29 us
  transfers between devices with their start and end apart: 10, of which 1 were waited for; matrix products, arithmetic and copies ran while one was open for 40% of the time, Pallas kernels for 0%

profile of v7, /device:TPU:52, one launch (start us, length us, event | category | flops | bytes accessed | tf_op | source)
XLA Modules:
  0.0 160.7 jit_solution(989818514581505281)
XLA Ops:
  7.3 2.1 %pad_maximum_fusion.1 = bf16[144,2048]{1,0:T(8,128)(2,1)} fusion(bf16[48,2048]{1,0:T(8,128)(2,1)} %bitcast.194, bf16[48,2048]{1,0:T(8,128)(2,1)} %bitcast.195, bf16[48,2048]{1,0:T(8,128)(2,1)} %bitcast.196), kind=kLoop, calls=%fused_computation.53 | loop fusion | flops 1769472 | bytes 1179648 | tf_op jit(solution)/shard_map/concatenate | solution.py:128
  9.4 14.0 %all_gather.12 = bf16[64,2048]{1,0:T(8,128)(2,1)S(1)} all-gather(bf16[64,256]{1,0:T(8,128)(2,1)} %param.19), channel_id=1, replica_groups=mesh['req'=16,'kv'=8] {'kv'}, dimensions={1}, use_global_device_ids=true | all-gather | bytes 294912 | tf_op jit(solution)/shard_map/all_gather | solution.py:133
  23.4 0.2 fusion.35
  23.5 1.7 %fusion.89 = f32[64,256]{1,0:T(8,128)S(1)} fusion(bf16[2048,256]{1,0:T(8,128)(2,1)} %param.23, bf16[64,2048]{1,0:T(8,128)(2,1)S(1)} %all_gather.12, f32[2048]{0:T(1024)} %param.20, f32[64]{0:T(128)S(1)} %add_rsqrt_fusion.3), kind=kOutput, calls=%fused_computation.166 | convolution fusion | flops 67633152 | bytes 1384704 | tf_op jit(solution)/shard_map/dot_general | solution.py:135
  25.3 0.4 multiply_reduce_fusion.1
  25.7 0.1 multiply_bitcast_fusion
  25.8 0.2 fusion.75
  26.0 0.1 multiply_reduce_fusion
  26.2 0.1 fusion.103
  26.3 0.2 multiply_cosine_fusion.1
  26.5 0.1 fusion.53
  26.6 0.1 subtract_convert_fusion
  26.7 0.1 pad_maximum_fusion.2
  26.8 0.2 fusion.71
  27.0 0.1 copy.49
  27.1 0.1 copy.43
  27.2 0.1 iota_compare_fusion.3
  27.3 0.7 fusion.14
  28.0 1.0 select_reduce_fusion
  29.1 1.6 %add.225 = s32[64,174,128]{2,1,0:T(8,128)S(1)} broadcast(s32[64,174]{1,0:T(8,128)S(1)} %select_reduce_fusion), dimensions={0,1} | broadcast | bytes 5746176 | tf_op jit(solution)/shard_map/add | solution.py:47
  30.7 2.1 %and.60 = pred[64,174,128]{2,1,0:T(8,128)(4,1)S(1)} broadcast(pred[64,174]{1,0:T(8,128)(4,1)S(1)} %fusion.14), dimensions={0,1} | broadcast | bytes 1436544 | tf_op jit(solution)/shard_map/and | solution.py:48
  32.8 3.9 %fusion.6 = pred[64,22272]{1,0:T(8,128)(4,1)S(1)} fusion(s32[8,8,174,128]{3,2,1,0:T(8,128)S(1)} %bitcast.184, pred[8,8,174,128]{3,2,1,0:T(8,128)(4,1)S(1)} %bitcast.188, s32[64]{0:T(128)S(1)} %copy-done.1, s32[22272]{0:T(1024)S(1)} %iota_bitcast_fusion), kind=kLoop, calls=%fused_computation.21 | loop fusion | flops 4276224 | bytes 8641792 | tf_op jit(solution)/shard_map/and | solution.py:48
  36.7 4.2 %fusion.93 = (f32[64,2]{0,1:T(2,128)S(1)}, f32[64,1,2,22272]{3,0,2,1:T(8,128)S(1)}) fusion(bf16[64,2,128]{2,0,1:T(8,128)(2,1)S(1)} %pad_maximum_fusion.2, bf16[22272,128,1]{1,0,2:T(8,128)(2,1)} %bitcast.185, pred[64,22272]{1,0:T(8,128)(4,1)S(1)} %fusion.6), kind=kOutput, calls=%fused_computation.167 | convolution fusion | flops 738361216 | bytes 18563584 | tf_op jit(solution)/shard_map/rkgd,tkd->rkgt/dot_general | solution.py:54
  41.0 2.3 %fusion.2 = f32[64,2]{0,1:T(2,128)S(1)} fusion(f32[64,1,2,22272]{3,0,2,1:T(8,128)S(1)} %get-tuple-element.36, f32[64,2]{0,1:T(2,128)S(1)} %fusion.76), kind=kLoop, calls=%fused_computation.16 | loop fusion | flops 5701504 | bytes 11404288 | tf_op jit(solution)/shard_map/reduce_sum | solution.py:65
  43.3 0.3 fusion.94
  43.6 5.3 %fusion.30 = f32[64,1,2,128]{3,0,2,1:T(8,128)S(1)} fusion(bf16[22272,128,1]{1,0,2:T(8,128)(2,1)} %bitcast.191, f32[64,2]{0,1:T(2,128)S(1)} %get-tuple-element.22, f32[64,1,2,22272]{3,0,2,1:T(8,128)S(1)} %get-tuple-element.36, f32[64,2]{0,1:T(2,128)S(1)} %fusion.76, f32[64,128]{1,0:T(8,128)S(1)} %get-tuple-element.37, f32[64,2]{0,1:T(2,128)S(1)} %get-tuple-element.21), kind=kOutput, calls=%fused_computation.45 | convolution fusion | flops 738394112 | bytes 17204736 | tf_op jit(solution)/shard_map/rkgt,tkd->rkgd/dot_general | solution.py:71
  49.0 0.9 fusion.34
  49.9 0.9 copy.86
  50.7 4.5 %all-to-all-start = ((f32[8,64,256]{2,1,0:T(8,128)}), f32[8,64,256]{2,1,0:T(8,128)}, u32[]{:S(2)}, u32[]{:S(2)}) async-start(f32[8,64,256]{2,1,0:T(8,128)} %bitcast.175), calls=%async_computation | async-start | bytes 1048576 | tf_op jit(solution)/shard_map/all_to_all | solution.py:79
  55.3 0.8 scatter_custom_fusion
  56.1 0.7 gather_fusion
  56.8 0.1 iota_add_fusion.2
  56.9 0.7 gather_fusion.8
  57.5 0.7 gather_fusion.9
  58.2 0.7 gather_fusion.6
  58.9 0.7 gather_fusion.7
  59.6 0.1 copy.46
  59.7 0.1 reshape.485
  59.8 3.6 %gather_fusion.2 = bf16[64,128,128]{2,1,0:T(8,128)(2,1)S(1)} fusion(bf16[174,128,128]{2,1,0:T(8,128)(2,1)} %param.28, s32[1024]{0:T(1024)S(1)} %pad_clamp_fusion), kind=kCustom, calls=%fused_computation.2 | custom fusion | bytes 4194560 | tf_op jit(solution)/shard_map/gather | solution.py:161
  63.4 4.8 %gather_fusion.4 = bf16[64,128,128]{2,1,0:T(8,128)(2,1)} fusion(bf16[174,128,128]{2,1,0:T(8,128)(2,1)} %param.29, s32[1024]{0:T(1024)S(1)} %pad_clamp_fusion), kind=kCustom, calls=%fused_computation.4 | custom fusion | bytes 4194560 | tf_op jit(solution)/shard_map/gather | solution.py:161
  68.2 0.7 gather_fusion.1
  68.9 0.1 pad_maximum_fusion.3
  69.0 0.6 gather_fusion.3
  69.5 0.6 gather_fusion.5
  70.1 0.1 iota_compare_fusion.2
  70.2 5.6 %select_select_fusion.1 = (bf16[16,1,512,128]{3,2,1,0:T(8,128)(2,1)S(1)}, bf16[16,1,512,128]{3,2,1,0:T(8,128)(2,1)S(1)}) fusion(bf16[16,1,512,128]{3,2,1,0:T(8,128)(2,1)S(1)} %bitcast.186, pred[16,512]{1,0:T(8,128)(4,1)S(1)} %get-tuple-element.28, pred[16,512]{1,0:T(8,128)(4,1)S(1)} %get-tuple-element.27, bf16[16,128]{1,0:T(8,128)(2,1)S(1)} %gather_fusion.3, ...), kind=kLoop, calls=%fused_computation.32 | loop fusion | flops 4194304 | bytes 8413184 | tf_op jit(solution)/shard_map/jit(_where)/select_n | solution.py:163
  75.8 2.5 %pad_maximum_fusion = bf16[16,2,512,128]{3,2,1,0:T(8,128)(2,1)} fusion(bf16[16,1,512,128]{3,2,1,0:T(8,128)(2,1)S(1)} %get-tuple-element.20, bf16[16,1,512,128]{3,2,1,0:T(8,128)(2,1)S(1)} %get-tuple-element.19), kind=kLoop, calls=%fused_computation.22 | loop fusion | flops 2097152 | bytes 8388608 | tf_op jit(solution)/shard_map/stack | solution.py:168
  78.3 7.4 %all-to-all-start.1 = ((bf16[16,2,512,128]{3,2,1,0:T(8,128)(2,1)}), bf16[16,2,512,128]{3,2,1,0:T(8,128)(2,1)}, u32[]{:S(2)}, u32[]{:S(2)}) async-start(bf16[16,2,512,128]{3,2,1,0:T(8,128)(2,1)} %pad_maximum_fusion), calls=%async_computation.1 | async-start | bytes 8388608 | tf_op jit(solution)/shard_map/all_to_all | solution.py:167
  85.7 1.1 reduce_sum.68
  86.8 12.8 %all_gather.13 = bf16[64,2048]{1,0:T(8,128)(2,1)S(1)} all-gather(bf16[64,256]{1,0:T(8,128)(2,1)S(1)} %add_convert_fusion), channel_id=1, replica_groups=mesh['req'=16,'kv'=8] {'kv'}, dimensions={1}, use_global_device_ids=true | all-gather | bytes 294912 | tf_op jit(solution)/shard_map/all_gather | solution.py:186
  99.6 0.2 fusion.38
  99.8 2.9 %fusion.11 = f32[64,16,48]{0,2,1:T(8,128)S(1)} fusion(bf16[16,144,2048]{2,1,0:T(8,128)(2,1)} %bitcast.208, bf16[64,2048]{1,0:T(8,128)(2,1)S(1)} %all_gather.13, f32[2048]{0:T(1024)S(1)} %copy-done.12, f32[64]{0:T(128)S(1)} %add_rsqrt_fusion.1), kind=kOutput, calls=%fused_computation.27 | convolution fusion | flops 201850880 | bytes 3612928 | tf_op jit(solution)/shard_map/rd,sud->rsu/dot_general | solution.py:188
  102.7 5.2 %fusion.7 = f32[64,2048,1]{1,0,2:T(8,128)S(1)} fusion(bf16[16,144,2048]{2,1,0:T(8,128)(2,1)} %bitcast.209, f32[64,16,48]{0,2,1:T(8,128)S(1)} %fusion.11, bf16[64,2048]{1,0:T(8,128)(2,1)S(1)} %all_gather.13, f32[2048]{0:T(1024)S(1)} %copy-done.12, f32[64]{0:T(128)S(1)} %add_rsqrt_fusion.1), kind=kOutput, calls=%fused_computation.23 | convolution fusion | flops 403472384 | bytes 7282944 | tf_op jit(solution)/shard_map/rsu,suc->rc/dot_general | solution.py:191
  107.9 0.2 copy.63
  108.1 0.4 constant_dynamic-slice_fusion.7
  108.5 0.4 collective-permute-start
  108.9 0.3 collective-permute-start.1
  109.1 2.3 %collective-permute-start.2 = (f32[64,256]{1,0:T(8,128)S(1)}, f32[64,256]{1,0:T(8,128)S(1)}, u32[]{:S(2)}, u32[]{:S(2)}) collective-permute-start(f32[64,256]{1,0:T(8,128)S(1)} %bitcast.197), channel_id=1, source_target_pairs={{0,3},{1,4},{2,5},{3,6},{4,7},{5,0},{6,1},{7,2},{8,11},{9,12},{10,... | collective-permute-start | bytes 196616 | tf_op jit(solution)/shard_map/ppermute | solution.py:89
  111.5 1.0 collective-permute-start.3
  112.4 2.4 %collective-permute-start.4 = (f32[64,256]{1,0:T(8,128)S(1)}, f32[64,256]{1,0:T(8,128)S(1)}, u32[]{:S(2)}, u32[]{:S(2)}) collective-permute-start(f32[64,256]{1,0:T(8,128)S(1)} %bitcast.199), channel_id=1, source_target_pairs={{0,5},{1,6},{2,7},{3,0},{4,1},{5,2},{6,3},{7,4},{8,13},{9,14},{10,... | collective-permute-start | bytes 196616 | tf_op jit(solution)/shard_map/ppermute | solution.py:89
  114.8 1.8 %collective-permute-start.5 = (f32[64,256]{1,0:T(8,128)S(1)}, f32[64,256]{1,0:T(8,128)S(1)}, u32[]{:S(2)}, u32[]{:S(2)}) collective-permute-start(f32[64,256]{1,0:T(8,128)S(1)} %bitcast.201), channel_id=1, source_target_pairs={{0,6},{1,7},{2,0},{3,1},{4,2},{5,3},{6,4},{7,5},{8,14},{9,15},{10,... | collective-permute-start | bytes 196616 | tf_op jit(solution)/shard_map/ppermute | solution.py:89
  116.7 31.8 %all-to-all-done.1 = bf16[16,2,512,128]{3,2,1,0:T(8,128)(2,1)} async-done(((bf16[16,2,512,128]{3,2,1,0:T(8,128)(2,1)}), bf16[16,2,512,128]{3,2,1,0:T(8,128)(2,1)}, u32[]{:S(2)}, u32[]{:S(2)}) %all-to-all-start.1) | async-done | bytes 4194336 | tf_op jit(solution)/shard_map/all_to_all | solution.py:167
  148.4 4.7 %slice_bitcast_fusion = (bf16[16,512,128]{2,1,0:T(8,128)(2,1)}, bf16[16,512,128]{2,1,0:T(8,128)(2,1)}) fusion(bf16[16,2,512,128]{3,2,1,0:T(8,128)(2,1)} %all-to-all-done.1), kind=kLoop, calls=%fused_computation.29 | loop fusion | bytes 8388608 | tf_op jit(solution)/shard_map/squeeze | solution.py:175
  153.2 0.7 fusion.61
  (72 shorter events, 0.6 us)
Async XLA Ops:
  7.2 41.8 %copy-start = (bf16[256,2048]{1,0:T(8,128)(2,1)S(1)}, bf16[256,2048]{1,0:T(8,128)(2,1)}, u32[]{:S(2)}) copy-start(bf16[256,2048]{1,0:T(8,128)(2,1)} %param.27) | copy-start | bytes 3145732
  7.2 18.1 %copy-start.7 = (f32[2048]{0:T(1024)S(1)}, f32[2048]{0:T(1024)}, u32[]{:S(2)}) copy-start(f32[2048]{0:T(1024)} %param.20) | copy-start | bytes 24580
  7.2 18.1 %copy-start.1 = (s32[64]{0:T(128)S(1)}, s32[64]{0:T(128)}, u32[]{:S(2)}) copy-start(s32[64]{0:T(128)} %param.30) | copy-start | bytes 772
  7.2 18.1 %copy-start.11 = (bf16[2048,128]{1,0:T(8,128)(2,1)S(1)}, bf16[2048,128]{1,0:T(8,128)(2,1)}, u32[]{:S(2)}) copy-start(bf16[2048,128]{1,0:T(8,128)(2,1)} %param.25) | copy-start | bytes 1572868
  7.2 18.5 %copy-start.8 = (f32[128]{0:T(128)S(1)}, f32[128]{0:T(128)}, u32[]{:S(2)}) copy-start(f32[128]{0:T(128)} %param.22) | copy-start | bytes 1540
  7.2 19.3 %copy-start.9 = (f32[128]{0:T(128)S(1)}, f32[128]{0:T(128)}, u32[]{:S(2)}) copy-start(f32[128]{0:T(128)} %param.21) | copy-start | bytes 1540
  7.2 19.9 %copy-start.3 = (s32[64,32]{0,1:T(8,128)S(1)}, s32[64,32]{0,1:T(8,128)}, u32[]{:S(2)}) copy-start(s32[64,32]{0,1:T(8,128)} %param.31) | copy-start | bytes 24580
  7.2 92.5 %all-gather.3.cloned.1.call-start = ((), (), s32[]{:S(2)}) async-start(), calls=%async_computation.2 | async-start | bytes 10027008 | tf_op jit(solution)/shard_map/all_gather | solution.py:127
  41.0 2.3 %copy-start.5 = (bf16[2048,128]{1,0:T(8,128)(2,1)S(1)}, bf16[2048,128]{1,0:T(8,128)(2,1)}, u32[]{:S(2)}) copy-start(bf16[2048,128]{1,0:T(8,128)(2,1)} %param.26) | copy-start | bytes 1572868
  43.6 5.4 %copy-start.4 = (bf16[2048,256]{1,0:T(8,128)(2,1)S(1)}, bf16[2048,256]{1,0:T(8,128)(2,1)}, u32[]{:S(2)}) copy-start(bf16[2048,256]{1,0:T(8,128)(2,1)} %param.24) | copy-start | bytes 3145732
  48.9 6.4 %copy-start.13 = (s32[1,16]{1,0:T(1,128)S(1)}, s32[1,16]{1,0:T(1,128)}, u32[]{:S(2)}) copy-start(s32[1,16]{1,0:T(1,128)} %param.33) | copy-start | bytes 196
  48.9 7.2 %copy-start.2 = (s32[1,16]{1,0:T(1,128)S(1)}, s32[1,16]{1,0:T(1,128)}, u32[]{:S(2)}) copy-start(s32[1,16]{1,0:T(1,128)} %param.32) | copy-start | bytes 196
  48.9 7.9 %copy-start.10 = (s32[2]{0:T(128)S(1)}, s32[2]{0:T(128)}, u32[]{:S(2)}) copy-start(s32[2]{0:T(128)} %constant.124) | copy-start | bytes 28
  50.7 27.6 %all-to-all-start = ((f32[8,64,256]{2,1,0:T(8,128)}), f32[8,64,256]{2,1,0:T(8,128)}, u32[]{:S(2)}, u32[]{:S(2)}) async-start(f32[8,64,256]{2,1,0:T(8,128)} %bitcast.175), calls=%async_computation | async-start | bytes 1048576 | tf_op jit(solution)/shard_map/all_to_all | solution.py:79
  78.3 8.4 %copy-start.6 = (bf16[64,256]{1,0:T(8,128)(2,1)S(1)}, bf16[64,256]{1,0:T(8,128)(2,1)}, u32[]{:S(2)}) copy-start(bf16[64,256]{1,0:T(8,128)(2,1)} %param.19) | copy-start | bytes 98308
  78.3 21.5 %copy-start.12 = (f32[2048]{0:T(1024)S(1)}, f32[2048]{0:T(1024)}, u32[]{:S(2)}) copy-start(f32[2048]{0:T(1024)} %param.34) | copy-start | bytes 24580
  78.3 70.1 %all-to-all-start.1 = ((bf16[16,2,512,128]{3,2,1,0:T(8,128)(2,1)}), bf16[16,2,512,128]{3,2,1,0:T(8,128)(2,1)}, u32[]{:S(2)}, u32[]{:S(2)}) async-start(bf16[16,2,512,128]{3,2,1,0:T(8,128)(2,1)} %pad_maximum_fusion), calls=%async_computation.1 | async-start | bytes 8388608 | tf_op jit(solution)/shard_map/all_to_all | solution.py:167
  108.5 6.3 %collective-permute-start = (f32[64,256]{1,0:T(8,128)S(1)}, f32[64,256]{1,0:T(8,128)S(1)}, u32[]{:S(2)}, u32[]{:S(2)}) collective-permute-start(f32[64,256]{1,0:T(8,128)S(1)} %bitcast.203), channel_id=1, source_target_pairs={{0,1},{1,2},{2,3},{3,4},{4,5},{5,6},{6,7},{7,0},{8,9},{9,10},{10,1... | collective-permute-start | bytes 196616 | tf_op jit(solution)/shard_map/ppermute | solution.py:89
  108.9 7.8 %collective-permute-start.1 = (f32[64,256]{1,0:T(8,128)S(1)}, f32[64,256]{1,0:T(8,128)S(1)}, u32[]{:S(2)}, u32[]{:S(2)}) collective-permute-start(f32[64,256]{1,0:T(8,128)S(1)} %bitcast.202), channel_id=1, source_target_pairs={{0,2},{1,3},{2,4},{3,5},{4,6},{5,7},{6,0},{7,1},{8,10},{9,11},{10,... | collective-permute-start | bytes 196616 | tf_op jit(solution)/shard_map/ppermute | solution.py:89
  109.1 44.0 %collective-permute-start.2 = (f32[64,256]{1,0:T(8,128)S(1)}, f32[64,256]{1,0:T(8,128)S(1)}, u32[]{:S(2)}, u32[]{:S(2)}) collective-permute-start(f32[64,256]{1,0:T(8,128)S(1)} %bitcast.197), channel_id=1, source_target_pairs={{0,3},{1,4},{2,5},{3,6},{4,7},{5,0},{6,1},{7,2},{8,11},{9,12},{10,... | collective-permute-start | bytes 196616 | tf_op jit(solution)/shard_map/ppermute | solution.py:89
  111.5 41.7 %collective-permute-start.3 = (f32[64,256]{1,0:T(8,128)S(1)}, f32[64,256]{1,0:T(8,128)S(1)}, u32[]{:S(2)}, u32[]{:S(2)}) collective-permute-start(f32[64,256]{1,0:T(8,128)S(1)} %bitcast.198), channel_id=1, source_target_pairs={{0,4},{1,5},{2,6},{3,7},{4,0},{5,1},{6,2},{7,3},{8,12},{9,13},{10,... | collective-permute-start | bytes 196616 | tf_op jit(solution)/shard_map/ppermute | solution.py:89
  112.4 40.7 %collective-permute-start.4 = (f32[64,256]{1,0:T(8,128)S(1)}, f32[64,256]{1,0:T(8,128)S(1)}, u32[]{:S(2)}, u32[]{:S(2)}) collective-permute-start(f32[64,256]{1,0:T(8,128)S(1)} %bitcast.199), channel_id=1, source_target_pairs={{0,5},{1,6},{2,7},{3,0},{4,1},{5,2},{6,3},{7,4},{8,13},{9,14},{10,... | collective-permute-start | bytes 196616 | tf_op jit(solution)/shard_map/ppermute | solution.py:89
  114.8 38.3 %collective-permute-start.5 = (f32[64,256]{1,0:T(8,128)S(1)}, f32[64,256]{1,0:T(8,128)S(1)}, u32[]{:S(2)}, u32[]{:S(2)}) collective-permute-start(f32[64,256]{1,0:T(8,128)S(1)} %bitcast.201), channel_id=1, source_target_pairs={{0,6},{1,7},{2,0},{3,1},{4,2},{5,3},{6,4},{7,5},{8,14},{9,15},{10,... | collective-permute-start | bytes 196616 | tf_op jit(solution)/shard_map/ppermute | solution.py:89
  116.6 36.5 %collective-permute-start.6 = (f32[64,256]{1,0:T(8,128)S(1)}, f32[64,256]{1,0:T(8,128)S(1)}, u32[]{:S(2)}, u32[]{:S(2)}) collective-permute-start(f32[64,256]{1,0:T(8,128)S(1)} %bitcast.200), channel_id=1, source_target_pairs={{0,7},{1,0},{2,1},{3,2},{4,3},{5,4},{6,5},{7,6},{8,15},{9,8},{10,9... | collective-permute-start | bytes 196616 | tf_op jit(solution)/shard_map/ppermute | solution.py:89
Sparse Core Ops, SparseCore 0:
  10.8 75.6 all-gather.2

commit v8 on v7

--- a/solution.py
+++ b/solution.py
@@ -71,13 +71,6 @@
     return start_sum + jnp.einsum(
         "rkgt,tkd->rkgd", weights, values, preferred_element_type=jnp.float32
     )
-
-
-def reduce_to_slice(partial, kv_count, slice_width):
-    rows = partial.shape[0]
-    pieces = partial.reshape(rows, kv_count, slice_width).transpose(1, 0, 2)
-    arrived = lax.all_to_all(pieces, "kv", 0, 0, tiled=True)
-    return jnp.sum(arrived, axis=0)
 
 
 def reduce_by_permutes(partial, kv_count, slice_width):
@@ -165,14 +158,14 @@
         )
 
     moving = lax.all_to_all(
-        jnp.stack([place_cache(k_pool, new_keys), place_cache(v_pool, new_values)], axis=1),
+        jnp.stack([place_cache(k_pool, new_keys), place_cache(v_pool, new_values)], axis=0),
         "req",
-        0,
-        0,
+        1,
+        1,
         tiled=True,
     )
-    mig_keys = moving[:, 0]
-    mig_values = moving[:, 1]
+    mig_keys = moving[0]
+    mig_values = moving[1]
     context = attend_pool(queries, new_keys, new_values, k_pool, v_pool, lengths, page_table)
     gated = (jax.nn.sigmoid(gate_raw) * context.reshape(req_count, q_local * head_dim)).astype(
         jnp.bfloat16
@@ -181,7 +174,7 @@
     kv_count = lax.axis_size("kv")
     slice_width = model_width // kv_count
     mid_slice = (
-        hidden.astype(jnp.float32) + reduce_to_slice(head_terms, kv_count, slice_width)
+        hidden.astype(jnp.float32) + reduce_by_permutes(head_terms, kv_count, slice_width)
     ).astype(jnp.bfloat16)
     mid_stream = lax.all_gather(mid_slice, "kv", axis=1, tiled=True)
     normed_mlp = rms_norm(mid_stream, mlp_gain).astype(jnp.bfloat16)

time: 161 us -> 166 us (1.031)
  the two profiles are of different devices: /device:TPU:52 before, /device:TPU:1 now
where the time goes in v8:
time: 166 us
  waiting for transfers between devices  31.4 us (19%)
  blocking collectives  28.2 us (17%)
  starting transfers between devices  25.8 us (16%)
  local copies, waits for them, and re-layouts  25.6 us (15%)
  other arithmetic  21.4 us (13%)
  matrix products  18.9 us (11%)
  between operations  14.7 us (9%)
    all_gather x1, waiting for transfers between devices, layer_body(): lax.all_gather(jnp.concatenate([w_gate.T, w_up.T, w_down.T], axis=0), 're...  26.9 us
    ppermute x14, starting transfers between devices, reduce_by_permutes(): lax.ppermute(pieces[(me + shift) % kv_count], 'kv', [(k, (k + shift) % kv...  18.9 us
    all_gather x1, blocking collectives, layer_body(): whole_rows = lax.all_gather(hidden, 'kv', axis=1, tiled=True)  15.6 us
    all_gather x1, blocking collectives, layer_body(): mid_stream = lax.all_gather(mid_slice, 'kv', axis=1, tiled=True)  12.6 us
    gather x2, local copies, waits for them, and re-layouts, place_cache(): cached = pool[moved_pages].reshape(mig_count, slot_count, channels)  8.4 us
    all_to_all x1, starting transfers between devices, layer_body(): lax.all_to_all(jnp.stack([place_cache(k_pool, new_keys), place_cache(v_po...  6.86 us
    select_n x1, other arithmetic, place_cache(): jnp.where(slot_pos < moved_len, cached, jnp.where(slot_pos == moved_len,...  5.75 us
    dot_general x1, matrix products, attend_pool(): jnp.einsum('rkgt,tkd->rkgd', weights, values, preferred_element_type=jnp....  5.41 us
  transfers between devices with their start and end apart: 16, of which 4 were waited for; matrix products, arithmetic and copies ran while one was open for 38% of the time, Pallas kernels for 0%

profile of v8, /device:TPU:1, one launch (start us, length us, event | category | flops | bytes accessed | tf_op | source)
XLA Modules:
  0.0 165.9 jit_solution(10391686221967815773)
XLA Ops:
  7.3 2.1 %pad_maximum_fusion.1 = bf16[144,2048]{1,0:T(8,128)(2,1)} fusion(bf16[48,2048]{1,0:T(8,128)(2,1)} %bitcast.231, bf16[48,2048]{1,0:T(8,128)(2,1)} %bitcast.232, bf16[48,2048]{1,0:T(8,128)(2,1)} %bitcast.233), kind=kLoop, calls=%fused_computation.53 | loop fusion | flops 1769472 | bytes 1179648 | tf_op jit(solution)/shard_map/concatenate | solution.py:121
  9.4 0.7 fusion.85
  10.1 0.6 scatter_custom_fusion
  10.7 1.3 gather_fusion
  12.1 1.3 gather_fusion.1
  13.4 15.6 %all_gather.12 = bf16[64,2048]{1,0:T(8,128)(2,1)S(1)} all-gather(bf16[64,256]{1,0:T(8,128)(2,1)} %param.19), channel_id=1, replica_groups=mesh['req'=16,'kv'=8] {'kv'}, dimensions={1}, use_global_device_ids=true | all-gather | bytes 294912 | tf_op jit(solution)/shard_map/all_gather | solution.py:126
  29.0 0.2 fusion.35
  29.1 0.4 multiply_reduce_fusion.1
  29.6 0.2 fusion.83
  29.9 0.6 gather_fusion.3
  30.6 0.7 gather_fusion.8
  31.3 0.7 gather_fusion.9
  32.0 0.7 gather_fusion.6
  32.6 0.7 gather_fusion.7
  33.4 0.1 reshape.501
  33.5 3.6 %gather_fusion.2 = bf16[64,128,128]{2,1,0:T(8,128)(2,1)S(1)} fusion(bf16[174,128,128]{2,1,0:T(8,128)(2,1)} %param.28, s32[1024]{0:T(1024)S(1)} %pad_clamp_fusion), kind=kCustom, calls=%fused_computation.2 | custom fusion | bytes 4194560 | tf_op jit(solution)/shard_map/gather | solution.py:154
  37.2 4.8 %gather_fusion.4 = bf16[64,128,128]{2,1,0:T(8,128)(2,1)} fusion(bf16[174,128,128]{2,1,0:T(8,128)(2,1)} %param.29, s32[1024]{0:T(1024)S(1)} %pad_clamp_fusion), kind=kCustom, calls=%fused_computation.4 | custom fusion | bytes 4194560 | tf_op jit(solution)/shard_map/gather | solution.py:154
  41.9 1.3 fusion.102
  43.2 0.6 gather_fusion.5
  43.9 5.7 %select_select_fusion.1 = (bf16[1,16,512,128]{3,2,0,1:T(8,128)(2,1)S(1)}, bf16[1,16,512,128]{3,2,0,1:T(8,128)(2,1)S(1)}) fusion(bf16[1,16,512,128]{3,2,0,1:T(8,128)(2,1)S(1)} %bitcast.222, pred[16,512]{1,0:T(8,128)(4,1)S(1)} %get-tuple-element.36, pred[16,512]{1,0:T(8,128)(4,1)S(1)} %get-tuple-element.35, bf16[16,128]{1,0:T(8,128)(2,1)S(1)} %gather_fusion.3, ...), kind=kLoop, calls=%fused_computation.32 | loop fusion | flops 4194304 | bytes 8413184 | tf_op jit(solution)/shard_map/jit(_where)/select_n | solution.py:156
  49.7 2.3 %pad_maximum_fusion = bf16[2,16,512,128]{3,2,0,1:T(8,128)(2,1)} fusion(bf16[1,16,512,128]{3,2,0,1:T(8,128)(2,1)S(1)} %get-tuple-element.28, bf16[1,16,512,128]{3,2,0,1:T(8,128)(2,1)S(1)} %get-tuple-element.27), kind=kLoop, calls=%fused_computation.22 | loop fusion | flops 2097152 | bytes 8388608 | tf_op jit(solution)/shard_map/stack | solution.py:161
  52.0 6.9 %all-to-all-start = ((bf16[2,16,512,128]{3,2,0,1:T(8,128)(2,1)}), bf16[2,16,512,128]{3,2,0,1:T(8,128)(2,1)}, u32[]{:S(2)}, u32[]{:S(2)}) async-start(bf16[2,16,512,128]{3,2,0,1:T(8,128)(2,1)} %pad_maximum_fusion), calls=%async_computation | async-start | bytes 8388608 | tf_op jit(solution)/shard_map/all_to_all | solution.py:160
  59.0 0.3 fusion.97
  59.4 0.1 multiply_reduce_fusion
  59.6 0.1 fusion.111
  59.7 0.2 multiply_cosine_fusion.1
  60.0 0.1 subtract_convert_fusion
  60.2 0.2 fusion.79
  60.6 0.7 fusion.14
  61.3 1.0 select_reduce_fusion
  62.4 1.6 add.268
  64.0 2.1 %and.67 = pred[64,174,128]{2,1,0:T(8,128)(4,1)S(1)} broadcast(pred[64,174]{1,0:T(8,128)(4,1)S(1)} %fusion.14), dimensions={0,1} | broadcast | bytes 1436544 | tf_op jit(solution)/shard_map/and | solution.py:48
  66.1 4.1 %fusion.6 = pred[64,22272]{1,0:T(8,128)(4,1)S(1)} fusion(s32[8,8,174,128]{3,2,1,0:T(8,128)S(1)} %bitcast.218, pred[8,8,174,128]{3,2,1,0:T(8,128)(4,1)S(1)} %bitcast.224, s32[64]{0:T(128)S(1)} %copy-done.1, s32[22272]{0:T(1024)S(1)} %iota_bitcast_fusion), kind=kLoop, calls=%fused_computation.21 | loop fusion | flops 4276224 | bytes 8641792 | tf_op jit(solution)/shard_map/and | solution.py:48
  70.2 2.3 %fusion.101 = (f32[64,2]{0,1:T(2,128)S(1)}, f32[64,1,2,22272]{3,0,2,1:T(8,128)S(1)}) fusion(bf16[64,2,128]{2,0,1:T(8,128)(2,1)S(1)} %pad_maximum_fusion.2, bf16[22272,128,1]{1,0,2:T(8,128)(2,1)S(1)} %bitcast.221, pred[64,22272]{1,0:T(8,128)(4,1)S(1)} %fusion.6), kind=kOutput, calls=%fused_computation.189 | convolution fusion | flops 738361216 | bytes 18563584 | tf_op jit(solution)/shard_map/rkgd,tkd->rkgt/dot_general | solution.py:54
  72.5 2.3 %fusion.2 = f32[64,2]{0,1:T(2,128)S(1)} fusion(f32[64,1,2,22272]{3,0,2,1:T(8,128)S(1)} %get-tuple-element.44, f32[64,2]{0,1:T(2,128)S(1)} %fusion.84), kind=kLoop, calls=%fused_computation.16 | loop fusion | flops 5701504 | bytes 11404288 | tf_op jit(solution)/shard_map/reduce_sum | solution.py:65
  74.8 5.4 %fusion.30 = f32[64,1,2,128]{3,0,2,1:T(8,128)S(1)} fusion(bf16[22272,128,1]{1,0,2:T(8,128)(2,1)} %bitcast.228, f32[64,2]{0,1:T(2,128)S(1)} %get-tuple-element.30, f32[64,1,2,22272]{3,0,2,1:T(8,128)S(1)} %get-tuple-element.44, f32[64,2]{0,1:T(2,128)S(1)} %fusion.84, f32[64,128]{1,0:T(8,128)S(1)} %get-tuple-element.45, f32[64,2]{0,1:T(2,128)S(1)} %get-tuple-element.29), kind=kOutput, calls=%fused_computation.45 | convolution fusion | flops 738394112 | bytes 17204736 | tf_op jit(solution)/shard_map/rkgt,tkd->rkgd/dot_general | solution.py:71
  80.4 0.9 fusion.34
  81.2 0.2 copy.67
  81.4 0.4 constant_dynamic-slice_fusion.15
  81.8 1.7 %collective-permute-start = (f32[64,256]{1,0:T(8,128)S(1)}, f32[64,256]{1,0:T(8,128)S(1)}, u32[]{:S(2)}, u32[]{:S(2)}) collective-permute-start(f32[64,256]{1,0:T(8,128)S(1)} %bitcast.243), channel_id=1, source_target_pairs={{0,1},{1,2},{2,3},{3,4},{4,5},{5,6},{6,7},{7,0},{8,9},{9,10},{10,1... | collective-permute-start | bytes 196616 | tf_op jit(solution)/shard_map/ppermute | solution.py:82
  83.6 2.8 %collective-permute-start.2 = (f32[64,256]{1,0:T(8,128)S(1)}, f32[64,256]{1,0:T(8,128)S(1)}, u32[]{:S(2)}, u32[]{:S(2)}) collective-permute-start(f32[64,256]{1,0:T(8,128)S(1)} %bitcast.239), channel_id=1, source_target_pairs={{0,3},{1,4},{2,5},{3,6},{4,7},{5,0},{6,1},{7,2},{8,11},{9,12},{10,... | collective-permute-start | bytes 196616 | tf_op jit(solution)/shard_map/ppermute | solution.py:82
  86.3 0.6 collective-permute-start.3
  86.9 1.8 %collective-permute-start.4 = (f32[64,256]{1,0:T(8,128)S(1)}, f32[64,256]{1,0:T(8,128)S(1)}, u32[]{:S(2)}, u32[]{:S(2)}) collective-permute-start(f32[64,256]{1,0:T(8,128)S(1)} %bitcast.244), channel_id=1, source_target_pairs={{0,5},{1,6},{2,7},{3,0},{4,1},{5,2},{6,3},{7,4},{8,13},{9,14},{10,... | collective-permute-start | bytes 196616 | tf_op jit(solution)/shard_map/ppermute | solution.py:82
  88.8 0.8 collective-permute-start.5
  89.6 0.5 collective-permute-start.6
  90.1 2.1 %collective-permute-done.3 = f32[64,256]{1,0:T(8,128)S(1)} collective-permute-done((f32[64,256]{1,0:T(8,128)S(1)}, f32[64,256]{1,0:T(8,128)S(1)}, u32[]{:S(2)}, u32[]{:S(2)}) %collective-permute-start.3) | collective-permute-done | bytes 65568 | tf_op jit(solution)/shard_map/ppermute | solution.py:82
  92.2 0.7 collective-permute-done.4
  92.9 1.6 collective-permute-done.6
  94.5 12.6 %all_gather.13 = bf16[64,2048]{1,0:T(8,128)(2,1)S(1)} all-gather(bf16[64,256]{1,0:T(8,128)(2,1)S(1)} %fusion.69), channel_id=1, replica_groups=mesh['req'=16,'kv'=8] {'kv'}, dimensions={1}, use_global_device_ids=true | all-gather | bytes 294912 | tf_op jit(solution)/shard_map/all_gather | solution.py:179
  107.1 0.2 fusion.38
  107.3 26.9 %all-gather.3.cloned.1.call-done = bf16[2304,2048]{1,0:T(8,128)(2,1)} async-done(((bf16[144,2048]{1,0:T(8,128)(2,1)}), bf16[2304,2048]{1,0:T(8,128)(2,1)}) %all-gather.3.cloned.1.call-update) | async-done | bytes 9437200 | tf_op jit(solution)/shard_map/all_gather | solution.py:120
  134.2 2.9 %fusion.11 = f32[64,16,48]{0,2,1:T(8,128)S(1)} fusion(bf16[16,144,2048]{2,1,0:T(8,128)(2,1)} %bitcast.252, bf16[64,2048]{1,0:T(8,128)(2,1)S(1)} %all_gather.13, f32[2048]{0:T(1024)S(1)} %copy-done.11, f32[64]{0:T(128)S(1)} %add_rsqrt_fusion.1), kind=kOutput, calls=%fused_computation.27 | convolution fusion | flops 201850880 | bytes 3612928 | tf_op jit(solution)/shard_map/rd,sud->rsu/dot_general | solution.py:181
  137.2 5.2 %fusion.7 = f32[64,2048,1]{1,0,2:T(8,128)S(1)} fusion(bf16[16,144,2048]{2,1,0:T(8,128)(2,1)} %bitcast.253, f32[64,16,48]{0,2,1:T(8,128)S(1)} %fusion.11, bf16[64,2048]{1,0:T(8,128)(2,1)S(1)} %all_gather.13, f32[2048]{0:T(1024)S(1)} %copy-done.11, f32[64]{0:T(128)S(1)} %add_rsqrt_fusion.1), kind=kOutput, calls=%fused_computation.23 | convolution fusion | flops 403472384 | bytes 7282944 | tf_op jit(solution)/shard_map/rsu,suc->rc/dot_general | solution.py:184
  142.4 0.2 copy.68
  142.5 0.4 constant_dynamic-slice_fusion.7
  142.9 2.9 %collective-permute-start.10 = (f32[64,256]{1,0:T(8,128)S(1)}, f32[64,256]{1,0:T(8,128)S(1)}, u32[]{:S(2)}, u32[]{:S(2)}) collective-permute-start(f32[64,256]{1,0:T(8,128)S(1)} %bitcast.246), channel_id=1, source_target_pairs={{0,4},{1,5},{2,6},{3,7},{4,0},{5,1},{6,2},{7,3},{8,12},{9,13},{10,... | collective-permute-start | bytes 196616 | tf_op jit(solution)/shard_map/ppermute | solution.py:82
  145.9 1.8 %collective-permute-start.11 = (f32[64,256]{1,0:T(8,128)S(1)}, f32[64,256]{1,0:T(8,128)S(1)}, u32[]{:S(2)}, u32[]{:S(2)}) collective-permute-start(f32[64,256]{1,0:T(8,128)S(1)} %bitcast.242), channel_id=1, source_target_pairs={{0,5},{1,6},{2,7},{3,0},{4,1},{5,2},{6,3},{7,4},{8,13},{9,14},{10,... | collective-permute-start | bytes 196616 | tf_op jit(solution)/shard_map/ppermute | solution.py:82
  147.7 0.3 collective-permute-start.12
  148.0 1.4 collective-permute-start.13
  149.4 0.4 collective-permute-start.7
  149.8 1.5 collective-permute-start.8
  151.2 2.5 %collective-permute-start.9 = (f32[64,256]{1,0:T(8,128)S(1)}, f32[64,256]{1,0:T(8,128)S(1)}, u32[]{:S(2)}, u32[]{:S(2)}) collective-permute-start(f32[64,256]{1,0:T(8,128)S(1)} %bitcast.237), channel_id=1, source_target_pairs={{0,3},{1,4},{2,5},{3,6},{4,7},{5,0},{6,1},{7,2},{8,11},{9,12},{10,... | collective-permute-start | bytes 196616 | tf_op jit(solution)/shard_map/ppermute | solution.py:82
  153.7 4.7 %slice_bitcast_fusion = (bf16[16,512,128]{2,1,0:T(8,128)(2,1)}, bf16[16,512,128]{2,1,0:T(8,128)(2,1)}) fusion(bf16[2,16,512,128]{3,2,0,1:T(8,128)(2,1)} %all-to-all-done), kind=kLoop, calls=%fused_computation.29 | loop fusion | bytes 8388608 | tf_op jit(solution)/shard_map/squeeze | solution.py:168
  158.4 0.7 fusion.61
  (92 shorter events, 1.4 us)
Async XLA Ops:
  7.2 73.2 %copy-start = (bf16[256,2048]{1,0:T(8,128)(2,1)S(1)}, bf16[256,2048]{1,0:T(8,128)(2,1)}, u32[]{:S(2)}) copy-start(bf16[256,2048]{1,0:T(8,128)(2,1)} %param.27) | copy-start | bytes 3145732
  7.2 23.3 %copy-start.9 = (s32[2]{0:T(128)S(1)}, s32[2]{0:T(128)}, u32[]{:S(2)}) copy-start(s32[2]{0:T(128)} %constant.138) | copy-start | bytes 28
  7.2 22.3 %copy-start.1 = (s32[64]{0:T(128)S(1)}, s32[64]{0:T(128)}, u32[]{:S(2)}) copy-start(s32[64]{0:T(128)} %param.30) | copy-start | bytes 772
  7.2 21.9 %copy-start.6 = (f32[2048]{0:T(1024)S(1)}, f32[2048]{0:T(1024)}, u32[]{:S(2)}) copy-start(f32[2048]{0:T(1024)} %param.20) | copy-start | bytes 24580
  7.2 21.9 %copy-start.10 = (bf16[2048,128]{1,0:T(8,128)(2,1)S(1)}, bf16[2048,128]{1,0:T(8,128)(2,1)}, u32[]{:S(2)}) copy-start(bf16[2048,128]{1,0:T(8,128)(2,1)} %param.25) | copy-start | bytes 1572868
  7.2 22.3 %copy-start.7 = (f32[128]{0:T(128)S(1)}, f32[128]{0:T(128)}, u32[]{:S(2)}) copy-start(f32[128]{0:T(128)} %param.22) | copy-start | bytes 1540
  7.2 23.4 %copy-start.2 = (s32[64,32]{0,1:T(8,128)S(1)}, s32[64,32]{0,1:T(8,128)}, u32[]{:S(2)}) copy-start(s32[64,32]{0,1:T(8,128)} %param.31) | copy-start | bytes 24580
  7.2 127.0 %all-gather.3.cloned.1.call-start = ((), (), s32[]{:S(2)}) async-start(), calls=%async_computation.1 | async-start | bytes 10027008 | tf_op jit(solution)/shard_map/all_gather | solution.py:120
  52.0 7.0 %copy-start.4 = (bf16[2048,256]{1,0:T(8,128)(2,1)S(1)}, bf16[2048,256]{1,0:T(8,128)(2,1)}, u32[]{:S(2)}) copy-start(bf16[2048,256]{1,0:T(8,128)(2,1)} %param.23) | copy-start | bytes 3145732
  52.0 7.9 %copy-start.8 = (f32[128]{0:T(128)S(1)}, f32[128]{0:T(128)}, u32[]{:S(2)}) copy-start(f32[128]{0:T(128)} %param.21) | copy-start | bytes 1540
  52.0 101.7 %all-to-all-start = ((bf16[2,16,512,128]{3,2,0,1:T(8,128)(2,1)}), bf16[2,16,512,128]{3,2,0,1:T(8,128)(2,1)}, u32[]{:S(2)}, u32[]{:S(2)}) async-start(bf16[2,16,512,128]{3,2,0,1:T(8,128)(2,1)} %pad_maximum_fusion), calls=%async_computation | async-start | bytes 8388608 | tf_op jit(solution)/shard_map/all_to_all | solution.py:160
  62.4 7.8 %slice-start = ((s8[5701632]{0:T(1024)(128)(4,1)}), s8[4194304]{0:T(1024)(128)(4,1)S(1)}, s32[]{:S(2)}) async-start(s8[5701632]{0:T(1024)(128)(4,1)} %bitcast.219), calls=%async_computation.2 | async-start | bytes 8388608
  66.1 4.1 %slice-start.1 = ((s8[5701632]{0:T(1024)(128)(4,1)}), s8[1507328]{0:T(1024)(128)(4,1)S(1)}, s32[]{:S(2)}) async-start(s8[5701632]{0:T(1024)(128)(4,1)} %bitcast.219), calls=%async_computation.3 | async-start | bytes 3014656
  74.8 5.5 %copy-start.3 = (bf16[2048,256]{1,0:T(8,128)(2,1)S(1)}, bf16[2048,256]{1,0:T(8,128)(2,1)}, u32[]{:S(2)}) copy-start(bf16[2048,256]{1,0:T(8,128)(2,1)} %param.24) | copy-start | bytes 3145732
  80.3 14.2 %copy-start.5 = (bf16[64,256]{1,0:T(8,128)(2,1)S(1)}, bf16[64,256]{1,0:T(8,128)(2,1)}, u32[]{:S(2)}) copy-start(bf16[64,256]{1,0:T(8,128)(2,1)} %param.19) | copy-start | bytes 98308
  80.4 53.9 %copy-start.11 = (f32[2048]{0:T(1024)S(1)}, f32[2048]{0:T(1024)}, u32[]{:S(2)}) copy-start(f32[2048]{0:T(1024)} %param.34) | copy-start | bytes 24580
  81.8 6.9 %collective-permute-start = (f32[64,256]{1,0:T(8,128)S(1)}, f32[64,256]{1,0:T(8,128)S(1)}, u32[]{:S(2)}, u32[]{:S(2)}) collective-permute-start(f32[64,256]{1,0:T(8,128)S(1)} %bitcast.243), channel_id=1, source_target_pairs={{0,1},{1,2},{2,3},{3,4},{4,5},{5,6},{6,7},{7,0},{8,9},{9,10},{10,1... | collective-permute-start | bytes 196616 | tf_op jit(solution)/shard_map/ppermute | solution.py:82
  83.6 6.0 %collective-permute-start.1 = (f32[64,256]{1,0:T(8,128)S(1)}, f32[64,256]{1,0:T(8,128)S(1)}, u32[]{:S(2)}, u32[]{:S(2)}) collective-permute-start(f32[64,256]{1,0:T(8,128)S(1)} %bitcast.240), channel_id=1, source_target_pairs={{0,2},{1,3},{2,4},{3,5},{4,6},{5,7},{6,0},{7,1},{8,10},{9,11},{10,... | collective-permute-start | bytes 196616 | tf_op jit(solution)/shard_map/ppermute | solution.py:82
  83.6 6.5 %collective-permute-start.2 = (f32[64,256]{1,0:T(8,128)S(1)}, f32[64,256]{1,0:T(8,128)S(1)}, u32[]{:S(2)}, u32[]{:S(2)}) collective-permute-start(f32[64,256]{1,0:T(8,128)S(1)} %bitcast.239), channel_id=1, source_target_pairs={{0,3},{1,4},{2,5},{3,6},{4,7},{5,0},{6,1},{7,2},{8,11},{9,12},{10,... | collective-permute-start | bytes 196616 | tf_op jit(solution)/shard_map/ppermute | solution.py:82
  86.3 5.9 %collective-permute-start.3 = (f32[64,256]{1,0:T(8,128)S(1)}, f32[64,256]{1,0:T(8,128)S(1)}, u32[]{:S(2)}, u32[]{:S(2)}) collective-permute-start(f32[64,256]{1,0:T(8,128)S(1)} %bitcast.241), channel_id=1, source_target_pairs={{0,4},{1,5},{2,6},{3,7},{4,0},{5,1},{6,2},{7,3},{8,12},{9,13},{10,... | collective-permute-start | bytes 196616 | tf_op jit(solution)/shard_map/ppermute | solution.py:82
  86.9 6.0 %collective-permute-start.4 = (f32[64,256]{1,0:T(8,128)S(1)}, f32[64,256]{1,0:T(8,128)S(1)}, u32[]{:S(2)}, u32[]{:S(2)}) collective-permute-start(f32[64,256]{1,0:T(8,128)S(1)} %bitcast.244), channel_id=1, source_target_pairs={{0,5},{1,6},{2,7},{3,0},{4,1},{5,2},{6,3},{7,4},{8,13},{9,14},{10,... | collective-permute-start | bytes 196616 | tf_op jit(solution)/shard_map/ppermute | solution.py:82
  88.8 4.2 %collective-permute-start.5 = (f32[64,256]{1,0:T(8,128)S(1)}, f32[64,256]{1,0:T(8,128)S(1)}, u32[]{:S(2)}, u32[]{:S(2)}) collective-permute-start(f32[64,256]{1,0:T(8,128)S(1)} %bitcast.247), channel_id=1, source_target_pairs={{0,6},{1,7},{2,0},{3,1},{4,2},{5,3},{6,4},{7,5},{8,14},{9,15},{10,... | collective-permute-start | bytes 196616 | tf_op jit(solution)/shard_map/ppermute | solution.py:82
  89.6 4.9 %collective-permute-start.6 = (f32[64,256]{1,0:T(8,128)S(1)}, f32[64,256]{1,0:T(8,128)S(1)}, u32[]{:S(2)}, u32[]{:S(2)}) collective-permute-start(f32[64,256]{1,0:T(8,128)S(1)} %bitcast.245), channel_id=1, source_target_pairs={{0,7},{1,0},{2,1},{3,2},{4,3},{5,4},{6,5},{7,6},{8,15},{9,8},{10,9... | collective-permute-start | bytes 196616 | tf_op jit(solution)/shard_map/ppermute | solution.py:82
  142.9 6.8 %collective-permute-start.10 = (f32[64,256]{1,0:T(8,128)S(1)}, f32[64,256]{1,0:T(8,128)S(1)}, u32[]{:S(2)}, u32[]{:S(2)}) collective-permute-start(f32[64,256]{1,0:T(8,128)S(1)} %bitcast.246), channel_id=1, source_target_pairs={{0,4},{1,5},{2,6},{3,7},{4,0},{5,1},{6,2},{7,3},{8,12},{9,13},{10,... | collective-permute-start | bytes 196616 | tf_op jit(solution)/shard_map/ppermute | solution.py:82
  145.9 5.3 %collective-permute-start.11 = (f32[64,256]{1,0:T(8,128)S(1)}, f32[64,256]{1,0:T(8,128)S(1)}, u32[]{:S(2)}, u32[]{:S(2)}) collective-permute-start(f32[64,256]{1,0:T(8,128)S(1)} %bitcast.242), channel_id=1, source_target_pairs={{0,5},{1,6},{2,7},{3,0},{4,1},{5,2},{6,3},{7,4},{8,13},{9,14},{10,... | collective-permute-start | bytes 196616 | tf_op jit(solution)/shard_map/ppermute | solution.py:82
  147.7 10.7 %collective-permute-start.12 = (f32[64,256]{1,0:T(8,128)S(1)}, f32[64,256]{1,0:T(8,128)S(1)}, u32[]{:S(2)}, u32[]{:S(2)}) collective-permute-start(f32[64,256]{1,0:T(8,128)S(1)} %bitcast.234), channel_id=1, source_target_pairs={{0,6},{1,7},{2,0},{3,1},{4,2},{5,3},{6,4},{7,5},{8,14},{9,15},{10,... | collective-permute-start | bytes 196616 | tf_op jit(solution)/shard_map/ppermute | solution.py:82
  148.0 10.4 %collective-permute-start.13 = (f32[64,256]{1,0:T(8,128)S(1)}, f32[64,256]{1,0:T(8,128)S(1)}, u32[]{:S(2)}, u32[]{:S(2)}) collective-permute-start(f32[64,256]{1,0:T(8,128)S(1)} %bitcast.235), channel_id=1, source_target_pairs={{0,7},{1,0},{2,1},{3,2},{4,3},{5,4},{6,5},{7,6},{8,15},{9,8},{10,9... | collective-permute-start | bytes 196616 | tf_op jit(solution)/shard_map/ppermute | solution.py:82
  149.4 9.0 %collective-permute-start.7 = (f32[64,256]{1,0:T(8,128)S(1)}, f32[64,256]{1,0:T(8,128)S(1)}, u32[]{:S(2)}, u32[]{:S(2)}) collective-permute-start(f32[64,256]{1,0:T(8,128)S(1)} %bitcast.236), channel_id=1, source_target_pairs={{0,1},{1,2},{2,3},{3,4},{4,5},{5,6},{6,7},{7,0},{8,9},{9,10},{10,1... | collective-permute-start | bytes 196616 | tf_op jit(solution)/shard_map/ppermute | solution.py:82
  149.8 8.6 %collective-permute-start.8 = (f32[64,256]{1,0:T(8,128)S(1)}, f32[64,256]{1,0:T(8,128)S(1)}, u32[]{:S(2)}, u32[]{:S(2)}) collective-permute-start(f32[64,256]{1,0:T(8,128)S(1)} %bitcast.238), channel_id=1, source_target_pairs={{0,2},{1,3},{2,4},{3,5},{4,6},{5,7},{6,0},{7,1},{8,10},{9,11},{10,... | collective-permute-start | bytes 196616 | tf_op jit(solution)/shard_map/ppermute | solution.py:82
  151.2 7.2 %collective-permute-start.9 = (f32[64,256]{1,0:T(8,128)S(1)}, f32[64,256]{1,0:T(8,128)S(1)}, u32[]{:S(2)}, u32[]{:S(2)}) collective-permute-start(f32[64,256]{1,0:T(8,128)S(1)} %bitcast.237), channel_id=1, source_target_pairs={{0,3},{1,4},{2,5},{3,6},{4,7},{5,0},{6,1},{7,2},{8,11},{9,12},{10,... | collective-permute-start | bytes 196616 | tf_op jit(solution)/shard_map/ppermute | solution.py:82
Sparse Core Ops, SparseCore 0:
  10.8 123.3 all-gather.2

commit v9 on v7

--- a/solution.py
+++ b/solution.py
@@ -71,13 +71,6 @@
     return start_sum + jnp.einsum(
         "rkgt,tkd->rkgd", weights, values, preferred_element_type=jnp.float32
     )
-
-
-def reduce_to_slice(partial, kv_count, slice_width):
-    rows = partial.shape[0]
-    pieces = partial.reshape(rows, kv_count, slice_width).transpose(1, 0, 2)
-    arrived = lax.all_to_all(pieces, "kv", 0, 0, tiled=True)
-    return jnp.sum(arrived, axis=0)
 
 
 def reduce_by_permutes(partial, kv_count, slice_width):
@@ -125,11 +118,18 @@
     model_width = mlp_gain.shape[0]
     unit_count = w_gate.shape[1]
     stacked = lax.all_gather(
-        jnp.concatenate([w_gate.T, w_up.T, w_down.T], axis=0), "req", axis=0, tiled=False
+        jnp.concatenate([w_gate.T, w_up.T], axis=0), "req", axis=0, tiled=False
+    )
+    req_groups = lax.axis_size("req")
+    down_w = lax.all_to_all(
+        jnp.broadcast_to(w_down.T[None], (req_groups,) + w_down.T.shape),
+        "req",
+        0,
+        0,
+        tiled=True,
     )
     gate_w = stacked[:, :unit_count, :]
-    up_w = stacked[:, unit_count : 2 * unit_count, :]
-    down_w = stacked[:, 2 * unit_count :, :]
+    up_w = stacked[:, unit_count:, :]
     whole_rows = lax.all_gather(hidden, "kv", axis=1, tiled=True)
     normed = rms_norm(whole_rows, attn_gain).astype(jnp.bfloat16)
     query_raw = jnp.dot(normed, w_q, preferred_element_type=jnp.float32).reshape(
@@ -181,7 +181,7 @@
     kv_count = lax.axis_size("kv")
     slice_width = model_width // kv_count
     mid_slice = (
-        hidden.astype(jnp.float32) + reduce_to_slice(head_terms, kv_count, slice_width)
+        hidden.astype(jnp.float32) + reduce_by_permutes(head_terms, kv_count, slice_width)
     ).astype(jnp.bfloat16)
     mid_stream = lax.all_gather(mid_slice, "kv", axis=1, tiled=True)
     normed_mlp = rms_norm(mid_stream, mlp_gain).astype(jnp.bfloat16)

time: 161 us -> 185 us (1.15)
  starting transfers between devices: 20 us -> 31.6 us
  local copies, waits for them, and re-layouts: 24.8 us -> 30.4 us
  waiting for transfers between devices: 31.8 us -> 36.9 us
  matrix products: 21.1 us -> 23.6 us
    all_gather x1, waiting for transfers between devices: 0.02 us -> 14.9 us  [layer_body(): lax.all_gather(jnp.concatenate([w_gate.T, w_up.T], axis=0), 'req', axis=0...]
    all_to_all x1, waiting for transfers between devices: 31.8 us -> 18.8 us  [layer_body(): lax.all_to_all(jnp.stack([place_cache(k_pool, new_keys), place_cache(v_po...]
    ppermute x7 -> x14, starting transfers between devices: 8.1 us -> 17 us  [reduce_by_permutes(): lax.ppermute(pieces[(me + shift) % kv_count], 'kv', [(k, (k + shift) % kv...]
    ppermute x7 -> x14, waiting for transfers between devices: 0.02 us -> 3.1 us  [reduce_by_permutes(): lax.ppermute(pieces[(me + shift) % kv_count], 'kv', [(k, (k + shift) % kv...]
    broadcast_in_dim x0 -> x1, local copies, waits for them, and re-layouts: none -> 2.98 us  [layer_body(): jnp.broadcast_to(w_down.T[None], (req_groups,) + w_down.T.shape)]
    all_to_all x1, starting transfers between devices: 4.53 us -> 7.37 us  [layer_body(): lax.all_to_all(jnp.broadcast_to(w_down.T[None], (req_groups,) + w_down.T....]
    dot_general x1, matrix products: 5.29 us -> 8.05 us  [attend_pool(): jnp.einsum('rkgt,tkd->rkgd', weights, values, preferred_element_type=jnp....]
    unnamed x37 -> x47, local copies, waits for them, and re-layouts: 0.36 us -> 2.53 us
  transfers between devices with their start and end apart: 10 -> 17, of which waited for: 1 -> 5; matrix products, arithmetic and copies ran while one was open for 40% -> 38% of each run, Pallas kernels for 0% -> 0%
where the time goes in v9:
time: 185 us; the launch traced here: 184 us
  waiting for transfers between devices  36.9 us (20%)
  starting transfers between devices  31.6 us (17%)
  local copies, waits for them, and re-layouts  30.4 us (16%)
  blocking collectives  26.6 us (14%)
  matrix products  23.6 us (13%)
  other arithmetic  20.6 us (11%)
  between operations  14.8 us (8%)
    all_to_all x1, waiting for transfers between devices, layer_body(): lax.all_to_all(jnp.stack([place_cache(k_pool, new_keys), place_cache(v_po...  18.8 us
    ppermute x14, starting transfers between devices, reduce_by_permutes(): lax.ppermute(pieces[(me + shift) % kv_count], 'kv', [(k, (k + shift) % kv...  17 us
    all_gather x1, waiting for transfers between devices, layer_body(): lax.all_gather(jnp.concatenate([w_gate.T, w_up.T], axis=0), 'req', axis=0...  14.9 us
    all_gather x1, blocking collectives, layer_body(): whole_rows = lax.all_gather(hidden, 'kv', axis=1, tiled=True)  13.7 us
    all_gather x1, blocking collectives, layer_body(): mid_stream = lax.all_gather(mid_slice, 'kv', axis=1, tiled=True)  12.8 us
    gather x2, local copies, waits for them, and re-layouts, place_cache(): cached = pool[moved_pages].reshape(mig_count, slot_count, channels)  9.54 us
    dot_general x1, matrix products, attend_pool(): jnp.einsum('rkgt,tkd->rkgd', weights, values, preferred_element_type=jnp....  8.05 us
    all_to_all x1, starting transfers between devices, layer_body(): lax.all_to_all(jnp.broadcast_to(w_down.T[None], (req_groups,) + w_down.T....  7.37 us
  transfers between devices with their start and end apart: 17, of which 5 were waited for; matrix products, arithmetic and copies ran while one was open for 38% of the time, Pallas kernels for 0%

profile of v9, /device:TPU:52, one launch (start us, length us, event | category | flops | bytes accessed | tf_op | source)
XLA Modules:
  0.0 184.5 jit_solution(584810390729265647)
XLA Ops:
  7.2 1.9 %pad_maximum_fusion.1 = bf16[96,2048]{1,0:T(8,128)(2,1)} fusion(bf16[48,2048]{1,0:T(8,128)(2,1)} %bitcast.231, bf16[48,2048]{1,0:T(8,128)(2,1)} %bitcast.232), kind=kLoop, calls=%fused_computation.58 | loop fusion | flops 786432 | bytes 786432 | tf_op jit(solution)/shard_map/concatenate | solution.py:121
  9.2 3.0 %broadcast_in_dim.72 = bf16[16,48,2048]{2,1,0:T(8,128)(2,1)} broadcast(bf16[48,2048]{1,0:T(8,128)(2,1)} %bitcast.230), dimensions={1,2} | broadcast | bytes 3342336 | tf_op jit(solution)/shard_map/broadcast_in_dim | solution.py:125
  12.2 7.4 %all-to-all-start = ((bf16[16,48,2048]{2,1,0:T(8,128)(2,1)}), bf16[16,48,2048]{2,1,0:T(8,128)(2,1)}, u32[]{:S(2)}, u32[]{:S(2)}) async-start(bf16[16,48,2048]{2,1,0:T(8,128)(2,1)} %broadcast_in_dim.72), calls=%async_computation | async-start | bytes 6291456 | tf_op jit(solution)/shard_map/all_to_all | solution.py:124
  19.7 13.7 %all_gather.12 = bf16[64,2048]{1,0:T(8,128)(2,1)S(1)} all-gather(bf16[64,256]{1,0:T(8,128)(2,1)S(1)} %copy-done.7), channel_id=1, replica_groups=mesh['req'=16,'kv'=8] {'kv'}, dimensions={1}, use_global_device_ids=true | all-gather | bytes 294912 | tf_op jit(solution)/shard_map/all_gather | solution.py:133
  33.5 0.2 fusion.34
  33.7 0.4 multiply_reduce_fusion.1
  34.0 0.2 multiply_cosine_fusion.1
  34.3 0.2 fusion.82
  34.7 0.3 fusion.96
  35.1 0.1 multiply_reduce_fusion
  35.3 0.1 fusion.52
  35.4 0.1 subtract_convert_fusion
  35.5 0.1 pad_maximum_fusion.2
  35.6 0.2 fusion.78
  36.1 0.6 scatter_custom_fusion
  36.8 0.7 gather_fusion
  37.5 0.7 gather_fusion.1
  38.1 0.6 gather_fusion.3
  38.8 0.7 gather_fusion.8
  39.5 0.7 gather_fusion.9
  40.1 0.7 gather_fusion.6
  40.8 0.7 gather_fusion.7
  41.6 0.1 reshape.502
  41.7 4.8 %gather_fusion.2 = bf16[64,128,128]{2,1,0:T(8,128)(2,1)} fusion(bf16[174,128,128]{2,1,0:T(8,128)(2,1)} %param.28, s32[1024]{0:T(1024)S(1)} %pad_clamp_fusion), kind=kCustom, calls=%fused_computation.2 | custom fusion | bytes 4194560 | tf_op jit(solution)/shard_map/gather | solution.py:161
  46.5 4.7 %gather_fusion.4 = bf16[64,128,128]{2,1,0:T(8,128)(2,1)} fusion(bf16[174,128,128]{2,1,0:T(8,128)(2,1)} %param.29, s32[1024]{0:T(1024)S(1)} %pad_clamp_fusion), kind=kCustom, calls=%fused_computation.4 | custom fusion | bytes 4194560 | tf_op jit(solution)/shard_map/gather | solution.py:161
  51.2 0.7 fusion.12
  52.0 1.1 select_reduce_fusion
  53.0 1.6 add.268
  54.7 2.1 %and.67 = pred[64,174,128]{2,1,0:T(8,128)(4,1)S(1)} broadcast(pred[64,174]{1,0:T(8,128)(4,1)S(1)} %fusion.12), dimensions={0,1} | broadcast | bytes 1436544 | tf_op jit(solution)/shard_map/and | solution.py:48
  56.8 3.9 %fusion.6 = pred[64,22272]{1,0:T(8,128)(4,1)S(1)} fusion(s32[8,8,174,128]{3,2,1,0:T(8,128)S(1)} %bitcast.219, pred[8,8,174,128]{3,2,1,0:T(8,128)(4,1)S(1)} %bitcast.223, s32[64]{0:T(128)S(1)} %copy-done.1, s32[22272]{0:T(1024)S(1)} %iota_bitcast_fusion), kind=kLoop, calls=%fused_computation.21 | loop fusion | flops 4276224 | bytes 8641792 | tf_op jit(solution)/shard_map/and | solution.py:48
  60.7 0.3 fusion.101
  61.0 0.6 gather_fusion.5
  61.6 6.0 %select_select_fusion.1 = (bf16[16,1,512,128]{3,2,1,0:T(8,128)(2,1)S(1)}, bf16[16,1,512,128]{3,2,1,0:T(8,128)(2,1)S(1)}) fusion(bf16[16,1,512,128]{3,2,1,0:T(8,128)(2,1)} %bitcast.221, pred[16,512]{1,0:T(8,128)(4,1)S(1)} %get-tuple-element.36, pred[16,512]{1,0:T(8,128)(4,1)S(1)} %get-tuple-element.35, bf16[16,128]{1,0:T(8,128)(2,1)S(1)} %gather_fusion.3, ...), kind=kLoop, calls=%fused_computation.30 | loop fusion | flops 4194304 | bytes 8413184 | tf_op jit(solution)/shard_map/jit(_where)/select_n | solution.py:163
  67.6 2.4 %pad_maximum_fusion = bf16[16,2,512,128]{3,2,1,0:T(8,128)(2,1)} fusion(bf16[16,1,512,128]{3,2,1,0:T(8,128)(2,1)S(1)} %get-tuple-element.28, bf16[16,1,512,128]{3,2,1,0:T(8,128)(2,1)S(1)} %get-tuple-element.27), kind=kLoop, calls=%fused_computation.22 | loop fusion | flops 2097152 | bytes 8388608 | tf_op jit(solution)/shard_map/stack | solution.py:168
  70.0 4.2 %fusion.100 = (f32[64,2]{0,1:T(2,128)S(1)}, f32[64,1,2,22272]{3,0,2,1:T(8,128)S(1)}) fusion(bf16[64,2,128]{2,0,1:T(8,128)(2,1)S(1)} %pad_maximum_fusion.2, bf16[22272,128,1]{1,0,2:T(8,128)(2,1)} %bitcast.220, pred[64,22272]{1,0:T(8,128)(4,1)S(1)} %fusion.6), kind=kOutput, calls=%fused_computation.188 | convolution fusion | flops 738361216 | bytes 18563584 | tf_op jit(solution)/shard_map/rkgd,tkd->rkgt/dot_general | solution.py:54
  74.2 2.3 %fusion.2 = f32[64,2]{0,1:T(2,128)S(1)} fusion(f32[64,1,2,22272]{3,0,2,1:T(8,128)S(1)} %get-tuple-element.44, f32[64,2]{0,1:T(2,128)S(1)} %fusion.83), kind=kLoop, calls=%fused_computation.16 | loop fusion | flops 5701504 | bytes 11404288 | tf_op jit(solution)/shard_map/reduce_sum | solution.py:65
  76.5 2.0 %copy-done.4 = f32[64,1,2,22272]{3,0,2,1:T(8,128)} copy-done((f32[64,1,2,22272]{3,0,2,1:T(8,128)}, f32[64,1,2,22272]{3,0,2,1:T(8,128)S(1)}, u32[]{:S(2)}) %copy-start.4) | copy-done | bytes 11403288
  78.5 7.2 %all-to-all-start.1 = ((bf16[16,2,512,128]{3,2,1,0:T(8,128)(2,1)}), bf16[16,2,512,128]{3,2,1,0:T(8,128)(2,1)}, u32[]{:S(2)}, u32[]{:S(2)}) async-start(bf16[16,2,512,128]{3,2,1,0:T(8,128)(2,1)} %pad_maximum_fusion), calls=%async_computation.1 | async-start | bytes 8388608 | tf_op jit(solution)/shard_map/all_to_all | solution.py:167
  85.7 8.0 %fusion.29 = f32[64,1,2,128]{3,0,2,1:T(8,128)S(1)} fusion(bf16[22272,128,1]{1,0,2:T(8,128)(2,1)} %bitcast.227, f32[64,2]{0,1:T(2,128)S(1)} %get-tuple-element.30, f32[64,1,2,22272]{3,0,2,1:T(8,128)} %copy-done.4, f32[64,2]{0,1:T(2,128)S(1)} %fusion.83, f32[64,128]{1,0:T(8,128)S(1)} %get-tuple-element.45, f32[64,2]{0,1:T(2,128)S(1)} %get-tuple-element.29), kind=kOutput, calls=%fused_computation.44 | convolution fusion | flops 738394112 | bytes 17204736 | tf_op jit(solution)/shard_map/rkgt,tkd->rkgd/dot_general | solution.py:71
  93.9 2.1 %fusion.33 = f32[64,2048]{1,0:T(8,128)S(1)} fusion(bf16[256,2048]{1,0:T(8,128)(2,1)S(1)} %copy-done, bf16[2048,256]{1,0:T(8,128)(2,1)} %param.24, f32[8,8,2,128]{3,2,1,0:T(2,128)S(1)} %bitcast.229, bf16[64,2048]{1,0:T(8,128)(2,1)S(1)} %all_gather.12, f32[2048]{0:T(1024)S(1)} %copy-done.8, f32[64]{0:T(128)S(1)} %add_rsqrt_fusion.3), kind=kOutput, calls=%fused_computation.46 | convolution fusion | flops 134823936 | bytes 2957568 | tf_op jit(solution)/shard_map/dot_general | solution.py:180
  96.0 0.2 copy.67
  96.2 0.4 constant_dynamic-slice_fusion.15
  96.7 2.3 %collective-permute-start.2 = (f32[64,256]{1,0:T(8,128)S(1)}, f32[64,256]{1,0:T(8,128)S(1)}, u32[]{:S(2)}, u32[]{:S(2)}) collective-permute-start(f32[64,256]{1,0:T(8,128)S(1)} %bitcast.238), channel_id=1, source_target_pairs={{0,3},{1,4},{2,5},{3,6},{4,7},{5,0},{6,1},{7,2},{8,11},{9,12},{10,... | collective-permute-start | bytes 196616 | tf_op jit(solution)/shard_map/ppermute | solution.py:82
  99.1 1.4 collective-permute-start.3
  100.5 1.6 collective-permute-start.4
  102.2 2.3 %collective-permute-start.5 = (f32[64,256]{1,0:T(8,128)S(1)}, f32[64,256]{1,0:T(8,128)S(1)}, u32[]{:S(2)}, u32[]{:S(2)}) collective-permute-start(f32[64,256]{1,0:T(8,128)S(1)} %bitcast.246), channel_id=1, source_target_pairs={{0,6},{1,7},{2,0},{3,1},{4,2},{5,3},{6,4},{7,5},{8,14},{9,15},{10,... | collective-permute-start | bytes 196616 | tf_op jit(solution)/shard_map/ppermute | solution.py:82
  104.5 0.6 collective-permute-done.3
  105.1 0.8 collective-permute-done.4
  105.9 1.6 collective-permute-done.5
  107.6 12.8 %all_gather.13 = bf16[64,2048]{1,0:T(8,128)(2,1)S(1)} all-gather(bf16[64,256]{1,0:T(8,128)(2,1)S(1)} %fusion.68), channel_id=1, replica_groups=mesh['req'=16,'kv'=8] {'kv'}, dimensions={1}, use_global_device_ids=true | all-gather | bytes 294912 | tf_op jit(solution)/shard_map/all_gather | solution.py:186
  120.4 0.2 fusion.37
  120.6 14.9 %all-gather.3.cloned.1.call-done = bf16[1536,2048]{1,0:T(8,128)(2,1)} async-done(((bf16[96,2048]{1,0:T(8,128)(2,1)}), bf16[1536,2048]{1,0:T(8,128)(2,1)}) %all-gather.3.cloned.1.call-update) | async-done | bytes 6291472 | tf_op jit(solution)/shard_map/all_gather | solution.py:120
  135.5 2.9 %fusion.9 = f32[64,16,48]{0,2,1:T(8,128)S(1)} fusion(bf16[16,96,2048]{2,1,0:T(8,128)(2,1)} %bitcast.251, bf16[64,2048]{1,0:T(8,128)(2,1)S(1)} %all_gather.13, f32[2048]{0:T(1024)S(1)} %copy-done.13, f32[64]{0:T(128)S(1)} %add_rsqrt_fusion.1), kind=kOutput, calls=%fused_computation.25 | convolution fusion | flops 201850880 | bytes 3612928 | tf_op jit(solution)/shard_map/rd,sud->rsu/dot_general | solution.py:188
  138.4 5.2 %fusion.20 = f32[64,2048,1]{1,0,2:T(8,128)S(1)} fusion(bf16[16,48,2048]{2,1,0:T(8,128)(2,1)} %all-to-all-done, bf16[16,96,2048]{2,1,0:T(8,128)(2,1)} %bitcast.252, f32[64,16,48]{0,2,1:T(8,128)S(1)} %fusion.9, bf16[64,2048]{1,0:T(8,128)(2,1)S(1)} %all_gather.13, f32[2048]{0:T(1024)S(1)} %copy-done.13, f32[64]{0:T(128)S(1)} %add_rsqrt_fusion.1), kind=kOutput, calls=%fused_computation.37 | convolution fusion | flops 403472384 | bytes 7282944 | tf_op jit(solution)/shard_map/rsu,suc->rc/dot_general | solution.py:191
  143.6 0.2 copy.68
  143.8 0.4 constant_dynamic-slice_fusion.7
  144.2 2.5 %collective-permute-start.10 = (f32[64,256]{1,0:T(8,128)S(1)}, f32[64,256]{1,0:T(8,128)S(1)}, u32[]{:S(2)}, u32[]{:S(2)}) collective-permute-start(f32[64,256]{1,0:T(8,128)S(1)} %bitcast.245), channel_id=1, source_target_pairs={{0,4},{1,5},{2,6},{3,7},{4,0},{5,1},{6,2},{7,3},{8,12},{9,13},{10,... | collective-permute-start | bytes 196616 | tf_op jit(solution)/shard_map/ppermute | solution.py:82
  146.8 2.9 %collective-permute-start.12 = (f32[64,256]{1,0:T(8,128)S(1)}, f32[64,256]{1,0:T(8,128)S(1)}, u32[]{:S(2)}, u32[]{:S(2)}) collective-permute-start(f32[64,256]{1,0:T(8,128)S(1)} %bitcast.233), channel_id=1, source_target_pairs={{0,6},{1,7},{2,0},{3,1},{4,2},{5,3},{6,4},{7,5},{8,14},{9,15},{10,... | collective-permute-start | bytes 196616 | tf_op jit(solution)/shard_map/ppermute | solution.py:82
  149.7 0.5 collective-permute-start.7
  150.2 3.1 %collective-permute-start.8 = (f32[64,256]{1,0:T(8,128)S(1)}, f32[64,256]{1,0:T(8,128)S(1)}, u32[]{:S(2)}, u32[]{:S(2)}) collective-permute-start(f32[64,256]{1,0:T(8,128)S(1)} %bitcast.237), channel_id=1, source_target_pairs={{0,2},{1,3},{2,4},{3,5},{4,6},{5,7},{6,0},{7,1},{8,10},{9,11},{10,... | collective-permute-start | bytes 196616 | tf_op jit(solution)/shard_map/ppermute | solution.py:82
  153.3 0.1 collective-permute-start.9
  153.4 18.8 %all-to-all-done.1 = bf16[16,2,512,128]{3,2,1,0:T(8,128)(2,1)} async-done(((bf16[16,2,512,128]{3,2,1,0:T(8,128)(2,1)}), bf16[16,2,512,128]{3,2,1,0:T(8,128)(2,1)}, u32[]{:S(2)}, u32[]{:S(2)}) %all-to-all-start.1) | async-done | bytes 4194336 | tf_op jit(solution)/shard_map/all_to_all | solution.py:167
  172.3 4.7 %slice_bitcast_fusion = (bf16[16,512,128]{2,1,0:T(8,128)(2,1)}, bf16[16,512,128]{2,1,0:T(8,128)(2,1)}) fusion(bf16[16,2,512,128]{3,2,1,0:T(8,128)(2,1)} %all-to-all-done.1), kind=kLoop, calls=%fused_computation.27 | loop fusion | bytes 8388608 | tf_op jit(solution)/shard_map/squeeze | solution.py:175
  177.0 0.7 fusion.60
  (96 shorter events, 1.4 us)
Async XLA Ops:
  7.2 86.7 %copy-start = (bf16[256,2048]{1,0:T(8,128)(2,1)S(1)}, bf16[256,2048]{1,0:T(8,128)(2,1)}, u32[]{:S(2)}) copy-start(bf16[256,2048]{1,0:T(8,128)(2,1)} %param.27) | copy-start | bytes 3145732
  7.2 128.3 %all-gather.3.cloned.1.call-start = ((), (), s32[]{:S(2)}) async-start(), calls=%async_computation.2 | async-start | bytes 6684672 | tf_op jit(solution)/shard_map/all_gather | solution.py:120
  12.1 7.6 %copy-start.7 = (bf16[64,256]{1,0:T(8,128)(2,1)S(1)}, bf16[64,256]{1,0:T(8,128)(2,1)}, u32[]{:S(2)}) copy-start(bf16[64,256]{1,0:T(8,128)(2,1)} %param.19) | copy-start | bytes 98308
  12.1 21.5 %copy-start.1 = (s32[64]{0:T(128)S(1)}, s32[64]{0:T(128)}, u32[]{:S(2)}) copy-start(s32[64]{0:T(128)} %param.30) | copy-start | bytes 772
  12.1 21.5 %copy-start.8 = (f32[2048]{0:T(1024)S(1)}, f32[2048]{0:T(1024)}, u32[]{:S(2)}) copy-start(f32[2048]{0:T(1024)} %param.20) | copy-start | bytes 24580
  12.1 21.5 %copy-start.12 = (bf16[2048,128]{1,0:T(8,128)(2,1)S(1)}, bf16[2048,128]{1,0:T(8,128)(2,1)}, u32[]{:S(2)}) copy-start(bf16[2048,128]{1,0:T(8,128)(2,1)} %param.25) | copy-start | bytes 1572868
  12.1 22.1 %copy-start.9 = (f32[128]{0:T(128)S(1)}, f32[128]{0:T(128)}, u32[]{:S(2)}) copy-start(f32[128]{0:T(128)} %param.22) | copy-start | bytes 1540
  12.2 22.6 %copy-start.5 = (bf16[2048,256]{1,0:T(8,128)(2,1)S(1)}, bf16[2048,256]{1,0:T(8,128)(2,1)}, u32[]{:S(2)}) copy-start(bf16[2048,256]{1,0:T(8,128)(2,1)} %param.23) | copy-start | bytes 3145732
  12.2 66.3 %all-to-all-start = ((bf16[16,48,2048]{2,1,0:T(8,128)(2,1)}), bf16[16,48,2048]{2,1,0:T(8,128)(2,1)}, u32[]{:S(2)}, u32[]{:S(2)}) async-start(bf16[16,48,2048]{2,1,0:T(8,128)(2,1)} %broadcast_in_dim.72), calls=%async_computation | async-start | bytes 6291456 | tf_op jit(solution)/shard_map/all_to_all | solution.py:124
  19.5 15.8 %copy-start.10 = (f32[128]{0:T(128)S(1)}, f32[128]{0:T(128)}, u32[]{:S(2)}) copy-start(f32[128]{0:T(128)} %param.21) | copy-start | bytes 1540
  19.5 16.4 %copy-start.3 = (s32[64,32]{0,1:T(8,128)S(1)}, s32[64,32]{0,1:T(8,128)}, u32[]{:S(2)}) copy-start(s32[64,32]{0,1:T(8,128)} %param.31) | copy-start | bytes 24580
  19.6 16.5 %copy-start.14 = (s32[1,16]{1,0:T(1,128)S(1)}, s32[1,16]{1,0:T(1,128)}, u32[]{:S(2)}) copy-start(s32[1,16]{1,0:T(1,128)} %param.33) | copy-start | bytes 196
  19.6 17.2 %copy-start.2 = (s32[1,16]{1,0:T(1,128)S(1)}, s32[1,16]{1,0:T(1,128)}, u32[]{:S(2)}) copy-start(s32[1,16]{1,0:T(1,128)} %param.32) | copy-start | bytes 196
  19.6 19.1 %copy-start.11 = (s32[2]{0:T(128)S(1)}, s32[2]{0:T(128)}, u32[]{:S(2)}) copy-start(s32[2]{0:T(128)} %constant.138) | copy-start | bytes 28
  56.8 3.9 %copy-start.6 = (bf16[2048,128]{1,0:T(8,128)(2,1)S(1)}, bf16[2048,128]{1,0:T(8,128)(2,1)}, u32[]{:S(2)}) copy-start(bf16[2048,128]{1,0:T(8,128)(2,1)} %param.26) | copy-start | bytes 1572868
  74.2 4.3 %copy-start.4 = (f32[64,1,2,22272]{3,0,2,1:T(8,128)}, f32[64,1,2,22272]{3,0,2,1:T(8,128)S(1)}, u32[]{:S(2)}) copy-start(f32[64,1,2,22272]{3,0,2,1:T(8,128)S(1)} %get-tuple-element.44) | copy-start | bytes 34209796
  78.5 93.8 %all-to-all-start.1 = ((bf16[16,2,512,128]{3,2,1,0:T(8,128)(2,1)}), bf16[16,2,512,128]{3,2,1,0:T(8,128)(2,1)}, u32[]{:S(2)}, u32[]{:S(2)}) async-start(bf16[16,2,512,128]{3,2,1,0:T(8,128)(2,1)} %pad_maximum_fusion), calls=%async_computation.1 | async-start | bytes 8388608 | tf_op jit(solution)/shard_map/all_to_all | solution.py:167
  93.9 41.6 %copy-start.13 = (f32[2048]{0:T(1024)S(1)}, f32[2048]{0:T(1024)}, u32[]{:S(2)}) copy-start(f32[2048]{0:T(1024)} %param.34) | copy-start | bytes 24580
  96.6 5.6 %collective-permute-start = (f32[64,256]{1,0:T(8,128)S(1)}, f32[64,256]{1,0:T(8,128)S(1)}, u32[]{:S(2)}, u32[]{:S(2)}) collective-permute-start(f32[64,256]{1,0:T(8,128)S(1)} %bitcast.242), channel_id=1, source_target_pairs={{0,1},{1,2},{2,3},{3,4},{4,5},{5,6},{6,7},{7,0},{8,9},{9,10},{10,1... | collective-permute-start | bytes 196616 | tf_op jit(solution)/shard_map/ppermute | solution.py:82
  96.6 7.8 %collective-permute-start.1 = (f32[64,256]{1,0:T(8,128)S(1)}, f32[64,256]{1,0:T(8,128)S(1)}, u32[]{:S(2)}, u32[]{:S(2)}) collective-permute-start(f32[64,256]{1,0:T(8,128)S(1)} %bitcast.239), channel_id=1, source_target_pairs={{0,2},{1,3},{2,4},{3,5},{4,6},{5,7},{6,0},{7,1},{8,10},{9,11},{10,... | collective-permute-start | bytes 196616 | tf_op jit(solution)/shard_map/ppermute | solution.py:82
  96.7 7.7 %collective-permute-start.2 = (f32[64,256]{1,0:T(8,128)S(1)}, f32[64,256]{1,0:T(8,128)S(1)}, u32[]{:S(2)}, u32[]{:S(2)}) collective-permute-start(f32[64,256]{1,0:T(8,128)S(1)} %bitcast.238), channel_id=1, source_target_pairs={{0,3},{1,4},{2,5},{3,6},{4,7},{5,0},{6,1},{7,2},{8,11},{9,12},{10,... | collective-permute-start | bytes 196616 | tf_op jit(solution)/shard_map/ppermute | solution.py:82
  99.1 6.0 %collective-permute-start.3 = (f32[64,256]{1,0:T(8,128)S(1)}, f32[64,256]{1,0:T(8,128)S(1)}, u32[]{:S(2)}, u32[]{:S(2)}) collective-permute-start(f32[64,256]{1,0:T(8,128)S(1)} %bitcast.240), channel_id=1, source_target_pairs={{0,4},{1,5},{2,6},{3,7},{4,0},{5,1},{6,2},{7,3},{8,12},{9,13},{10,... | collective-permute-start | bytes 196616 | tf_op jit(solution)/shard_map/ppermute | solution.py:82
  100.5 5.4 %collective-permute-start.4 = (f32[64,256]{1,0:T(8,128)S(1)}, f32[64,256]{1,0:T(8,128)S(1)}, u32[]{:S(2)}, u32[]{:S(2)}) collective-permute-start(f32[64,256]{1,0:T(8,128)S(1)} %bitcast.243), channel_id=1, source_target_pairs={{0,5},{1,6},{2,7},{3,0},{4,1},{5,2},{6,3},{7,4},{8,13},{9,14},{10,... | collective-permute-start | bytes 196616 | tf_op jit(solution)/shard_map/ppermute | solution.py:82
  102.2 5.4 %collective-permute-start.5 = (f32[64,256]{1,0:T(8,128)S(1)}, f32[64,256]{1,0:T(8,128)S(1)}, u32[]{:S(2)}, u32[]{:S(2)}) collective-permute-start(f32[64,256]{1,0:T(8,128)S(1)} %bitcast.246), channel_id=1, source_target_pairs={{0,6},{1,7},{2,0},{3,1},{4,2},{5,3},{6,4},{7,5},{8,14},{9,15},{10,... | collective-permute-start | bytes 196616 | tf_op jit(solution)/shard_map/ppermute | solution.py:82
  104.5 3.1 %collective-permute-start.6 = (f32[64,256]{1,0:T(8,128)S(1)}, f32[64,256]{1,0:T(8,128)S(1)}, u32[]{:S(2)}, u32[]{:S(2)}) collective-permute-start(f32[64,256]{1,0:T(8,128)S(1)} %bitcast.244), channel_id=1, source_target_pairs={{0,7},{1,0},{2,1},{3,2},{4,3},{5,4},{6,5},{7,6},{8,15},{9,8},{10,9... | collective-permute-start | bytes 196616 | tf_op jit(solution)/shard_map/ppermute | solution.py:82
  144.2 6.1 %collective-permute-start.10 = (f32[64,256]{1,0:T(8,128)S(1)}, f32[64,256]{1,0:T(8,128)S(1)}, u32[]{:S(2)}, u32[]{:S(2)}) collective-permute-start(f32[64,256]{1,0:T(8,128)S(1)} %bitcast.245), channel_id=1, source_target_pairs={{0,4},{1,5},{2,6},{3,7},{4,0},{5,1},{6,2},{7,3},{8,12},{9,13},{10,... | collective-permute-start | bytes 196616 | tf_op jit(solution)/shard_map/ppermute | solution.py:82
  146.7 6.6 %collective-permute-start.11 = (f32[64,256]{1,0:T(8,128)S(1)}, f32[64,256]{1,0:T(8,128)S(1)}, u32[]{:S(2)}, u32[]{:S(2)}) collective-permute-start(f32[64,256]{1,0:T(8,128)S(1)} %bitcast.241), channel_id=1, source_target_pairs={{0,5},{1,6},{2,7},{3,0},{4,1},{5,2},{6,3},{7,4},{8,13},{9,14},{10,... | collective-permute-start | bytes 196616 | tf_op jit(solution)/shard_map/ppermute | solution.py:82
  146.8 30.2 %collective-permute-start.12 = (f32[64,256]{1,0:T(8,128)S(1)}, f32[64,256]{1,0:T(8,128)S(1)}, u32[]{:S(2)}, u32[]{:S(2)}) collective-permute-start(f32[64,256]{1,0:T(8,128)S(1)} %bitcast.233), channel_id=1, source_target_pairs={{0,6},{1,7},{2,0},{3,1},{4,2},{5,3},{6,4},{7,5},{8,14},{9,15},{10,... | collective-permute-start | bytes 196616 | tf_op jit(solution)/shard_map/ppermute | solution.py:82
  149.7 27.3 %collective-permute-start.13 = (f32[64,256]{1,0:T(8,128)S(1)}, f32[64,256]{1,0:T(8,128)S(1)}, u32[]{:S(2)}, u32[]{:S(2)}) collective-permute-start(f32[64,256]{1,0:T(8,128)S(1)} %bitcast.234), channel_id=1, source_target_pairs={{0,7},{1,0},{2,1},{3,2},{4,3},{5,4},{6,5},{7,6},{8,15},{9,8},{10,9... | collective-permute-start | bytes 196616 | tf_op jit(solution)/shard_map/ppermute | solution.py:82
  149.7 27.3 %collective-permute-start.7 = (f32[64,256]{1,0:T(8,128)S(1)}, f32[64,256]{1,0:T(8,128)S(1)}, u32[]{:S(2)}, u32[]{:S(2)}) collective-permute-start(f32[64,256]{1,0:T(8,128)S(1)} %bitcast.235), channel_id=1, source_target_pairs={{0,1},{1,2},{2,3},{3,4},{4,5},{5,6},{6,7},{7,0},{8,9},{9,10},{10,1... | collective-permute-start | bytes 196616 | tf_op jit(solution)/shard_map/ppermute | solution.py:82
  150.2 26.7 %collective-permute-start.8 = (f32[64,256]{1,0:T(8,128)S(1)}, f32[64,256]{1,0:T(8,128)S(1)}, u32[]{:S(2)}, u32[]{:S(2)}) collective-permute-start(f32[64,256]{1,0:T(8,128)S(1)} %bitcast.237), channel_id=1, source_target_pairs={{0,2},{1,3},{2,4},{3,5},{4,6},{5,7},{6,0},{7,1},{8,10},{9,11},{10,... | collective-permute-start | bytes 196616 | tf_op jit(solution)/shard_map/ppermute | solution.py:82
  153.3 23.7 %collective-permute-start.9 = (f32[64,256]{1,0:T(8,128)S(1)}, f32[64,256]{1,0:T(8,128)S(1)}, u32[]{:S(2)}, u32[]{:S(2)}) collective-permute-start(f32[64,256]{1,0:T(8,128)S(1)} %bitcast.236), channel_id=1, source_target_pairs={{0,3},{1,4},{2,5},{3,6},{4,7},{5,0},{6,1},{7,2},{8,11},{9,12},{10,... | collective-permute-start | bytes 196616 | tf_op jit(solution)/shard_map/ppermute | solution.py:82
Sparse Core Ops, SparseCore 0:
  10.2 125.2 all-gather.2

commit v10 on v4

--- a/solution.py
+++ b/solution.py
@@ -73,11 +73,15 @@
     )
 
 
-def reduce_to_slice(partial, kv_count, slice_width):
-    rows = partial.shape[0]
-    pieces = partial.reshape(rows, kv_count, slice_width).transpose(1, 0, 2)
-    arrived = lax.all_to_all(pieces, "kv", 0, 0, tiled=True)
-    return jnp.sum(arrived, axis=0)
+def sum_from_peers(pieces, axis):
+    count = lax.axis_size(axis)
+    me = lax.axis_index(axis)
+    total = pieces[me]
+    for shift in range(1, count):
+        total = total + lax.ppermute(
+            pieces[(me + shift) % count], axis, [(k, (k + shift) % count) for k in range(count)]
+        )
+    return total
 
 
 def layer_body(
@@ -111,7 +115,7 @@
     model_width = mlp_gain.shape[0]
     unit_count = w_gate.shape[1]
     stacked = lax.all_gather(
-        jnp.concatenate([w_gate.T, w_up.T, w_down.T], axis=0), "req", axis=0, tiled=False
+        jnp.concatenate([w_gate.T, w_up.T, w_down.T], axis=0), "kv", axis=0, tiled=False
     )
     gate_w = stacked[:, :unit_count, :]
     up_w = stacked[:, unit_count : 2 * unit_count, :]
@@ -165,20 +169,36 @@
     )
     head_terms = jnp.dot(gated, w_o, preferred_element_type=jnp.float32)
     kv_count = lax.axis_size("kv")
+    req_groups = lax.axis_size("req")
     slice_width = model_width // kv_count
-    mid_slice = (
-        hidden.astype(jnp.float32) + reduce_to_slice(head_terms, kv_count, slice_width)
-    ).astype(jnp.bfloat16)
-    mid_stream = lax.all_gather(mid_slice, "kv", axis=1, tiled=True)
-    normed_mlp = rms_norm(mid_stream, mlp_gain).astype(jnp.bfloat16)
-    gate_part = jnp.einsum("rd,sud->rsu", normed_mlp, gate_w, preferred_element_type=jnp.float32)
-    up_part = jnp.einsum("rd,sud->rsu", normed_mlp, up_w, preferred_element_type=jnp.float32)
+    row_share = req_count // kv_count
+    kv_index = lax.axis_index("kv")
+    attn_rows = sum_from_peers(head_terms.reshape(kv_count, row_share, model_width), "kv")
+    own_rows = lax.dynamic_slice_in_dim(whole_rows, kv_index * row_share, row_share, 0)
+    mid_rows = (own_rows.astype(jnp.float32) + attn_rows).astype(jnp.bfloat16)
+    normed_rows = rms_norm(mid_rows, mlp_gain).astype(jnp.bfloat16)
+    row_block = lax.all_gather(normed_rows, "req", axis=0, tiled=True)
+    gate_part = jnp.einsum("nd,sud->nsu", row_block, gate_w, preferred_element_type=jnp.float32)
+    up_part = jnp.einsum("nd,sud->nsu", row_block, up_w, preferred_element_type=jnp.float32)
     activation = (jax.nn.silu(gate_part) * up_part).astype(jnp.bfloat16)
     down_part = jnp.einsum(
-        "rsu,suc->rc", activation, down_w, preferred_element_type=jnp.float32
-    )
-    mlp_part = reduce_to_slice(down_part, kv_count, slice_width)
-    out_hidden = (mid_slice.astype(jnp.float32) + mlp_part).astype(jnp.bfloat16)
+        "nsu,suc->nc", activation, down_w, preferred_element_type=jnp.float32
+    )
+    mlp_rows = sum_from_peers(down_part.reshape(req_groups, row_share, model_width), "req")
+    out_rows = (mid_rows.astype(jnp.float32) + mlp_rows).astype(jnp.bfloat16)
+    col_pieces = out_rows.reshape(row_share, kv_count, slice_width).transpose(1, 0, 2)
+    by_shift = [col_pieces[kv_index]]
+    for shift in range(1, kv_count):
+        by_shift.append(
+            lax.ppermute(
+                col_pieces[(kv_index + shift) % kv_count],
+                "kv",
+                [(k, (k + shift) % kv_count) for k in range(kv_count)],
+            )
+        )
+    by_shift = jnp.stack(by_shift, axis=0)
+    sources = (kv_index - jnp.arange(kv_count, dtype=jnp.int32)) % kv_count
+    out_hidden = by_shift[sources].reshape(kv_count * row_share, slice_width)
     return (out_hidden, mig_keys, mig_values)
 
 

time: 177 us -> 196 us (1.11); the launches traced: 174 us -> 195 us
  starting transfers between devices: 28.4 us -> 58.5 us
  waiting for transfers between devices: 35.9 us -> 7.06 us
  blocking collectives: 29.5 us -> 53.5 us
  matrix products: 18.9 us -> 16.9 us
    ppermute x0 -> x29, starting transfers between devices: none -> 51.5 us  [the longest x22 33.8 us: sum_from_peers(): lax.ppermute(pieces[(me + shift) % count], axis, [(k, (k + shift) % count...]
    all_to_all x1, waiting for transfers between devices: 31.3 us -> 0.01 us  [layer_body(): lax.all_to_all(jnp.stack([place_cache(k_pool, new_keys), place_cache(v_po...]
    all_gather x1, blocking collectives: 13.9 us -> 37.9 us  [layer_body(): row_block = lax.all_gather(normed_rows, 'req', axis=0, tiled=True)]
    all_to_all x2 -> x0, starting transfers between devices: 21.2 us -> none  [reduce_to_slice(): arrived = lax.all_to_all(pieces, 'kv', 0, 0, tiled=True)]
    ppermute x0 -> x29, waiting for transfers between devices: none -> 7.04 us  [the longest x22 4.52 us: sum_from_peers(): lax.ppermute(pieces[(me + shift) % count], axis, [(k, (k + shift) % count...]
    all_to_all x2 -> x0, waiting for transfers between devices: 4.66 us -> none  [reduce_to_slice(): arrived = lax.all_to_all(pieces, 'kv', 0, 0, tiled=True)]
    dot_general x2, matrix products: 8.12 us -> 5.36 us  [the longest x1 3.37 us: layer_body(): jnp.einsum('nsu,suc->nc', activation, down_w, preferred_element_type=jnp....]
  transfers between devices with their start and end apart: 4 -> 31, of which waited for: 2 -> 5; matrix products, arithmetic and copies ran while one was open for 36% -> 30% of each run, Pallas kernels for 0% -> 0%
where the time goes in v10:
time: 196 us; the launch traced here: 195 us
  starting transfers between devices  58.5 us (30%)
  blocking collectives  53.5 us (27%)
  local copies, waits for them, and re-layouts  24.7 us (13%)
  other arithmetic  20 us (10%)
  matrix products  16.9 us (9%)
  between operations  14.8 us (8%)
  waiting for transfers between devices  7.06 us (4%)
    all_gather x1, blocking collectives, layer_body(): row_block = lax.all_gather(normed_rows, 'req', axis=0, tiled=True)  37.9 us
    ppermute x22, starting transfers between devices, sum_from_peers(): lax.ppermute(pieces[(me + shift) % count], axis, [(k, (k + shift) % count...  33.8 us
    ppermute x7, starting transfers between devices, layer_body(): lax.ppermute(col_pieces[(kv_index + shift) % kv_count], 'kv', [(k, (k + s...  17.7 us
    all_gather x1, blocking collectives, layer_body(): whole_rows = lax.all_gather(hidden, 'kv', axis=1, tiled=True)  15.6 us
    gather x2, local copies, waits for them, and re-layouts, place_cache(): cached = pool[moved_pages].reshape(mig_count, slot_count, channels)  8.55 us
    all_to_all x1, starting transfers between devices, layer_body(): lax.all_to_all(jnp.stack([place_cache(k_pool, new_keys), place_cache(v_po...  6.92 us
    select_n x1, other arithmetic, place_cache(): jnp.where(slot_pos < moved_len, cached, jnp.where(slot_pos == moved_len,...  5.61 us
    dot_general x1, matrix products, attend_pool(): jnp.einsum('rkgt,tkd->rkgd', weights, values, preferred_element_type=jnp....  5.29 us
  transfers between devices with their start and end apart: 31, of which 5 were waited for; matrix products, arithmetic and copies ran while one was open for 30% of the time, Pallas kernels for 0%

profile of v10, /device:TPU:1, one launch (start us, length us, event | category | flops | bytes accessed | tf_op | source)
XLA Modules:
  0.0 195.3 jit_solution(15010624065504162668)
XLA Ops:
  7.3 2.1 %pad_maximum_fusion.1 = bf16[144,2048]{1,0:T(8,128)(2,1)} fusion(bf16[48,2048]{1,0:T(8,128)(2,1)} %bitcast.280, bf16[48,2048]{1,0:T(8,128)(2,1)} %bitcast.281, bf16[48,2048]{1,0:T(8,128)(2,1)} %bitcast.282), kind=kLoop, calls=%fused_computation.52 | loop fusion | flops 1769472 | bytes 1179648 | tf_op jit(solution)/shard_map/concatenate | solution.py:118
  9.4 15.6 %all_gather.12 = bf16[64,2048]{1,0:T(8,128)(2,1)S(1)} all-gather(bf16[64,256]{1,0:T(8,128)(2,1)} %param.19), channel_id=1, replica_groups=mesh['req'=16,'kv'=8] {'kv'}, dimensions={1}, use_global_device_ids=true | all-gather | bytes 294912 | tf_op jit(solution)/shard_map/all_gather | solution.py:123
  25.2 0.4 multiply_reduce_fusion.1
  25.6 0.3 fusion.117
  26.0 0.6 scatter_custom_fusion
  26.6 0.7 gather_fusion.1
  27.3 0.7 gather_fusion.2
  28.1 0.2 fusion.87
  28.4 0.6 gather_fusion.4
  29.0 0.7 gather_fusion.9
  29.7 0.7 gather_fusion.10
  30.4 0.7 gather_fusion.7
  31.1 0.7 gather_fusion.8
  31.9 3.7 %gather_fusion.3 = bf16[64,128,128]{2,1,0:T(8,128)(2,1)S(1)} fusion(bf16[174,128,128]{2,1,0:T(8,128)(2,1)} %param.28, s32[1024]{0:T(1024)S(1)} %pad_clamp_fusion), kind=kCustom, calls=%fused_computation.3 | custom fusion | bytes 4194560 | tf_op jit(solution)/shard_map/gather | solution.py:151
  35.6 4.9 %gather_fusion.5 = bf16[64,128,128]{2,1,0:T(8,128)(2,1)} fusion(bf16[174,128,128]{2,1,0:T(8,128)(2,1)} %param.29, s32[1024]{0:T(1024)S(1)} %pad_clamp_fusion), kind=kCustom, calls=%fused_computation.5 | custom fusion | bytes 4194560 | tf_op jit(solution)/shard_map/gather | solution.py:151
  40.5 0.6 gather_fusion.6
  41.2 5.6 %select_select_fusion.1 = (bf16[16,1,512,128]{3,2,1,0:T(8,128)(2,1)S(1)}, bf16[16,1,512,128]{3,2,1,0:T(8,128)(2,1)S(1)}) fusion(bf16[16,1,512,128]{3,2,1,0:T(8,128)(2,1)S(1)} %bitcast.275, pred[16,512]{1,0:T(8,128)(4,1)S(1)} %get-tuple-element.51, pred[16,512]{1,0:T(8,128)(4,1)S(1)} %get-tuple-element.50, bf16[16,128]{1,0:T(8,128)(2,1)S(1)} %gather_fusion.4, ...), kind=kLoop, calls=%fused_computation.29 | loop fusion | flops 4194304 | bytes 8413184 | tf_op jit(solution)/shard_map/jit(_where)/select_n | solution.py:153
  46.8 2.4 %pad_maximum_fusion = bf16[16,2,512,128]{3,2,1,0:T(8,128)(2,1)} fusion(bf16[16,1,512,128]{3,2,1,0:T(8,128)(2,1)S(1)} %get-tuple-element.43, bf16[16,1,512,128]{3,2,1,0:T(8,128)(2,1)S(1)} %get-tuple-element.42), kind=kLoop, calls=%fused_computation.23 | loop fusion | flops 2097152 | bytes 8388608 | tf_op jit(solution)/shard_map/stack | solution.py:158
  49.2 6.9 %all-to-all-start = ((bf16[16,2,512,128]{3,2,1,0:T(8,128)(2,1)}), bf16[16,2,512,128]{3,2,1,0:T(8,128)(2,1)}, u32[]{:S(2)}, u32[]{:S(2)}) async-start(bf16[16,2,512,128]{3,2,1,0:T(8,128)(2,1)} %pad_maximum_fusion), calls=%async_computation | async-start | bytes 8388608 | tf_op jit(solution)/shard_map/all_to_all | solution.py:157
  56.2 0.2 multiply_cosine_fusion.1
  56.6 0.3 fusion.111
  57.5 0.2 fusion.83
  57.9 0.7 fusion.8
  58.7 1.0 select_reduce_fusion
  59.7 1.6 add.461
  61.4 2.1 %and.146 = pred[64,174,128]{2,1,0:T(8,128)(4,1)S(1)} broadcast(pred[64,174]{1,0:T(8,128)(4,1)S(1)} %fusion.8), dimensions={0,1} | broadcast | bytes 1436544 | tf_op jit(solution)/shard_map/and | solution.py:48
  63.4 3.9 %fusion.6 = pred[64,22272]{1,0:T(8,128)(4,1)S(1)} fusion(s32[8,8,174,128]{3,2,1,0:T(8,128)S(1)} %bitcast.273, pred[8,8,174,128]{3,2,1,0:T(8,128)(4,1)S(1)} %bitcast.277, s32[64]{0:T(128)S(1)} %copy-done.1, s32[22272]{0:T(1024)S(1)} %iota_bitcast_fusion), kind=kLoop, calls=%fused_computation.22 | loop fusion | flops 4276224 | bytes 8641792 | tf_op jit(solution)/shard_map/and | solution.py:48
  67.3 4.2 %fusion.116 = (f32[64,2]{0,1:T(2,128)S(1)}, f32[64,1,2,22272]{3,0,2,1:T(8,128)S(1)}) fusion(bf16[64,2,128]{2,0,1:T(8,128)(2,1)S(1)} %pad_maximum_fusion.2, bf16[22272,128,1]{1,0,2:T(8,128)(2,1)} %bitcast.274, pred[64,22272]{1,0:T(8,128)(4,1)S(1)} %fusion.6), kind=kOutput, calls=%fused_computation.222 | convolution fusion | flops 738361216 | bytes 18563584 | tf_op jit(solution)/shard_map/rkgd,tkd->rkgt/dot_general | solution.py:54
  71.5 2.3 %fusion.2 = f32[64,2]{0,1:T(2,128)S(1)} fusion(f32[64,1,2,22272]{3,0,2,1:T(8,128)S(1)} %get-tuple-element.59, f32[64,2]{0,1:T(2,128)S(1)} %fusion.96), kind=kLoop, calls=%fused_computation.17 | loop fusion | flops 5701504 | bytes 11404288 | tf_op jit(solution)/shard_map/reduce_sum | solution.py:65
  73.8 5.3 %fusion.29 = f32[64,1,2,128]{3,0,2,1:T(8,128)S(1)} fusion(bf16[22272,128,1]{1,0,2:T(8,128)(2,1)} %bitcast.278, f32[64,2]{0,1:T(2,128)S(1)} %get-tuple-element.45, f32[64,1,2,22272]{3,0,2,1:T(8,128)S(1)} %get-tuple-element.59, f32[64,2]{0,1:T(2,128)S(1)} %fusion.96, f32[64,128]{1,0:T(8,128)S(1)} %get-tuple-element.60, f32[64,2]{0,1:T(2,128)S(1)} %get-tuple-element.44), kind=kOutput, calls=%fused_computation.47 | convolution fusion | flops 738394112 | bytes 17204736 | tf_op jit(solution)/shard_map/rkgt,tkd->rkgd/dot_general | solution.py:71
  79.3 0.9 convolution_bitcast_fusion.1
  80.2 1.7 collective-permute-start
  81.9 2.8 %collective-permute-start.2 = (f32[8,2048]{1,0:T(8,128)S(1)}, f32[8,2048]{1,0:T(8,128)S(1)}, u32[]{:S(2)}, u32[]{:S(2)}) collective-permute-start(f32[8,2048]{1,0:T(8,128)S(1)} %get-tuple-element.29), channel_id=1, source_target_pairs={{0,3},{1,4},{2,5},{3,6},{4,7},{5,0},{6,1},{7,2},{8,11},{9,12},{10,... | collective-permute-start | bytes 196616 | tf_op jit(solution)/shard_map/ppermute | solution.py:81
  84.7 0.6 collective-permute-start.3
  85.2 1.8 collective-permute-start.4
  87.1 0.7 collective-permute-start.5
  87.8 0.5 collective-permute-start.6
  88.2 2.3 %collective-permute-done.3 = f32[8,2048]{1,0:T(8,128)S(1)} collective-permute-done((f32[8,2048]{1,0:T(8,128)S(1)}, f32[8,2048]{1,0:T(8,128)S(1)}, u32[]{:S(2)}, u32[]{:S(2)}) %collective-permute-start.3) | collective-permute-done | bytes 65568 | tf_op jit(solution)/shard_map/ppermute | solution.py:81
  90.5 0.3 collective-permute-done.4
  90.8 1.9 collective-permute-done.6
  93.0 37.9 %all_gather.13 = bf16[128,2048]{1,0:T(8,128)(2,1)S(1)} all-gather(bf16[8,2048]{1,0:T(8,128)(2,1)S(1)} %fusion.47), channel_id=1, replica_groups=mesh['req'=16,'kv'=8] {'req'}, dimensions={0}, use_global_device_ids=true | all-gather | bytes 557056 | tf_op jit(solution)/shard_map/all_gather | solution.py:180
  130.9 2.0 %fusion.12 = f32[128,8,48]{0,2,1:T(8,128)S(1)} fusion(bf16[8,144,2048]{2,1,0:T(8,128)(2,1)} %bitcast.290, bf16[128,2048]{1,0:T(8,128)(2,1)S(1)} %all_gather.13), kind=kOutput, calls=%fused_computation.37 | convolution fusion | flops 201326592 | bytes 2293760 | tf_op jit(solution)/shard_map/nd,sud->nsu/dot_general | solution.py:181
  132.8 3.4 %convolution_bitcast_fusion = f32[16,8,2048]{2,1,0:T(8,128)S(1)} fusion(bf16[8,144,2048]{2,1,0:T(8,128)(2,1)} %bitcast.291, bf16[128,2048]{1,0:T(8,128)(2,1)S(1)} %all_gather.13, f32[128,8,48]{0,2,1:T(8,128)S(1)} %fusion.12), kind=kOutput, calls=%fused_computation.24 | convolution fusion | flops 402948096 | bytes 4915200 | tf_op jit(solution)/shard_map/nsu,suc->nc/dot_general | solution.py:184
  136.4 1.2 collective-permute-start.11
  137.7 2.9 %collective-permute-start.12 = (f32[8,2048]{1,0:T(8,128)S(1)}, f32[8,2048]{1,0:T(8,128)S(1)}, u32[]{:S(2)}, u32[]{:S(2)}) collective-permute-start(f32[8,2048]{1,0:T(8,128)S(1)} %get-tuple-element.19), channel_id=1, source_target_pairs={{0,48},{8,56},{16,64},{24,72},{32,80},{40,88},{48,96},{56,104},{64... | collective-permute-start | bytes 196616 | tf_op jit(solution)/shard_map/ppermute | solution.py:81
  140.6 2.2 %collective-permute-start.13 = (f32[8,2048]{1,0:T(8,128)S(1)}, f32[8,2048]{1,0:T(8,128)S(1)}, u32[]{:S(2)}, u32[]{:S(2)}) collective-permute-start(f32[8,2048]{1,0:T(8,128)S(1)} %get-tuple-element.18), channel_id=1, source_target_pairs={{0,56},{8,64},{16,72},{24,80},{32,88},{40,96},{48,104},{56,112},{6... | collective-permute-start | bytes 196616 | tf_op jit(solution)/shard_map/ppermute | solution.py:81
  142.8 1.7 collective-permute-start.14
  144.6 2.3 %collective-permute-start.15 = (f32[8,2048]{1,0:T(8,128)S(1)}, f32[8,2048]{1,0:T(8,128)S(1)}, u32[]{:S(2)}, u32[]{:S(2)}) collective-permute-start(f32[8,2048]{1,0:T(8,128)S(1)} %get-tuple-element.16), channel_id=1, source_target_pairs={{0,72},{8,80},{16,88},{24,96},{32,104},{40,112},{48,120},{56,0},{6... | collective-permute-start | bytes 196616 | tf_op jit(solution)/shard_map/ppermute | solution.py:81
  146.9 2.4 %collective-permute-start.16 = (f32[8,2048]{1,0:T(8,128)S(1)}, f32[8,2048]{1,0:T(8,128)S(1)}, u32[]{:S(2)}, u32[]{:S(2)}) collective-permute-start(f32[8,2048]{1,0:T(8,128)S(1)} %get-tuple-element.15), channel_id=1, source_target_pairs={{0,80},{8,88},{16,96},{24,104},{32,112},{40,120},{48,0},{56,8},{64... | collective-permute-start | bytes 196616 | tf_op jit(solution)/shard_map/ppermute | solution.py:81
  149.4 2.8 %collective-permute-start.17 = (f32[8,2048]{1,0:T(8,128)S(1)}, f32[8,2048]{1,0:T(8,128)S(1)}, u32[]{:S(2)}, u32[]{:S(2)}) collective-permute-start(f32[8,2048]{1,0:T(8,128)S(1)} %get-tuple-element.14), channel_id=1, source_target_pairs={{0,88},{8,96},{16,104},{24,112},{32,120},{40,0},{48,8},{56,16},{64... | collective-permute-start | bytes 196616 | tf_op jit(solution)/shard_map/ppermute | solution.py:81
  152.2 2.0 %collective-permute-start.18 = (f32[8,2048]{1,0:T(8,128)S(1)}, f32[8,2048]{1,0:T(8,128)S(1)}, u32[]{:S(2)}, u32[]{:S(2)}) collective-permute-start(f32[8,2048]{1,0:T(8,128)S(1)} %get-tuple-element.13), channel_id=1, source_target_pairs={{0,96},{8,104},{16,112},{24,120},{32,0},{40,8},{48,16},{56,24},{64... | collective-permute-start | bytes 196616 | tf_op jit(solution)/shard_map/ppermute | solution.py:81
  154.2 0.7 collective-permute-start.20
  154.9 2.9 %collective-permute-start.21 = (f32[8,2048]{1,0:T(8,128)S(1)}, f32[8,2048]{1,0:T(8,128)S(1)}, u32[]{:S(2)}, u32[]{:S(2)}) collective-permute-start(f32[8,2048]{1,0:T(8,128)S(1)} %get-tuple-element.10), channel_id=1, source_target_pairs={{0,120},{8,0},{16,8},{24,16},{32,24},{40,32},{48,40},{56,48},{64,5... | collective-permute-start | bytes 196616 | tf_op jit(solution)/shard_map/ppermute | solution.py:81
  157.8 1.3 collective-permute-start.8
  159.2 3.1 %collective-permute-start.9 = (f32[8,2048]{1,0:T(8,128)S(1)}, f32[8,2048]{1,0:T(8,128)S(1)}, u32[]{:S(2)}, u32[]{:S(2)}) collective-permute-start(f32[8,2048]{1,0:T(8,128)S(1)} %get-tuple-element.22), channel_id=1, source_target_pairs={{0,24},{8,32},{16,40},{24,48},{32,56},{40,64},{48,72},{56,80},{64,... | collective-permute-start | bytes 196616 | tf_op jit(solution)/shard_map/ppermute | solution.py:81
  162.3 4.7 %slice_bitcast_fusion = (bf16[16,512,128]{2,1,0:T(8,128)(2,1)}, bf16[16,512,128]{2,1,0:T(8,128)(2,1)}) fusion(bf16[16,2,512,128]{3,2,1,0:T(8,128)(2,1)} %all-to-all-done), kind=kLoop, calls=%fused_computation.26 | loop fusion | bytes 8388608 | tf_op jit(solution)/shard_map/squeeze | solution.py:165
  167.1 11.3 %collective-permute-start.22 = (bf16[8,256]{1,0:T(8,128)(2,1)S(1)}, bf16[8,256]{1,0:T(8,128)(2,1)S(1)}, u32[]{:S(2)}, u32[]{:S(2)}) collective-permute-start(bf16[8,256]{1,0:T(8,128)(2,1)S(1)} %get-tuple-element.41), channel_id=1, source_target_pairs={{0,1},{1,2},{2,3},{3,4},{4,5},{5,6},{6,7},{7,0},{8,9},{9,10},{10,1... | collective-permute-start | bytes 12296 | tf_op jit(solution)/shard_map/ppermute | solution.py:193
  178.4 2.3 %collective-permute-start.24 = (bf16[8,256]{1,0:T(8,128)(2,1)S(1)}, bf16[8,256]{1,0:T(8,128)(2,1)S(1)}, u32[]{:S(2)}, u32[]{:S(2)}) collective-permute-start(bf16[8,256]{1,0:T(8,128)(2,1)S(1)} %get-tuple-element.39), channel_id=1, source_target_pairs={{0,3},{1,4},{2,5},{3,6},{4,7},{5,0},{6,1},{7,2},{8,11},{9,12},{10,... | collective-permute-start | bytes 12296 | tf_op jit(solution)/shard_map/ppermute | solution.py:193
  180.7 1.1 collective-permute-start.25
  181.8 1.9 collective-permute-start.26
  183.9 0.9 collective-permute-start.28
  184.8 1.5 collective-permute-done.26
  186.3 1.0 collective-permute-done.28
  187.3 1.2 gather_fusion
  (117 shorter events, 2.7 us)
Async XLA Ops:
  7.2 72.1 %copy-start = (bf16[256,2048]{1,0:T(8,128)(2,1)S(1)}, bf16[256,2048]{1,0:T(8,128)(2,1)}, u32[]{:S(2)}) copy-start(bf16[256,2048]{1,0:T(8,128)(2,1)} %param.27) | copy-start | bytes 3145732
  7.2 18.0 %copy-start.1 = (s32[64]{0:T(128)S(1)}, s32[64]{0:T(128)}, u32[]{:S(2)}) copy-start(s32[64]{0:T(128)} %param.30) | copy-start | bytes 772
  7.2 18.0 %copy-start.7 = (f32[2048]{0:T(1024)S(1)}, f32[2048]{0:T(1024)}, u32[]{:S(2)}) copy-start(f32[2048]{0:T(1024)} %param.20) | copy-start | bytes 24580
  7.2 18.0 %copy-start.12 = (bf16[2048,128]{1,0:T(8,128)(2,1)S(1)}, bf16[2048,128]{1,0:T(8,128)(2,1)}, u32[]{:S(2)}) copy-start(bf16[2048,128]{1,0:T(8,128)(2,1)} %param.25) | copy-start | bytes 1572868
  7.2 18.4 %copy-start.6 = (bf16[2048,128]{1,0:T(8,128)(2,1)S(1)}, bf16[2048,128]{1,0:T(8,128)(2,1)}, u32[]{:S(2)}) copy-start(bf16[2048,128]{1,0:T(8,128)(2,1)} %param.26) | copy-start | bytes 1572868
  7.2 18.7 %copy-start.13 = (s32[1,16]{1,0:T(1,128)S(1)}, s32[1,16]{1,0:T(1,128)}, u32[]{:S(2)}) copy-start(s32[1,16]{1,0:T(1,128)} %param.33) | copy-start | bytes 196
  7.2 19.4 %copy-start.2 = (s32[1,16]{1,0:T(1,128)S(1)}, s32[1,16]{1,0:T(1,128)}, u32[]{:S(2)}) copy-start(s32[1,16]{1,0:T(1,128)} %param.32) | copy-start | bytes 196
  7.2 123.6 %all-gather.3.cloned.1.call-start = ((), (), s32[]{:S(2)}) async-start(), calls=%async_computation.1 | async-start | bytes 5308416 | tf_op jit(solution)/shard_map/all_gather | solution.py:117
  9.4 18.6 %copy-start.9 = (f32[128]{0:T(128)S(1)}, f32[128]{0:T(128)}, u32[]{:S(2)}) copy-start(f32[128]{0:T(128)} %param.22) | copy-start | bytes 1540
  9.4 19.5 %copy-start.11 = (s32[2]{0:T(128)S(1)}, s32[2]{0:T(128)}, u32[]{:S(2)}) copy-start(s32[2]{0:T(128)} %constant.234) | copy-start | bytes 28
  9.4 19.6 %copy-start.3 = (s32[64,32]{0,1:T(8,128)S(1)}, s32[64,32]{0,1:T(8,128)}, u32[]{:S(2)}) copy-start(s32[64,32]{0,1:T(8,128)} %param.31) | copy-start | bytes 24580
  49.2 7.4 %copy-start.5 = (bf16[2048,256]{1,0:T(8,128)(2,1)S(1)}, bf16[2048,256]{1,0:T(8,128)(2,1)}, u32[]{:S(2)}) copy-start(bf16[2048,256]{1,0:T(8,128)(2,1)} %param.23) | copy-start | bytes 3145732
  49.2 113.1 %all-to-all-start = ((bf16[16,2,512,128]{3,2,1,0:T(8,128)(2,1)}), bf16[16,2,512,128]{3,2,1,0:T(8,128)(2,1)}, u32[]{:S(2)}, u32[]{:S(2)}) async-start(bf16[16,2,512,128]{3,2,1,0:T(8,128)(2,1)} %pad_maximum_fusion), calls=%async_computation | async-start | bytes 8388608 | tf_op jit(solution)/shard_map/all_to_all | solution.py:157
  56.1 1.1 copy-start.10
  73.8 5.4 %copy-start.4 = (bf16[2048,256]{1,0:T(8,128)(2,1)S(1)}, bf16[2048,256]{1,0:T(8,128)(2,1)}, u32[]{:S(2)}) copy-start(bf16[2048,256]{1,0:T(8,128)(2,1)} %param.24) | copy-start | bytes 3145732
  79.3 13.6 %copy-start.8 = (f32[2048]{0:T(1024)S(1)}, f32[2048]{0:T(1024)}, u32[]{:S(2)}) copy-start(f32[2048]{0:T(1024)} %param.34) | copy-start | bytes 24580
  80.2 6.9 %collective-permute-start = (f32[8,2048]{1,0:T(8,128)S(1)}, f32[8,2048]{1,0:T(8,128)S(1)}, u32[]{:S(2)}, u32[]{:S(2)}) collective-permute-start(f32[8,2048]{1,0:T(8,128)S(1)} %get-tuple-element.24), channel_id=1, source_target_pairs={{0,1},{1,2},{2,3},{3,4},{4,5},{5,6},{6,7},{7,0},{8,9},{9,10},{10,1... | collective-permute-start | bytes 196616 | tf_op jit(solution)/shard_map/ppermute | solution.py:81
  81.9 5.9 %collective-permute-start.1 = (f32[8,2048]{1,0:T(8,128)S(1)}, f32[8,2048]{1,0:T(8,128)S(1)}, u32[]{:S(2)}, u32[]{:S(2)}) collective-permute-start(f32[8,2048]{1,0:T(8,128)S(1)} %get-tuple-element.30), channel_id=1, source_target_pairs={{0,2},{1,3},{2,4},{3,5},{4,6},{5,7},{6,0},{7,1},{8,10},{9,11},{10,... | collective-permute-start | bytes 196616 | tf_op jit(solution)/shard_map/ppermute | solution.py:81
  81.9 6.3 %collective-permute-start.2 = (f32[8,2048]{1,0:T(8,128)S(1)}, f32[8,2048]{1,0:T(8,128)S(1)}, u32[]{:S(2)}, u32[]{:S(2)}) collective-permute-start(f32[8,2048]{1,0:T(8,128)S(1)} %get-tuple-element.29), channel_id=1, source_target_pairs={{0,3},{1,4},{2,5},{3,6},{4,7},{5,0},{6,1},{7,2},{8,11},{9,12},{10,... | collective-permute-start | bytes 196616 | tf_op jit(solution)/shard_map/ppermute | solution.py:81
  84.7 5.9 %collective-permute-start.3 = (f32[8,2048]{1,0:T(8,128)S(1)}, f32[8,2048]{1,0:T(8,128)S(1)}, u32[]{:S(2)}, u32[]{:S(2)}) collective-permute-start(f32[8,2048]{1,0:T(8,128)S(1)} %get-tuple-element.28), channel_id=1, source_target_pairs={{0,4},{1,5},{2,6},{3,7},{4,0},{5,1},{6,2},{7,3},{8,12},{9,13},{10,... | collective-permute-start | bytes 196616 | tf_op jit(solution)/shard_map/ppermute | solution.py:81
  85.2 5.6 %collective-permute-start.4 = (f32[8,2048]{1,0:T(8,128)S(1)}, f32[8,2048]{1,0:T(8,128)S(1)}, u32[]{:S(2)}, u32[]{:S(2)}) collective-permute-start(f32[8,2048]{1,0:T(8,128)S(1)} %get-tuple-element.27), channel_id=1, source_target_pairs={{0,5},{1,6},{2,7},{3,0},{4,1},{5,2},{6,3},{7,4},{8,13},{9,14},{10,... | collective-permute-start | bytes 196616 | tf_op jit(solution)/shard_map/ppermute | solution.py:81
  87.1 3.8 %collective-permute-start.5 = (f32[8,2048]{1,0:T(8,128)S(1)}, f32[8,2048]{1,0:T(8,128)S(1)}, u32[]{:S(2)}, u32[]{:S(2)}) collective-permute-start(f32[8,2048]{1,0:T(8,128)S(1)} %get-tuple-element.26), channel_id=1, source_target_pairs={{0,6},{1,7},{2,0},{3,1},{4,2},{5,3},{6,4},{7,5},{8,14},{9,15},{10,... | collective-permute-start | bytes 196616 | tf_op jit(solution)/shard_map/ppermute | solution.py:81
  87.8 4.9 %collective-permute-start.6 = (f32[8,2048]{1,0:T(8,128)S(1)}, f32[8,2048]{1,0:T(8,128)S(1)}, u32[]{:S(2)}, u32[]{:S(2)}) collective-permute-start(f32[8,2048]{1,0:T(8,128)S(1)} %get-tuple-element.25), channel_id=1, source_target_pairs={{0,7},{1,0},{2,1},{3,2},{4,3},{5,4},{6,5},{7,6},{8,15},{9,8},{10,9... | collective-permute-start | bytes 196616 | tf_op jit(solution)/shard_map/ppermute | solution.py:81
  136.4 8.2 %collective-permute-start.10 = (f32[8,2048]{1,0:T(8,128)S(1)}, f32[8,2048]{1,0:T(8,128)S(1)}, u32[]{:S(2)}, u32[]{:S(2)}) collective-permute-start(f32[8,2048]{1,0:T(8,128)S(1)} %get-tuple-element.21), channel_id=1, source_target_pairs={{0,32},{8,40},{16,48},{24,56},{32,64},{40,72},{48,80},{56,88},{64,... | collective-permute-start | bytes 196616 | tf_op jit(solution)/shard_map/ppermute | solution.py:81
  136.4 10.5 %collective-permute-start.11 = (f32[8,2048]{1,0:T(8,128)S(1)}, f32[8,2048]{1,0:T(8,128)S(1)}, u32[]{:S(2)}, u32[]{:S(2)}) collective-permute-start(f32[8,2048]{1,0:T(8,128)S(1)} %get-tuple-element.20), channel_id=1, source_target_pairs={{0,40},{8,48},{16,56},{24,64},{32,72},{40,80},{48,88},{56,96},{64,... | collective-permute-start | bytes 196616 | tf_op jit(solution)/shard_map/ppermute | solution.py:81
  137.7 11.7 %collective-permute-start.12 = (f32[8,2048]{1,0:T(8,128)S(1)}, f32[8,2048]{1,0:T(8,128)S(1)}, u32[]{:S(2)}, u32[]{:S(2)}) collective-permute-start(f32[8,2048]{1,0:T(8,128)S(1)} %get-tuple-element.19), channel_id=1, source_target_pairs={{0,48},{8,56},{16,64},{24,72},{32,80},{40,88},{48,96},{56,104},{64... | collective-permute-start | bytes 196616 | tf_op jit(solution)/shard_map/ppermute | solution.py:81
  140.6 11.6 %collective-permute-start.13 = (f32[8,2048]{1,0:T(8,128)S(1)}, f32[8,2048]{1,0:T(8,128)S(1)}, u32[]{:S(2)}, u32[]{:S(2)}) collective-permute-start(f32[8,2048]{1,0:T(8,128)S(1)} %get-tuple-element.18), channel_id=1, source_target_pairs={{0,56},{8,64},{16,72},{24,80},{32,88},{40,96},{48,104},{56,112},{6... | collective-permute-start | bytes 196616 | tf_op jit(solution)/shard_map/ppermute | solution.py:81
  142.8 11.3 %collective-permute-start.14 = (f32[8,2048]{1,0:T(8,128)S(1)}, f32[8,2048]{1,0:T(8,128)S(1)}, u32[]{:S(2)}, u32[]{:S(2)}) collective-permute-start(f32[8,2048]{1,0:T(8,128)S(1)} %get-tuple-element.17), channel_id=1, source_target_pairs={{0,64},{8,72},{16,80},{24,88},{32,96},{40,104},{48,112},{56,120},{... | collective-permute-start | bytes 196616 | tf_op jit(solution)/shard_map/ppermute | solution.py:81
  144.6 9.6 %collective-permute-start.15 = (f32[8,2048]{1,0:T(8,128)S(1)}, f32[8,2048]{1,0:T(8,128)S(1)}, u32[]{:S(2)}, u32[]{:S(2)}) collective-permute-start(f32[8,2048]{1,0:T(8,128)S(1)} %get-tuple-element.16), channel_id=1, source_target_pairs={{0,72},{8,80},{16,88},{24,96},{32,104},{40,112},{48,120},{56,0},{6... | collective-permute-start | bytes 196616 | tf_op jit(solution)/shard_map/ppermute | solution.py:81
  146.9 8.0 %collective-permute-start.16 = (f32[8,2048]{1,0:T(8,128)S(1)}, f32[8,2048]{1,0:T(8,128)S(1)}, u32[]{:S(2)}, u32[]{:S(2)}) collective-permute-start(f32[8,2048]{1,0:T(8,128)S(1)} %get-tuple-element.15), channel_id=1, source_target_pairs={{0,80},{8,88},{16,96},{24,104},{32,112},{40,120},{48,0},{56,8},{64... | collective-permute-start | bytes 196616 | tf_op jit(solution)/shard_map/ppermute | solution.py:81
  149.4 8.4 %collective-permute-start.17 = (f32[8,2048]{1,0:T(8,128)S(1)}, f32[8,2048]{1,0:T(8,128)S(1)}, u32[]{:S(2)}, u32[]{:S(2)}) collective-permute-start(f32[8,2048]{1,0:T(8,128)S(1)} %get-tuple-element.14), channel_id=1, source_target_pairs={{0,88},{8,96},{16,104},{24,112},{32,120},{40,0},{48,8},{56,16},{64... | collective-permute-start | bytes 196616 | tf_op jit(solution)/shard_map/ppermute | solution.py:81
  152.2 5.7 %collective-permute-start.18 = (f32[8,2048]{1,0:T(8,128)S(1)}, f32[8,2048]{1,0:T(8,128)S(1)}, u32[]{:S(2)}, u32[]{:S(2)}) collective-permute-start(f32[8,2048]{1,0:T(8,128)S(1)} %get-tuple-element.13), channel_id=1, source_target_pairs={{0,96},{8,104},{16,112},{24,120},{32,0},{40,8},{48,16},{56,24},{64... | collective-permute-start | bytes 196616 | tf_op jit(solution)/shard_map/ppermute | solution.py:81
  154.2 5.0 %collective-permute-start.19 = (f32[8,2048]{1,0:T(8,128)S(1)}, f32[8,2048]{1,0:T(8,128)S(1)}, u32[]{:S(2)}, u32[]{:S(2)}) collective-permute-start(f32[8,2048]{1,0:T(8,128)S(1)} %get-tuple-element.12), channel_id=1, source_target_pairs={{0,104},{8,112},{16,120},{24,0},{32,8},{40,16},{48,24},{56,32},{64... | collective-permute-start | bytes 196616 | tf_op jit(solution)/shard_map/ppermute | solution.py:81
  154.2 12.8 %collective-permute-start.20 = (f32[8,2048]{1,0:T(8,128)S(1)}, f32[8,2048]{1,0:T(8,128)S(1)}, u32[]{:S(2)}, u32[]{:S(2)}) collective-permute-start(f32[8,2048]{1,0:T(8,128)S(1)} %get-tuple-element.11), channel_id=1, source_target_pairs={{0,112},{8,120},{16,0},{24,8},{32,16},{40,24},{48,32},{56,40},{64,... | collective-permute-start | bytes 196616 | tf_op jit(solution)/shard_map/ppermute | solution.py:81
  154.9 12.1 %collective-permute-start.21 = (f32[8,2048]{1,0:T(8,128)S(1)}, f32[8,2048]{1,0:T(8,128)S(1)}, u32[]{:S(2)}, u32[]{:S(2)}) collective-permute-start(f32[8,2048]{1,0:T(8,128)S(1)} %get-tuple-element.10), channel_id=1, source_target_pairs={{0,120},{8,0},{16,8},{24,16},{32,24},{40,32},{48,40},{56,48},{64,5... | collective-permute-start | bytes 196616 | tf_op jit(solution)/shard_map/ppermute | solution.py:81
  157.8 9.1 %collective-permute-start.7 = (f32[8,2048]{1,0:T(8,128)S(1)}, f32[8,2048]{1,0:T(8,128)S(1)}, u32[]{:S(2)}, u32[]{:S(2)}) collective-permute-start(f32[8,2048]{1,0:T(8,128)S(1)} %get-tuple-element.9), channel_id=1, source_target_pairs={{0,8},{8,16},{16,24},{24,32},{32,40},{40,48},{48,56},{56,64},{64,7... | collective-permute-start | bytes 196616 | tf_op jit(solution)/shard_map/ppermute | solution.py:81
  157.8 9.1 %collective-permute-start.8 = (f32[8,2048]{1,0:T(8,128)S(1)}, f32[8,2048]{1,0:T(8,128)S(1)}, u32[]{:S(2)}, u32[]{:S(2)}) collective-permute-start(f32[8,2048]{1,0:T(8,128)S(1)} %get-tuple-element.23), channel_id=1, source_target_pairs={{0,16},{8,24},{16,32},{24,40},{32,48},{40,56},{48,64},{56,72},{64,... | collective-permute-start | bytes 196616 | tf_op jit(solution)/shard_map/ppermute | solution.py:81
  159.2 7.8 %collective-permute-start.9 = (f32[8,2048]{1,0:T(8,128)S(1)}, f32[8,2048]{1,0:T(8,128)S(1)}, u32[]{:S(2)}, u32[]{:S(2)}) collective-permute-start(f32[8,2048]{1,0:T(8,128)S(1)} %get-tuple-element.22), channel_id=1, source_target_pairs={{0,24},{8,32},{16,40},{24,48},{32,56},{40,64},{48,72},{56,80},{64,... | collective-permute-start | bytes 196616 | tf_op jit(solution)/shard_map/ppermute | solution.py:81
  167.1 16.6 %collective-permute-start.22 = (bf16[8,256]{1,0:T(8,128)(2,1)S(1)}, bf16[8,256]{1,0:T(8,128)(2,1)S(1)}, u32[]{:S(2)}, u32[]{:S(2)}) collective-permute-start(bf16[8,256]{1,0:T(8,128)(2,1)S(1)} %get-tuple-element.41), channel_id=1, source_target_pairs={{0,1},{1,2},{2,3},{3,4},{4,5},{5,6},{6,7},{7,0},{8,9},{9,10},{10,1... | collective-permute-start | bytes 12296 | tf_op jit(solution)/shard_map/ppermute | solution.py:193
  178.4 5.4 %collective-permute-start.23 = (bf16[8,256]{1,0:T(8,128)(2,1)S(1)}, bf16[8,256]{1,0:T(8,128)(2,1)S(1)}, u32[]{:S(2)}, u32[]{:S(2)}) collective-permute-start(bf16[8,256]{1,0:T(8,128)(2,1)S(1)} %get-tuple-element.40), channel_id=1, source_target_pairs={{0,2},{1,3},{2,4},{3,5},{4,6},{5,7},{6,0},{7,1},{8,10},{9,11},{10,... | collective-permute-start | bytes 12296 | tf_op jit(solution)/shard_map/ppermute | solution.py:193
  178.4 6.3 %collective-permute-start.24 = (bf16[8,256]{1,0:T(8,128)(2,1)S(1)}, bf16[8,256]{1,0:T(8,128)(2,1)S(1)}, u32[]{:S(2)}, u32[]{:S(2)}) collective-permute-start(bf16[8,256]{1,0:T(8,128)(2,1)S(1)} %get-tuple-element.39), channel_id=1, source_target_pairs={{0,3},{1,4},{2,5},{3,6},{4,7},{5,0},{6,1},{7,2},{8,11},{9,12},{10,... | collective-permute-start | bytes 12296 | tf_op jit(solution)/shard_map/ppermute | solution.py:193
  180.7 4.1 %collective-permute-start.25 = (bf16[8,256]{1,0:T(8,128)(2,1)S(1)}, bf16[8,256]{1,0:T(8,128)(2,1)S(1)}, u32[]{:S(2)}, u32[]{:S(2)}) collective-permute-start(bf16[8,256]{1,0:T(8,128)(2,1)S(1)} %get-tuple-element.38), channel_id=1, source_target_pairs={{0,4},{1,5},{2,6},{3,7},{4,0},{5,1},{6,2},{7,3},{8,12},{9,13},{10,... | collective-permute-start | bytes 12296 | tf_op jit(solution)/shard_map/ppermute | solution.py:193
  181.8 4.5 %collective-permute-start.26 = (bf16[8,256]{1,0:T(8,128)(2,1)S(1)}, bf16[8,256]{1,0:T(8,128)(2,1)S(1)}, u32[]{:S(2)}, u32[]{:S(2)}) collective-permute-start(bf16[8,256]{1,0:T(8,128)(2,1)S(1)} %get-tuple-element.37), channel_id=1, source_target_pairs={{0,5},{1,6},{2,7},{3,0},{4,1},{5,2},{6,3},{7,4},{8,13},{9,14},{10,... | collective-permute-start | bytes 12296 | tf_op jit(solution)/shard_map/ppermute | solution.py:193
  183.7 2.7 %collective-permute-start.27 = (bf16[8,256]{1,0:T(8,128)(2,1)S(1)}, bf16[8,256]{1,0:T(8,128)(2,1)S(1)}, u32[]{:S(2)}, u32[]{:S(2)}) collective-permute-start(bf16[8,256]{1,0:T(8,128)(2,1)S(1)} %get-tuple-element.36), channel_id=1, source_target_pairs={{0,6},{1,7},{2,0},{3,1},{4,2},{5,3},{6,4},{7,5},{8,14},{9,15},{10,... | collective-permute-start | bytes 12296 | tf_op jit(solution)/shard_map/ppermute | solution.py:193
  183.9 3.5 %collective-permute-start.28 = (bf16[8,256]{1,0:T(8,128)(2,1)S(1)}, bf16[8,256]{1,0:T(8,128)(2,1)S(1)}, u32[]{:S(2)}, u32[]{:S(2)}) collective-permute-start(bf16[8,256]{1,0:T(8,128)(2,1)S(1)} %get-tuple-element.35), channel_id=1, source_target_pairs={{0,7},{1,0},{2,1},{3,2},{4,3},{5,4},{6,5},{7,6},{8,15},{9,8},{10,9... | collective-permute-start | bytes 12296 | tf_op jit(solution)/shard_map/ppermute | solution.py:193
Sparse Core Ops, SparseCore 0:
  10.3 38.0 all-gather.2

commit v11 on v7

--- a/solution.py
+++ b/solution.py
@@ -164,15 +164,8 @@
             slot_pos < moved_len, cached, jnp.where(slot_pos == moved_len, fresh_row, zero_value)
         )
 
-    moving = lax.all_to_all(
-        jnp.stack([place_cache(k_pool, new_keys), place_cache(v_pool, new_values)], axis=1),
-        "req",
-        0,
-        0,
-        tiled=True,
-    )
-    mig_keys = moving[:, 0]
-    mig_values = moving[:, 1]
+    mig_keys = lax.all_to_all(place_cache(k_pool, new_keys), "req", 0, 0, tiled=True)
+    mig_values = lax.all_to_all(place_cache(v_pool, new_values), "req", 0, 0, tiled=True)
     context = attend_pool(queries, new_keys, new_values, k_pool, v_pool, lengths, page_table)
     gated = (jax.nn.sigmoid(gate_raw) * context.reshape(req_count, q_local * head_dim)).astype(
         jnp.bfloat16
@@ -188,9 +181,7 @@
     gate_part = jnp.einsum("rd,sud->rsu", normed_mlp, gate_w, preferred_element_type=jnp.float32)
     up_part = jnp.einsum("rd,sud->rsu", normed_mlp, up_w, preferred_element_type=jnp.float32)
     activation = (jax.nn.silu(gate_part) * up_part).astype(jnp.bfloat16)
-    down_part = jnp.einsum(
-        "rsu,suc->rc", activation, down_w, preferred_element_type=jnp.float32
-    )
+    down_part = jnp.einsum("rsu,suc->rc", activation, down_w, preferred_element_type=jnp.float32)
     mlp_part = reduce_by_permutes(down_part, kv_count, slice_width)
     out_hidden = (mid_slice.astype(jnp.float32) + mlp_part).astype(jnp.bfloat16)
     return (out_hidden, mig_keys, mig_values)

time: 161 us -> 174 us (1.081)
  the two profiles are of different devices: /device:TPU:52 before, /device:TPU:1 now
where the time goes in v11:
time: 174 us; the launch traced here: 173 us
  blocking collectives  64.9 us (37%)
  local copies, waits for them, and re-layouts  28.7 us (16%)
  matrix products  22.6 us (13%)
  other arithmetic  21.6 us (12%)
  starting transfers between devices  16.6 us (10%)
  between operations  14.6 us (8%)
  waiting for transfers between devices  4.28 us (2%)
    all_to_all x1, blocking collectives, layer_body(): lax.all_to_all(place_cache(k_pool, new_keys), 'req', 0, 0, tiled=True)  34 us
    all_gather x1, blocking collectives, layer_body(): whole_rows = lax.all_gather(hidden, 'kv', axis=1, tiled=True)  15.6 us
    all_gather x1, blocking collectives, layer_body(): mid_stream = lax.all_gather(mid_slice, 'kv', axis=1, tiled=True)  15.3 us
    unnamed x39, local copies, waits for them, and re-layouts  8.92 us
    gather x2, local copies, waits for them, and re-layouts, place_cache(): cached = pool[moved_pages].reshape(mig_count, slot_count, channels)  8.44 us
    ppermute x7, starting transfers between devices, reduce_by_permutes(): lax.ppermute(pieces[(me + shift) % kv_count], 'kv', [(k, (k + shift) % kv...  7.59 us
    select_n x1, other arithmetic, place_cache(): jnp.where(slot_pos < moved_len, cached, jnp.where(slot_pos == moved_len,...  7.24 us
    dot_general x1, matrix products, layer_body(): jnp.einsum('rsu,suc->rc', activation, down_w, preferred_element_type=jnp....  6.08 us
  transfers between devices with their start and end apart: 10, of which 4 were waited for; matrix products, arithmetic and copies ran while one was open for 37% of the time, Pallas kernels for 0%

profile of v11, /device:TPU:1, one launch (start us, length us, event | category | flops | bytes accessed | tf_op | source)
XLA Modules:
  0.0 173.3 jit_solution(10402446371289711138)
XLA Ops:
  7.3 2.1 %pad_maximum_fusion = bf16[144,2048]{1,0:T(8,128)(2,1)} fusion(bf16[48,2048]{1,0:T(8,128)(2,1)} %bitcast.193, bf16[48,2048]{1,0:T(8,128)(2,1)} %bitcast.194, bf16[48,2048]{1,0:T(8,128)(2,1)} %bitcast.195), kind=kLoop, calls=%fused_computation.50 | loop fusion | flops 1769472 | bytes 1179648 | tf_op jit(solution)/shard_map/concatenate | solution.py:128
  9.4 15.6 %all_gather.12 = bf16[64,2048]{1,0:T(8,128)(2,1)S(1)} all-gather(bf16[64,256]{1,0:T(8,128)(2,1)} %param.19), channel_id=1, replica_groups=mesh['req'=16,'kv'=8] {'kv'}, dimensions={1}, use_global_device_ids=true | all-gather | bytes 294912 | tf_op jit(solution)/shard_map/all_gather | solution.py:133
  25.0 0.2 fusion.35
  25.1 1.6 fusion.89
  26.8 0.4 multiply_reduce_fusion.1
  27.3 0.1 multiply_reduce_fusion
  27.5 0.2 fusion.75
  27.8 0.2 multiply_cosine_fusion.1
  28.1 0.1 subtract_convert_fusion
  28.2 0.1 pad_maximum_fusion.1
  28.3 0.2 fusion.71
  28.8 0.7 fusion.14
  29.5 1.0 select_reduce_fusion
  30.6 1.6 add.225
  32.2 2.1 %and.60 = pred[64,174,128]{2,1,0:T(8,128)(4,1)S(1)} broadcast(pred[64,174]{1,0:T(8,128)(4,1)S(1)} %fusion.14), dimensions={0,1} | broadcast | bytes 1436544 | tf_op jit(solution)/shard_map/and | solution.py:48
  34.3 3.9 %fusion.6 = pred[64,22272]{1,0:T(8,128)(4,1)S(1)} fusion(s32[8,8,174,128]{3,2,1,0:T(8,128)S(1)} %bitcast.183, pred[8,8,174,128]{3,2,1,0:T(8,128)(4,1)S(1)} %bitcast.187, s32[64]{0:T(128)S(1)} %copy-done.1, s32[22272]{0:T(1024)S(1)} %iota_bitcast_fusion), kind=kLoop, calls=%fused_computation.21 | loop fusion | flops 4276224 | bytes 8641792 | tf_op jit(solution)/shard_map/and | solution.py:48
  38.2 4.2 %fusion.93 = (f32[64,2]{0,1:T(2,128)S(1)}, f32[64,1,2,22272]{3,0,2,1:T(8,128)S(1)}) fusion(bf16[64,2,128]{2,0,1:T(8,128)(2,1)S(1)} %pad_maximum_fusion.1, bf16[22272,128,1]{1,0,2:T(8,128)(2,1)} %bitcast.184, pred[64,22272]{1,0:T(8,128)(4,1)S(1)} %fusion.6), kind=kOutput, calls=%fused_computation.164 | convolution fusion | flops 738361216 | bytes 18563584 | tf_op jit(solution)/shard_map/rkgd,tkd->rkgt/dot_general | solution.py:54
  42.5 2.3 %fusion.2 = f32[64,2]{0,1:T(2,128)S(1)} fusion(f32[64,1,2,22272]{3,0,2,1:T(8,128)S(1)} %get-tuple-element.34, f32[64,2]{0,1:T(2,128)S(1)} %fusion.76), kind=kLoop, calls=%fused_computation.16 | loop fusion | flops 5701504 | bytes 11404288 | tf_op jit(solution)/shard_map/reduce_sum | solution.py:65
  44.8 0.3 fusion.94
  45.1 5.3 %fusion.30 = f32[64,1,2,128]{3,0,2,1:T(8,128)S(1)} fusion(bf16[22272,128,1]{1,0,2:T(8,128)(2,1)} %bitcast.190, f32[64,2]{0,1:T(2,128)S(1)} %get-tuple-element.20, f32[64,1,2,22272]{3,0,2,1:T(8,128)S(1)} %get-tuple-element.34, f32[64,2]{0,1:T(2,128)S(1)} %fusion.76, f32[64,128]{1,0:T(8,128)S(1)} %get-tuple-element.35, f32[64,2]{0,1:T(2,128)S(1)} %get-tuple-element.19), kind=kOutput, calls=%fused_computation.42 | convolution fusion | flops 738394112 | bytes 17204736 | tf_op jit(solution)/shard_map/rkgt,tkd->rkgd/dot_general | solution.py:71
  50.5 0.9 fusion.34
  51.4 0.9 copy.86
  52.2 4.3 %all-to-all-start = ((f32[8,64,256]{2,1,0:T(8,128)}), f32[8,64,256]{2,1,0:T(8,128)}, u32[]{:S(2)}, u32[]{:S(2)}) async-start(f32[8,64,256]{2,1,0:T(8,128)} %bitcast.173), calls=%async_computation | async-start | bytes 1048576 | tf_op jit(solution)/shard_map/all_to_all | solution.py:79
  56.6 0.8 scatter_custom_fusion
  57.4 0.7 gather_fusion
  58.2 0.7 gather_fusion.8
  58.8 0.7 gather_fusion.9
  59.5 0.7 gather_fusion.6
  60.2 0.7 gather_fusion.7
  61.0 0.1 reshape.459
  61.1 3.7 %gather_fusion.4 = bf16[64,128,128]{2,1,0:T(8,128)(2,1)S(1)} fusion(bf16[174,128,128]{2,1,0:T(8,128)(2,1)} %param.29, s32[1024]{0:T(1024)S(1)} %pad_clamp_fusion), kind=kCustom, calls=%fused_computation.4 | custom fusion | bytes 4194560 | tf_op jit(solution)/shard_map/gather | solution.py:161
  64.7 4.8 %gather_fusion.2 = bf16[64,128,128]{2,1,0:T(8,128)(2,1)} fusion(bf16[174,128,128]{2,1,0:T(8,128)(2,1)} %param.28, s32[1024]{0:T(1024)S(1)} %pad_clamp_fusion), kind=kCustom, calls=%fused_computation.2 | custom fusion | bytes 4194560 | tf_op jit(solution)/shard_map/gather | solution.py:161
  69.5 0.7 gather_fusion.1
  70.2 0.1 pad_maximum_fusion.2
  70.3 0.6 gather_fusion.3
  70.9 0.6 gather_fusion.5
  71.5 7.2 %bitcast_select_fusion = (bf16[16,512,128]{2,1,0:T(8,128)(2,1)}, bf16[16,512,128]{2,1,0:T(8,128)(2,1)}) fusion(pred[16,512]{1,0:T(8,128)(4,1)S(1)} %get-tuple-element.26, pred[16,512]{1,0:T(8,128)(4,1)S(1)} %get-tuple-element.25, bf16[16,128]{1,0:T(8,128)(2,1)S(1)} %gather_fusion.5, bf16[16,128]{1,0:T(8,128)(2,1)S(1)} %gather_fusion.3, ...), kind=kLoop, calls=%fused_computation.28 | loop fusion | flops 4194304 | bytes 8413184 | tf_op jit(solution)/shard_map/jit(_where)/select_n | solution.py:163
  78.8 34.0 %all_to_all.15 = bf16[16,512,128]{2,1,0:T(8,128)(2,1)S(1)} all-to-all(bf16[16,512,128]{2,1,0:T(8,128)(2,1)} %get-tuple-element.18), channel_id=1, replica_groups=mesh['req'=16,'kv'=8] {'req'}, dimensions={0} | all-to-all | bytes 4194304 | tf_op jit(solution)/shard_map/all_to_all | solution.py:167
  112.7 4.6 %all-to-all-start.2 = ((bf16[16,512,128]{2,1,0:T(8,128)(2,1)}), bf16[16,512,128]{2,1,0:T(8,128)(2,1)}, u32[]{:S(2)}, u32[]{:S(2)}) async-start(bf16[16,512,128]{2,1,0:T(8,128)(2,1)} %get-tuple-element.17), calls=%async_computation.2 | async-start | bytes 4194304 | tf_op jit(solution)/shard_map/all_to_all | solution.py:168
  117.5 1.1 reduce_sum.68
  118.6 15.3 %all_gather.13 = bf16[64,2048]{1,0:T(8,128)(2,1)S(1)} all-gather(bf16[64,256]{1,0:T(8,128)(2,1)S(1)} %add_convert_fusion), channel_id=1, replica_groups=mesh['req'=16,'kv'=8] {'kv'}, dimensions={1}, use_global_device_ids=true | all-gather | bytes 294912 | tf_op jit(solution)/shard_map/all_gather | solution.py:179
  133.9 0.2 fusion.38
  134.1 3.7 %fusion.11 = f32[64,16,48]{0,2,1:T(8,128)} fusion(bf16[16,144,2048]{2,1,0:T(8,128)(2,1)} %bitcast.202, bf16[64,2048]{1,0:T(8,128)(2,1)S(1)} %all_gather.13, f32[2048]{0:T(1024)S(1)} %copy-done.12, f32[64]{0:T(128)S(1)} %add_rsqrt_fusion.1), kind=kOutput, calls=%fused_computation.26 | convolution fusion | flops 201850880 | bytes 3612928 | tf_op jit(solution)/shard_map/rd,sud->rsu/dot_general | solution.py:181
  137.8 6.1 %fusion.7 = f32[64,2048,1]{1,0,2:T(8,128)} fusion(bf16[16,144,2048]{2,1,0:T(8,128)(2,1)} %bitcast.203, f32[64,16,48]{0,2,1:T(8,128)} %fusion.11, bf16[64,2048]{1,0:T(8,128)(2,1)S(1)} %all_gather.13, f32[2048]{0:T(1024)S(1)} %copy-done.12, f32[64]{0:T(128)S(1)} %add_rsqrt_fusion.1), kind=kOutput, calls=%fused_computation.22 | convolution fusion | flops 403472384 | bytes 7479552 | tf_op jit(solution)/shard_map/rsu,suc->rc/dot_general | solution.py:184
  143.9 1.2 copy.63
  145.1 0.4 constant_dynamic-slice_fusion.7
  145.5 1.0 collective-permute-start
  146.5 0.6 copy.91
  147.1 3.0 %collective-permute-start.2 = (f32[64,256]{1,0:T(8,128)}, f32[64,256]{1,0:T(8,128)}, u32[]{:S(2)}, u32[]{:S(2)}) collective-permute-start(f32[64,256]{1,0:T(8,128)} %bitcast.178), channel_id=1, source_target_pairs={{0,3},{1,4},{2,5},{3,6},{4,7},{5,0},{6,1},{7,2},{8,11},{9,12},{10,... | collective-permute-start | bytes 196616 | tf_op jit(solution)/shard_map/ppermute | solution.py:89
  150.1 0.6 copy.90
  150.7 0.6 collective-permute-start.3
  151.3 0.6 copy.89
  151.9 2.0 %collective-permute-start.4 = (f32[64,256]{1,0:T(8,128)}, f32[64,256]{1,0:T(8,128)S(1)}, u32[]{:S(2)}, u32[]{:S(2)}) collective-permute-start(f32[64,256]{1,0:T(8,128)} %bitcast.176), channel_id=1, source_target_pairs={{0,5},{1,6},{2,7},{3,0},{4,1},{5,2},{6,3},{7,4},{8,13},{9,14},{10,... | collective-permute-start | bytes 196616 | tf_op jit(solution)/shard_map/ppermute | solution.py:89
  153.9 0.6 copy.88
  154.5 0.6 copy.87
  155.2 0.3 collective-permute-start.5
  155.5 0.7 collective-permute-start.6
  156.2 0.2 collective-permute-done.3
  156.4 0.9 collective-permute-done.4
  157.3 1.2 collective-permute-done.5
  158.5 1.9 %collective-permute-done.6 = f32[64,256]{1,0:T(8,128)S(1)} collective-permute-done((f32[64,256]{1,0:T(8,128)}, f32[64,256]{1,0:T(8,128)S(1)}, u32[]{:S(2)}, u32[]{:S(2)}) %collective-permute-start.6) | collective-permute-done | bytes 65568 | tf_op jit(solution)/shard_map/ppermute | solution.py:89
  160.4 1.6 fusion.61
  162.0 1.3 copy.96
  163.3 3.1 %copy.97 = bf16[16,512,128]{2,1,0:T(8,128)(2,1)} copy(bf16[16,512,128]{2,1,0:T(8,128)(2,1)} %all-to-all-done.2) | data formatting | bytes 4194304
  (73 shorter events, 1.3 us)
Async XLA Ops:
  7.2 43.3 %copy-start = (bf16[256,2048]{1,0:T(8,128)(2,1)S(1)}, bf16[256,2048]{1,0:T(8,128)(2,1)}, u32[]{:S(2)}) copy-start(bf16[256,2048]{1,0:T(8,128)(2,1)} %param.27) | copy-start | bytes 3145732
  7.2 19.6 %copy-start.7 = (f32[2048]{0:T(1024)S(1)}, f32[2048]{0:T(1024)}, u32[]{:S(2)}) copy-start(f32[2048]{0:T(1024)} %param.20) | copy-start | bytes 24580
  7.2 19.6 %copy-start.1 = (s32[64]{0:T(128)S(1)}, s32[64]{0:T(128)}, u32[]{:S(2)}) copy-start(s32[64]{0:T(128)} %param.30) | copy-start | bytes 772
  7.2 19.6 %copy-start.11 = (bf16[2048,128]{1,0:T(8,128)(2,1)S(1)}, bf16[2048,128]{1,0:T(8,128)(2,1)}, u32[]{:S(2)}) copy-start(bf16[2048,128]{1,0:T(8,128)(2,1)} %param.25) | copy-start | bytes 1572868
  7.2 20.0 %copy-start.8 = (f32[128]{0:T(128)S(1)}, f32[128]{0:T(128)}, u32[]{:S(2)}) copy-start(f32[128]{0:T(128)} %param.22) | copy-start | bytes 1540
  7.2 20.8 %copy-start.9 = (f32[128]{0:T(128)S(1)}, f32[128]{0:T(128)}, u32[]{:S(2)}) copy-start(f32[128]{0:T(128)} %param.21) | copy-start | bytes 1540
  7.2 21.4 %copy-start.3 = (s32[64,32]{0,1:T(8,128)S(1)}, s32[64,32]{0,1:T(8,128)}, u32[]{:S(2)}) copy-start(s32[64,32]{0,1:T(8,128)} %param.31) | copy-start | bytes 24580
  7.2 126.8 %all-gather.3.cloned.1.call-start = ((), (), s32[]{:S(2)}) async-start(), calls=%async_computation.3 | async-start | bytes 10027008 | tf_op jit(solution)/shard_map/all_gather | solution.py:127
  42.5 2.3 %copy-start.5 = (bf16[2048,128]{1,0:T(8,128)(2,1)S(1)}, bf16[2048,128]{1,0:T(8,128)(2,1)}, u32[]{:S(2)}) copy-start(bf16[2048,128]{1,0:T(8,128)(2,1)} %param.26) | copy-start | bytes 1572868
  45.1 5.4 %copy-start.4 = (bf16[2048,256]{1,0:T(8,128)(2,1)S(1)}, bf16[2048,256]{1,0:T(8,128)(2,1)}, u32[]{:S(2)}) copy-start(bf16[2048,256]{1,0:T(8,128)(2,1)} %param.24) | copy-start | bytes 3145732
  50.4 6.2 %copy-start.13 = (s32[1,16]{1,0:T(1,128)S(1)}, s32[1,16]{1,0:T(1,128)}, u32[]{:S(2)}) copy-start(s32[1,16]{1,0:T(1,128)} %param.33) | copy-start | bytes 196
  50.4 7.0 %copy-start.2 = (s32[1,16]{1,0:T(1,128)S(1)}, s32[1,16]{1,0:T(1,128)}, u32[]{:S(2)}) copy-start(s32[1,16]{1,0:T(1,128)} %param.32) | copy-start | bytes 196
  50.4 7.7 %copy-start.10 = (s32[2]{0:T(128)S(1)}, s32[2]{0:T(128)}, u32[]{:S(2)}) copy-start(s32[2]{0:T(128)} %constant.124) | copy-start | bytes 28
  52.2 26.5 %all-to-all-start = ((f32[8,64,256]{2,1,0:T(8,128)}), f32[8,64,256]{2,1,0:T(8,128)}, u32[]{:S(2)}, u32[]{:S(2)}) async-start(f32[8,64,256]{2,1,0:T(8,128)} %bitcast.173), calls=%async_computation | async-start | bytes 1048576 | tf_op jit(solution)/shard_map/all_to_all | solution.py:79
  112.7 5.8 %copy-start.6 = (bf16[64,256]{1,0:T(8,128)(2,1)S(1)}, bf16[64,256]{1,0:T(8,128)(2,1)}, u32[]{:S(2)}) copy-start(bf16[64,256]{1,0:T(8,128)(2,1)} %param.19) | copy-start | bytes 98308
  112.7 21.4 %copy-start.12 = (f32[2048]{0:T(1024)S(1)}, f32[2048]{0:T(1024)}, u32[]{:S(2)}) copy-start(f32[2048]{0:T(1024)} %param.34) | copy-start | bytes 24580
  112.7 43.5 %all-to-all-start.2 = ((bf16[16,512,128]{2,1,0:T(8,128)(2,1)}), bf16[16,512,128]{2,1,0:T(8,128)(2,1)}, u32[]{:S(2)}, u32[]{:S(2)}) async-start(bf16[16,512,128]{2,1,0:T(8,128)(2,1)} %get-tuple-element.17), calls=%async_computation.2 | async-start | bytes 4194304 | tf_op jit(solution)/shard_map/all_to_all | solution.py:168
  145.5 9.7 %collective-permute-start = (f32[64,256]{1,0:T(8,128)S(1)}, f32[64,256]{1,0:T(8,128)S(1)}, u32[]{:S(2)}, u32[]{:S(2)}) collective-permute-start(f32[64,256]{1,0:T(8,128)S(1)} %bitcast.197), channel_id=1, source_target_pairs={{0,1},{1,2},{2,3},{3,4},{4,5},{5,6},{6,7},{7,0},{8,9},{9,10},{10,1... | collective-permute-start | bytes 196616 | tf_op jit(solution)/shard_map/ppermute | solution.py:89
  146.4 9.0 %collective-permute-start.1 = (f32[64,256]{1,0:T(8,128)S(1)}, f32[64,256]{1,0:T(8,128)}, u32[]{:S(2)}, u32[]{:S(2)}) collective-permute-start(f32[64,256]{1,0:T(8,128)S(1)} %bitcast.196), channel_id=1, source_target_pairs={{0,2},{1,3},{2,4},{3,5},{4,6},{5,7},{6,0},{7,1},{8,10},{9,11},{10,... | collective-permute-start | bytes 196616 | tf_op jit(solution)/shard_map/ppermute | solution.py:89
  147.1 9.1 %collective-permute-start.2 = (f32[64,256]{1,0:T(8,128)}, f32[64,256]{1,0:T(8,128)}, u32[]{:S(2)}, u32[]{:S(2)}) collective-permute-start(f32[64,256]{1,0:T(8,128)} %bitcast.178), channel_id=1, source_target_pairs={{0,3},{1,4},{2,5},{3,6},{4,7},{5,0},{6,1},{7,2},{8,11},{9,12},{10,... | collective-permute-start | bytes 196616 | tf_op jit(solution)/shard_map/ppermute | solution.py:89
  150.7 5.8 %collective-permute-start.3 = (f32[64,256]{1,0:T(8,128)}, f32[64,256]{1,0:T(8,128)}, u32[]{:S(2)}, u32[]{:S(2)}) collective-permute-start(f32[64,256]{1,0:T(8,128)} %bitcast.177), channel_id=1, source_target_pairs={{0,4},{1,5},{2,6},{3,7},{4,0},{5,1},{6,2},{7,3},{8,12},{9,13},{10,... | collective-permute-start | bytes 196616 | tf_op jit(solution)/shard_map/ppermute | solution.py:89
  151.9 5.4 %collective-permute-start.4 = (f32[64,256]{1,0:T(8,128)}, f32[64,256]{1,0:T(8,128)S(1)}, u32[]{:S(2)}, u32[]{:S(2)}) collective-permute-start(f32[64,256]{1,0:T(8,128)} %bitcast.176), channel_id=1, source_target_pairs={{0,5},{1,6},{2,7},{3,0},{4,1},{5,2},{6,3},{7,4},{8,13},{9,14},{10,... | collective-permute-start | bytes 196616 | tf_op jit(solution)/shard_map/ppermute | solution.py:89
  155.2 3.3 %collective-permute-start.5 = (f32[64,256]{1,0:T(8,128)}, f32[64,256]{1,0:T(8,128)S(1)}, u32[]{:S(2)}, u32[]{:S(2)}) collective-permute-start(f32[64,256]{1,0:T(8,128)} %bitcast.175), channel_id=1, source_target_pairs={{0,6},{1,7},{2,0},{3,1},{4,2},{5,3},{6,4},{7,5},{8,14},{9,15},{10,... | collective-permute-start | bytes 196616 | tf_op jit(solution)/shard_map/ppermute | solution.py:89
  155.5 5.0 %collective-permute-start.6 = (f32[64,256]{1,0:T(8,128)}, f32[64,256]{1,0:T(8,128)S(1)}, u32[]{:S(2)}, u32[]{:S(2)}) collective-permute-start(f32[64,256]{1,0:T(8,128)} %bitcast.174), channel_id=1, source_target_pairs={{0,7},{1,0},{2,1},{3,2},{4,3},{5,4},{6,5},{7,6},{8,15},{9,8},{10,9... | collective-permute-start | bytes 196616 | tf_op jit(solution)/shard_map/ppermute | solution.py:89
Sparse Core Ops, SparseCore 0:
  10.2 78.4 all-gather.2
